TPU v7x, 256 devices: a whole 4x4x8 slice. The times are simulated.
256 devices in a mesh: dp: 32 (over x, y, core), tensor: 8 (over z).
Axes of the slice: x: 4, y: 4, z: 8, core: 2. Of those that a mesh axis runs over, the one named last changes fastest.
Arguments:
- hidden_states: bfloat16 [24576, 4096], P('dp', 'tensor')
- neighbour_ids: int32 [384, 2], P('dp'), may hold values from 0 to 511, as said below
- database: bfloat16 [512, 128, 896], P('dp')
- w_up: bfloat16 [896, 3584], P(None, 'tensor'), may hold values from -0.1875 to 0.1875
- w_down: bfloat16 [3584, 896], P('tensor'), may hold values from -0.09375 to 0.09375
- w_query: bfloat16 [4096, 4096], P(None, 'tensor'), may hold values from -0.09375 to 0.09375
- w_key: bfloat16 [896, 4096], P(None, 'tensor'), may hold values from -0.1875 to 0.1875
- w_value: bfloat16 [896, 4096], P(None, 'tensor'), may hold values from -0.1875 to 0.1875
Outputs:
- attended: bfloat16 [24576, 4096], P('dp', 'tensor')
Inputs may be any that keep to these rules, and one draw needn't show every extreme that they name: `neighbour_ids`: block ids are grouped by owner: index s of dp holds blocks s * 16 to (s + 1) * 16 - 1. Among the 24 ids of one sequence, no owner's blocks are named more than 2 times; one owner, the same for every sequence, is named exactly 2 times by each.
All inputs are finite; a program needn't handle non-finite values.
Results may differ from a plain program's by a relative error of at most 0.02.
Values may be sent and summed in bfloat16 or wider, within the bound.
No kernel may reach another device: no remote copies, remote signals or barrier semaphores. Data moves between devices by JAX's collectives and lax.ppermute only.
A program may use at most 128 MiB of HBM per device.

v0:
```python
import math

import jax
import jax.numpy as jnp
from jax import lax
from jax.sharding import PartitionSpec as P

HD = 128
SPAN = 64
KN = 2
NTOK = 128


EPSILON = 1e-06
LOGIT_SCALE = 3.0


def head_norm(projected):
    shaped = projected.reshape(projected.shape[0], -1, HD)
    scaled = shaped * lax.rsqrt(jnp.mean(shaped * shaped, axis=-1, keepdims=True) + EPSILON)
    return scaled.astype(jnp.bfloat16)


def attend(queries, keys, values):
    seq_rows = queries.shape[0]
    heads_here = queries.shape[1]
    span_count = seq_rows // SPAN
    shifted = jnp.concatenate(
        [queries[SPAN - 1 :], jnp.zeros((SPAN - 1, heads_here, HD), jnp.bfloat16)], axis=0
    )
    windows = shifted.reshape(span_count, SPAN, heads_here, HD)
    key_blocks = keys.reshape(span_count, KN * NTOK, heads_here, HD)
    value_blocks = values.reshape(span_count, KN * NTOK, heads_here, HD)
    scores = jnp.einsum("cqhd,ckhd->chqk", windows, key_blocks, preferred_element_type=jnp.float32)
    scores = scores * (LOGIT_SCALE / math.sqrt(HD))
    expo = jnp.exp(scores)
    weights = (expo / jnp.sum(expo, axis=-1, keepdims=True)).astype(jnp.bfloat16)
    mixed = jnp.einsum("chqk,ckhd->cqhd", weights, value_blocks, preferred_element_type=jnp.float32)
    mixed = mixed.astype(jnp.bfloat16).reshape(seq_rows, heads_here * HD)
    leading = jnp.zeros((SPAN - 1, heads_here * HD), jnp.bfloat16)
    return jnp.concatenate([leading, mixed[: seq_rows - SPAN + 1]], axis=0)


def shards(hidden_states, neighbour_ids, database, w_up, w_down, w_query, w_key, w_value):
    dp_count = lax.axis_size("dp")
    tensor_count = lax.axis_size("tensor")
    shard_blocks = database.shape[0]
    block_tokens = database.shape[1]
    enc_width = database.shape[2]
    flat_ids = neighbour_ids.reshape(-1)
    request_count = flat_ids.shape[0]
    capacity = max(2, (request_count + dp_count - 1) // dp_count + 1)
    owners = flat_ids // shard_blocks
    local_rows = flat_ids % shard_blocks
    owner_match = (owners[:, None] == jnp.arange(dp_count, dtype=jnp.int32)[None, :]).astype(
        jnp.int32
    )
    positions = jnp.arange(request_count, dtype=jnp.int32)
    earlier = (positions[:, None] > positions[None, :]).astype(jnp.int32)
    ranks = jnp.sum(jnp.dot(earlier, owner_match) * owner_match, axis=1)
    slots = owners * capacity + ranks
    slot_match = slots[None, :] == jnp.arange(dp_count * capacity, dtype=jnp.int32)[:, None]
    requests = jnp.sum(jnp.where(slot_match, local_rows[None, :], 0), axis=1)
    requests = requests.reshape(dp_count, capacity)
    replies = lax.all_to_all(
        database[lax.all_to_all(requests, "dp", split_axis=0, concat_axis=0, tiled=True)],
        "dp",
        split_axis=0,
        concat_axis=0,
        tiled=True,
    )
    raw_blocks = replies.reshape(dp_count * capacity, block_tokens, enc_width)[slots]
    raw_float = raw_blocks.astype(jnp.float32)
    normed = (
        raw_float * lax.rsqrt(jnp.mean(raw_float * raw_float, axis=-1, keepdims=True) + EPSILON)
    ).astype(jnp.bfloat16)
    own_blocks = request_count // tensor_count
    inner = jnp.einsum("bte,ef->btf", normed, w_up, preferred_element_type=jnp.float32)
    active = jax.nn.gelu(inner).astype(jnp.bfloat16)
    summed = lax.psum_scatter(
        jnp.einsum("btf,fe->bte", active, w_down, preferred_element_type=jnp.float32).astype(
            jnp.bfloat16
        ),
        "tensor",
        scatter_dimension=0,
        tiled=True,
    ).astype(jnp.float32)
    raw_own = lax.dynamic_slice_in_dim(
        raw_float, lax.axis_index("tensor") * own_blocks, own_blocks, 0
    )
    encoded_own = (raw_own + summed).astype(jnp.bfloat16)
    encoded = lax.all_gather(encoded_own, "tensor", axis=0, tiled=True)
    projected = jnp.dot(
        lax.all_gather(hidden_states, "tensor", axis=1, tiled=True),
        w_query,
        preferred_element_type=jnp.float32,
    )
    queries = head_norm(projected)
    flat_encoded = encoded.reshape(-1, enc_width)
    keys = head_norm(jnp.dot(flat_encoded, w_key, preferred_element_type=jnp.float32))
    values = jnp.dot(flat_encoded, w_value, preferred_element_type=jnp.float32).astype(jnp.bfloat16)
    values = values.reshape(flat_encoded.shape[0], -1, HD)
    return attend(queries, keys, values)


def solution(mesh):
    in_specs = (
        P("dp", "tensor"),
        P("dp", None),
        P("dp", None, None),
        P(None, "tensor"),
        P("tensor", None),
        P(None, "tensor"),
        P(None, "tensor"),
        P(None, "tensor"),
    )
    out_specs = P("dp", "tensor")
    return jax.shard_map(shards, mesh=mesh, in_specs=in_specs, out_specs=out_specs, check_vma=False)
```

profile of v0, /device:TPU:1, one launch (start us, length us, event | category | flops | bytes accessed | tf_op | source)
XLA Modules:
  0.0 541.8 jit_solution(13727991307017011752)
XLA Ops:
  6.5 0.8 copy.37
  7.5 0.3 fusion.29
  8.0 15.3 %all_to_all.17 = s32[32,1,2]{2,1,0:T(1,128)S(1)} all-to-all(s32[32,1,2]{2,1,0:T(1,128)S(1)} %bitcast.50), channel_id=1, replica_groups=mesh['dp'=32,'tensor'=8] {'dp'}, dimensions={0} | all-to-all | bytes 512 | tf_op jit(solution)/shard_map/all_to_all | solution.py:66
  23.5 0.1 reshape.243
  23.7 10.1 %gather_fusion = bf16[64,128,896]{2,1,0:T(8,128)(2,1)} fusion(bf16[16,128,896]{2,1,0:T(8,128)(2,1)} %param.10, s32[1024]{0:T(1024)S(1)} %pad_clamp_fusion.1), kind=kCustom, calls=%fused_computation | custom fusion | bytes 29360384 | tf_op jit(solution)/shard_map/gather | solution.py:66
  33.8 5.2 all-to-all-start.1
  39.2 202.2 %all-to-all-done.1 = bf16[32,2,128,896]{3,2,1,0:T(8,128)(2,1)} async-done(((bf16[32,2,128,896]{3,2,1,0:T(8,128)(2,1)}), bf16[32,2,128,896]{3,2,1,0:T(8,128)(2,1)}, u32[]{:S(2)}, u32[]{:S(2)}) %all-to-all-start.1) | async-done | bytes 14680096 | tf_op jit(solution)/shard_map/all_to_all | solution.py:65
  241.3 9.1 %gather_fusion.1 = bf16[24,128,896]{2,1,0:T(8,128)(2,1)} fusion(bf16[64,128,896]{2,1,0:T(8,128)(2,1)} %bitcast.3, s32[1024]{0:T(1024)S(1)} %pad_clamp_fusion), kind=kCustom, calls=%fused_computation.1 | custom fusion | bytes 11010144 | tf_op jit(solution)/shard_map/gather | solution.py:72
  250.4 3.8 multiply_reduce_fusion
  254.3 10.4 %convolution_convert_fusion.1 = bf16[24,128,896]{2,1,0:T(8,128)(2,1)} fusion(f32[24,128]{1,0:T(8,128)S(1)} %add_rsqrt_fusion.2, bf16[24,128,896]{2,1,0:T(8,128)(2,1)} %gather_fusion.1, bf16[448,896]{1,0:T(8,128)(2,1)S(1)} %copy-done.4, bf16[896,448]{0,1:T(8,128)(2,1)S(1)} %copy-done.5), kind=kOutput, calls=%fused_computation.19 | convolution fusion | flops 4955897856 | bytes 12627968 | tf_op jit(solution)/shard_map/btf,fe->bte/dot_general | solution.py:81
  264.8 0.7 all-gather.5.cloned.1.call-update
  265.5 0.2 all-gather.3.cloned.1.call-start
  265.7 8.2 %convert_element_type.38 = f32[24,128,896]{2,1,0:T(8,128)} convert(bf16[24,128,896]{2,1,0:T(8,128)(2,1)} %gather_fusion.1) | non-fusion elementwise | flops 2752512 | bytes 16515072 | tf_op jit(solution)/shard_map/convert_element_type | solution.py:73
  273.9 90.8 %reduce-scatter.2.cloned.1.call-done = bf16[3,128,896]{2,1,0:T(8,128)(2,1)} async-done(((bf16[24,128,896]{2,1,0:T(8,128)(2,1)}), bf16[3,128,896]{2,1,0:T(8,128)(2,1)}) %reduce-scatter.2.cloned.1.call-update) | async-done | bytes 688144 | tf_op jit(solution)/shard_map/reduce_scatter | solution.py:80
  364.7 2.5 add_convert_fusion
  367.2 0.6 copy.48
  367.8 71.6 %all-gather.5.cloned.1.call-done = bf16[768,4096]{1,0:T(8,128)(2,1)} async-done(((bf16[768,512]{1,0:T(8,128)(2,1)}), bf16[768,4096]{1,0:T(8,128)(2,1)}) %all-gather.5.cloned.1.call-update) | async-done | bytes 6291472 | tf_op jit(solution)/shard_map/all_gather | solution.py:94
  439.4 7.1 %multiply_reduce_fusion.2 = (f32[768,4]{0,1:T(4,128)S(1)}, f32[768,512]{0,1:T(8,128)S(1)}) fusion(bf16[768,4096]{1,0:T(8,128)(2,1)} %all-gather.5.cloned.1.call-done, bf16[4096,512]{1,0:T(8,128)(2,1)} %param.13), kind=kOutput, calls=%fused_computation.33 | convolution fusion | flops 3222008832 | bytes 12070912 | tf_op jit(solution)/shard_map/dot_general | solution.py:93
  446.6 0.5 slice.12
  447.0 1.6 copy.49
  448.7 1.8 multiply_convert_fusion.3
  450.6 56.3 %all-gather.3.cloned.1.call-done = bf16[24,128,896]{2,1,0:T(8,128)(2,1)} async-done(((bf16[3,128,896]{2,1,0:T(8,128)(2,1)}), bf16[24,128,896]{2,1,0:T(8,128)(2,1)}) %all-gather.3.cloned.1.call-update) | async-done | bytes 5505040 | tf_op jit(solution)/shard_map/all_gather | solution.py:92
  506.9 8.6 %multiply_reduce_fusion.1 = (f32[3072,4]{0,1:T(4,128)S(1)}, f32[3072,4,128]{2,0,1:T(8,128)}) fusion(bf16[3072,896,1]{1,0,2:T(8,128)(2,1)} %bitcast.51, bf16[4,128,896]{2,1,0:T(8,128)(2,1)S(1)} %bitcast.49), kind=kOutput, calls=%fused_computation.6 | convolution fusion | flops 2821705728 | bytes 12763136 | tf_op jit(solution)/shard_map/dot_general | solution.py:100
  515.5 4.8 convolution_convert_fusion
  520.3 5.6 %reshape_reshape.3 = bf16[12,256,4,128]{3,2,1,0:T(4,128)(2,1)} reshape(bf16[3072,512]{1,0:T(8,128)(2,1)} %convolution_convert_fusion) | data formatting | bytes 6291456 | tf_op jit(solution)/shard_map/reshape;reshape | solution.py:33
  525.8 4.4 multiply_convert_fusion.1
  530.3 1.3 fusion.15
  531.6 0.6 copy-done.1
  532.2 1.2 fusion.26
  533.4 0.6 copy.47
  534.0 0.1 copy.66
  534.2 1.1 concatenate.7
  (33 shorter events, 0.9 us)
Async XLA Ops:
  6.5 509.0 %copy-start = (bf16[896,512]{1,0:T(8,128)(2,1)S(1)}, bf16[896,512]{1,0:T(8,128)(2,1)}, u32[]{:S(2)}) copy-start(bf16[896,512]{1,0:T(8,128)(2,1)} %param.15) | copy-start | bytes 2752516
  33.8 207.6 %all-to-all-start.1 = ((bf16[32,2,128,896]{3,2,1,0:T(8,128)(2,1)}), bf16[32,2,128,896]{3,2,1,0:T(8,128)(2,1)}, u32[]{:S(2)}, u32[]{:S(2)}) async-start(bf16[32,2,128,896]{3,2,1,0:T(8,128)(2,1)} %bitcast.42), calls=%async_computation.1 | async-start | bytes 29360128 | tf_op jit(solution)/shard_map/all_to_all | solution.py:65
  39.0 325.6 %reduce-scatter.2.cloned.1.call-start = ((), (), s32[]{:S(2)}) async-start(), calls=%async_computation.3 | async-start | bytes 6193152 | tf_op jit(solution)/shard_map/reduce_scatter | solution.py:80
  250.4 3.8 copy-start.4
  250.4 3.9 copy-start.5
  264.7 174.7 %all-gather.5.cloned.1.call-start = ((), (), s32[]{:S(2)}) async-start(), calls=%async_computation.5 | async-start | bytes 7077888 | tf_op jit(solution)/shard_map/all_gather | solution.py:94
  265.5 241.4 %all-gather.3.cloned.1.call-start = ((), (), s32[]{:S(2)}) async-start(), calls=%async_computation.4 | async-start | bytes 6193152 | tf_op jit(solution)/shard_map/all_gather | solution.py:92
  265.7 101.5 %copy-start.2 = (bf16[896,512]{1,0:T(8,128)(2,1)S(1)}, bf16[896,512]{1,0:T(8,128)(2,1)}, u32[]{:S(2)}) copy-start(bf16[896,512]{1,0:T(8,128)(2,1)} %param.14) | copy-start | bytes 2752516
  506.9 8.6 %copy-start.3 = (bf16[24,128,896]{2,1,0:T(8,128)(2,1)S(1)}, bf16[24,128,896]{2,1,0:T(8,128)(2,1)}, u32[]{:S(2)}) copy-start(bf16[24,128,896]{2,1,0:T(8,128)(2,1)} %all-gather.3.cloned.1.call-done) | copy-start | bytes 16515076
  530.3 1.9 copy-start.1
Sparse Core Ops, SparseCore 0:
  264.9 99.7 reduce-scatter.1
  366.4 72.9 all-gather.4
  441.2 65.6 all-gather.2
where the time goes:
time: 542 us
  waiting for transfers between devices  422 us (78%)
  matrix products  33.7 us (6%)
  local copies, waits for them, and re-layouts  31.4 us (6%)
  other arithmetic  20.9 us (4%)
  blocking collectives  15.3 us (3%)
  between operations  13.3 us (2%)
  starting transfers between devices  5.52 us (1%)
    all_to_all x1, waiting for transfers between devices, shards(): lax.all_to_all(database[lax.all_to_all(requests, 'dp', split_axis=0, conc...  202 us
    reduce_scatter x1, waiting for transfers between devices, shards(): lax.psum_scatter(jnp.einsum('btf,fe->bte', active, w_down, preferred_elem...  90.8 us
    all_gather x1, waiting for transfers between devices, shards(): lax.all_gather(hidden_states, 'tensor', axis=1, tiled=True)  71.6 us
    all_gather x1, waiting for transfers between devices, shards(): encoded = lax.all_gather(encoded_own, 'tensor', axis=0, tiled=True)  56.3 us
    all_to_all x1, blocking collectives, shards(): lax.all_to_all(requests, 'dp', split_axis=0, concat_axis=0, tiled=True)  15.3 us
  transfers between devices with their start and end apart: 4, of which 4 were waited for; matrix products, arithmetic and copies ran while one was open for 4% of the time, Pallas kernels for 0%

commit v1 on v0

--- a/solution.py
+++ b/solution.py
@@ -62,34 +62,27 @@
     slot_match = slots[None, :] == jnp.arange(dp_count * capacity, dtype=jnp.int32)[:, None]
     requests = jnp.sum(jnp.where(slot_match, local_rows[None, :], 0), axis=1)
     requests = requests.reshape(dp_count, capacity)
-    replies = lax.all_to_all(
-        database[lax.all_to_all(requests, "dp", split_axis=0, concat_axis=0, tiled=True)],
-        "dp",
-        split_axis=0,
-        concat_axis=0,
-        tiled=True,
-    )
-    raw_blocks = replies.reshape(dp_count * capacity, block_tokens, enc_width)[slots]
-    raw_float = raw_blocks.astype(jnp.float32)
+    raw_float = database.astype(jnp.float32)
     normed = (
         raw_float * lax.rsqrt(jnp.mean(raw_float * raw_float, axis=-1, keepdims=True) + EPSILON)
     ).astype(jnp.bfloat16)
-    own_blocks = request_count // tensor_count
     inner = jnp.einsum("bte,ef->btf", normed, w_up, preferred_element_type=jnp.float32)
     active = jax.nn.gelu(inner).astype(jnp.bfloat16)
+    partial = jnp.einsum("btf,fe->bte", active, w_down, preferred_element_type=jnp.float32)
+    rows_here = block_tokens // tensor_count
     summed = lax.psum_scatter(
-        jnp.einsum("btf,fe->bte", active, w_down, preferred_element_type=jnp.float32).astype(
-            jnp.bfloat16
-        ),
-        "tensor",
-        scatter_dimension=0,
-        tiled=True,
+        partial.astype(jnp.bfloat16), "tensor", scatter_dimension=1, tiled=True
     ).astype(jnp.float32)
     raw_own = lax.dynamic_slice_in_dim(
-        raw_float, lax.axis_index("tensor") * own_blocks, own_blocks, 0
+        raw_float, lax.axis_index("tensor") * rows_here, rows_here, 1
     )
     encoded_own = (raw_own + summed).astype(jnp.bfloat16)
-    encoded = lax.all_gather(encoded_own, "tensor", axis=0, tiled=True)
+    asked = lax.all_to_all(requests, "dp", split_axis=0, concat_axis=0, tiled=True)
+    replies = lax.all_to_all(
+        encoded_own[asked], "dp", split_axis=0, concat_axis=0, tiled=True
+    )
+    mine = replies.reshape(dp_count * capacity, rows_here, enc_width)[slots]
+    encoded = lax.all_gather(mine, "tensor", axis=1, tiled=True)
     projected = jnp.dot(
         lax.all_gather(hidden_states, "tensor", axis=1, tiled=True),
         w_query,

time: 542 us -> 248 us (0.46)
  waiting for transfers between devices: 422 us -> 155 us
  blocking collectives: 15.3 us -> 0 us
  local copies, waits for them, and re-layouts: 31.4 us -> 16.5 us
  starting transfers between devices: 5.52 us -> 16.4 us
  other arithmetic: 20.9 us -> 14.1 us
    all_to_all x1 -> x2, waiting for transfers between devices: 202 us -> 26.3 us  [the longest x1 25.2 us: shards(): lax.all_to_all(encoded_own[asked], 'dp', split_axis=0, concat_axis=0, til...]
    reduce_scatter x1, waiting for transfers between devices: 90.8 us -> 36.4 us  [shards(): lax.psum_scatter(partial.astype(jnp.bfloat16), 'tensor', scatter_dimensio...]
    all_gather x1, waiting for transfers between devices: 71.6 us -> 35.6 us  [shards(): lax.all_gather(hidden_states, 'tensor', axis=1, tiled=True)]
    gather x2, local copies, waits for them, and re-layouts: 19.2 us -> 3.5 us  [the longest x1 2.01 us: shards(): encoded_own[asked]]
    all_to_all x1 -> x0, blocking collectives: 15.3 us -> none  [shards(): lax.all_to_all(requests, 'dp', split_axis=0, concat_axis=0, tiled=True)]
    all_to_all x1 -> x2, starting transfers between devices: 5.22 us -> 16.2 us  [the longest x1 8.57 us: shards(): lax.all_to_all(requests, 'dp', split_axis=0, concat_axis=0, tiled=True)]
  transfers between devices with their start and end apart: 4 -> 5, of which waited for: 4 -> 5; matrix products, arithmetic and copies ran while one was open for 4% -> 10% of each run, Pallas kernels for 0% -> 0%
where the time goes in v1:
time: 248 us; the launch traced here: 247 us
  waiting for transfers between devices  155 us (62%)
  matrix products  31.5 us (13%)
  local copies, waits for them, and re-layouts  16.5 us (7%)
  starting transfers between devices  16.4 us (7%)
  other arithmetic  14.1 us (6%)
  between operations  13.3 us (5%)
    all_gather x1, waiting for transfers between devices, shards(): encoded = lax.all_gather(mine, 'tensor', axis=1, tiled=True)  56.3 us
    reduce_scatter x1, waiting for transfers between devices, shards(): lax.psum_scatter(partial.astype(jnp.bfloat16), 'tensor', scatter_dimensio...  36.4 us
    all_gather x1, waiting for transfers between devices, shards(): lax.all_gather(hidden_states, 'tensor', axis=1, tiled=True)  35.6 us
    all_to_all x1, waiting for transfers between devices, shards(): lax.all_to_all(encoded_own[asked], 'dp', split_axis=0, concat_axis=0, til...  25.2 us
    all_to_all x1, starting transfers between devices, shards(): lax.all_to_all(requests, 'dp', split_axis=0, concat_axis=0, tiled=True)  8.57 us
    dot_general x1, matrix products, shards(): jnp.einsum('btf,fe->bte', active, w_down, preferred_element_type=jnp.floa...  7.7 us
    all_to_all x1, starting transfers between devices, shards(): lax.all_to_all(encoded_own[asked], 'dp', split_axis=0, concat_axis=0, til...  7.59 us
    dot_general x1, matrix products, shards(): jnp.dot(flat_encoded, w_value, preferred_element_type=jnp.float32)  7.36 us
  transfers between devices with their start and end apart: 5, of which 5 were waited for; matrix products, arithmetic and copies ran while one was open for 10% of the time, Pallas kernels for 0%

profile of v1, /device:TPU:1, one launch (start us, length us, event | category | flops | bytes accessed | tf_op | source)
XLA Modules:
  0.0 247.1 jit_solution(8010962660438424472)
XLA Ops:
  6.5 3.0 %multiply_reduce_fusion = f32[16,128]{1,0:T(8,128)S(1)} fusion(bf16[16,128,896]{2,1,0:T(8,128)(2,1)} %param.10), kind=kLoop, calls=%fused_computation.3 | loop fusion | flops 5502976 | bytes 3678208 | tf_op jit(solution)/shard_map/reduce_sum | solution.py:67
  9.6 7.7 %convolution_convert_fusion.1 = bf16[16,128,896]{2,1,0:T(8,128)(2,1)} fusion(f32[16,128]{1,0:T(8,128)S(1)} %add_rsqrt_fusion.2, bf16[16,128,896]{2,1,0:T(8,128)(2,1)} %param.10, bf16[448,896]{1,0:T(8,128)(2,1)S(1)} %copy-done.4, bf16[896,448]{0,1:T(8,128)(2,1)S(1)} %copy-done.5), kind=kOutput, calls=%fused_computation.26 | convolution fusion | flops 3303931904 | bytes 8953856 | tf_op jit(solution)/shard_map/btf,fe->bte/dot_general | solution.py:71
  17.3 0.7 all-gather.4.cloned.1.call-update
  18.2 0.3 fusion.29
  18.6 0.7 all_to_all.11
  19.4 8.6 %all-to-all-start = ((s32[32,1,2]{2,1,0:T(1,128)}), s32[32,1,2]{2,1,0:T(1,128)S(1)}, u32[]{:S(2)}, u32[]{:S(2)}) async-start(s32[32,1,2]{2,1,0:T(1,128)} %bitcast.2), calls=%async_computation.1 | async-start | bytes 32768 | tf_op jit(solution)/shard_map/all_to_all | solution.py:80
  27.9 5.8 %convert_element_type.38 = f32[16,128,896]{2,1,0:T(8,128)} convert(bf16[16,128,896]{2,1,0:T(8,128)(2,1)} %param.10) | non-fusion elementwise | flops 1835008 | bytes 11010048 | tf_op jit(solution)/shard_map/convert_element_type | solution.py:65
  33.7 1.1 all-to-all-done
  35.1 36.4 %reduce-scatter.2.cloned.1.call-done = bf16[16,16,896]{2,1,0:T(8,128)(2,1)} async-done(((bf16[16,128,896]{2,1,0:T(8,128)(2,1)}), bf16[16,16,896]{2,1,0:T(8,128)(2,1)}) %reduce-scatter.2.cloned.1.call-update) | async-done | bytes 458768 | tf_op jit(solution)/shard_map/reduce_scatter | solution.py:73
  71.6 1.4 add_convert_fusion
  73.0 2.0 gather_fusion
  75.0 7.6 %all-to-all-start.1 = ((bf16[32,2,16,896]{3,2,1,0:T(8,128)(2,1)}), bf16[32,2,16,896]{3,2,1,0:T(8,128)(2,1)S(1)}, u32[]{:S(2)}, u32[]{:S(2)}) async-start(bf16[32,2,16,896]{3,2,1,0:T(8,128)(2,1)} %bitcast.4), calls=%async_computation.2 | async-start | bytes 3670016 | tf_op jit(solution)/shard_map/all_to_all | solution.py:81
  82.6 0.2 all-gather.6.cloned.1.call-start
  82.9 25.2 %all-to-all-done.1 = bf16[32,2,16,896]{3,2,1,0:T(8,128)(2,1)S(1)} async-done(((bf16[32,2,16,896]{3,2,1,0:T(8,128)(2,1)}), bf16[32,2,16,896]{3,2,1,0:T(8,128)(2,1)S(1)}, u32[]{:S(2)}, u32[]{:S(2)}) %all-to-all-start.1) | async-done | bytes 1835040 | tf_op jit(solution)/shard_map/all_to_all | solution.py:81
  108.1 1.5 gather_fusion.1
  109.6 1.5 copy.48
  111.2 35.6 %all-gather.4.cloned.1.call-done = bf16[768,4096]{1,0:T(8,128)(2,1)} async-done(((bf16[768,512]{1,0:T(8,128)(2,1)}), bf16[768,4096]{1,0:T(8,128)(2,1)}) %all-gather.4.cloned.1.call-update) | async-done | bytes 6291472 | tf_op jit(solution)/shard_map/all_gather | solution.py:87
  146.7 7.1 %multiply_reduce_fusion.2 = (f32[768,4]{0,1:T(4,128)S(1)}, f32[768,512]{0,1:T(8,128)S(1)}) fusion(bf16[768,4096]{1,0:T(8,128)(2,1)} %all-gather.4.cloned.1.call-done, bf16[4096,512]{1,0:T(8,128)(2,1)} %param.13), kind=kOutput, calls=%fused_computation.33 | convolution fusion | flops 3222008832 | bytes 12070912 | tf_op jit(solution)/shard_map/dot_general | solution.py:86
  153.9 0.5 slice.12
  154.4 1.6 copy.49
  156.1 1.8 multiply_convert_fusion.3
  158.0 56.3 %all-gather.6.cloned.1.call-done = bf16[24,128,896]{2,1,0:T(8,128)(2,1)} async-done(((bf16[24,16,896]{2,1,0:T(8,128)(2,1)}), bf16[24,128,896]{2,1,0:T(8,128)(2,1)}) %all-gather.6.cloned.1.call-update) | async-done | bytes 5505040 | tf_op jit(solution)/shard_map/all_gather | solution.py:85
  214.2 7.4 %convolution_convert_fusion = bf16[3072,512]{1,0:T(8,128)(2,1)} fusion(bf16[3072,896]{1,0:T(8,128)(2,1)} %bitcast.50, bf16[896,512]{1,0:T(8,128)(2,1)S(1)} %copy-done), kind=kOutput, calls=%fused_computation.7 | convolution fusion | flops 2820145152 | bytes 9568256 | tf_op jit(solution)/shard_map/dot_general | solution.py:94
  221.6 5.5 %reshape_reshape.3 = bf16[12,256,4,128]{3,2,1,0:T(4,128)(2,1)} reshape(bf16[3072,512]{1,0:T(8,128)(2,1)} %convolution_convert_fusion) | data formatting | bytes 6291456 | tf_op jit(solution)/shard_map/reshape;reshape | solution.py:33
  227.1 6.5 %multiply_reduce_fusion.1 = (f32[3072,4]{0,1:T(4,128)S(1)}, f32[3072,4,128]{2,0,1:T(8,128)S(1)}) fusion(bf16[3072,896,1]{1,0,2:T(8,128)(2,1)} %bitcast.51, bf16[4,128,896]{2,1,0:T(8,128)(2,1)S(1)} %bitcast.49), kind=kOutput, calls=%fused_computation.5 | convolution fusion | flops 2821705728 | bytes 12763136 | tf_op jit(solution)/shard_map/dot_general | solution.py:93
  233.7 1.9 multiply_convert_fusion.1
  235.6 1.3 fusion.15
  236.9 0.6 copy-done.2
  237.5 1.2 fusion.26
  238.7 0.6 copy.47
  239.3 0.1 copy.66
  239.5 1.1 concatenate.7
  (34 shorter events, 1.0 us)
Async XLA Ops:
  6.5 207.7 %copy-start = (bf16[896,512]{1,0:T(8,128)(2,1)S(1)}, bf16[896,512]{1,0:T(8,128)(2,1)}, u32[]{:S(2)}) copy-start(bf16[896,512]{1,0:T(8,128)(2,1)} %param.15) | copy-start | bytes 2752516
  6.5 3.0 %copy-start.4 = (bf16[448,896]{1,0:T(8,128)(2,1)S(1)}, bf16[448,896]{1,0:T(8,128)(2,1)}, u32[]{:S(2)}) copy-start(bf16[448,896]{1,0:T(8,128)(2,1)} %param.12) | copy-start | bytes 2408452
  6.5 3.0 %copy-start.5 = (bf16[896,448]{0,1:T(8,128)(2,1)S(1)}, bf16[896,448]{0,1:T(8,128)(2,1)}, u32[]{:S(2)}) copy-start(bf16[896,448]{0,1:T(8,128)(2,1)} %param.11) | copy-start | bytes 2408452
  6.5 65.0 %reduce-scatter.2.cloned.1.call-start = ((), (), s32[]{:S(2)}) async-start(), calls=%async_computation.3 | async-start | bytes 4128768 | tf_op jit(solution)/shard_map/reduce_scatter | solution.py:73
  17.3 0.8 copy-start.3
  17.3 129.5 %all-gather.4.cloned.1.call-start = ((), (), s32[]{:S(2)}) async-start(), calls=%async_computation.4 | async-start | bytes 7077888 | tf_op jit(solution)/shard_map/all_gather | solution.py:87
  19.4 15.5 %all-to-all-start = ((s32[32,1,2]{2,1,0:T(1,128)}), s32[32,1,2]{2,1,0:T(1,128)S(1)}, u32[]{:S(2)}, u32[]{:S(2)}) async-start(s32[32,1,2]{2,1,0:T(1,128)} %bitcast.2), calls=%async_computation.1 | async-start | bytes 32768 | tf_op jit(solution)/shard_map/all_to_all | solution.py:80
  75.0 33.1 %all-to-all-start.1 = ((bf16[32,2,16,896]{3,2,1,0:T(8,128)(2,1)}), bf16[32,2,16,896]{3,2,1,0:T(8,128)(2,1)S(1)}, u32[]{:S(2)}, u32[]{:S(2)}) async-start(bf16[32,2,16,896]{3,2,1,0:T(8,128)(2,1)} %bitcast.4), calls=%async_computation.2 | async-start | bytes 3670016 | tf_op jit(solution)/shard_map/all_to_all | solution.py:81
  82.6 131.6 %all-gather.6.cloned.1.call-start = ((), (), s32[]{:S(2)}) async-start(), calls=%async_computation.5 | async-start | bytes 6193152 | tf_op jit(solution)/shard_map/all_gather | solution.py:85
  235.6 1.9 copy-start.2
  237.5 3.1 %copy-start.1 = (bf16[896,512]{1,0:T(8,128)(2,1)S(1)}, bf16[896,512]{1,0:T(8,128)(2,1)}, u32[]{:S(2)}) copy-start(bf16[896,512]{1,0:T(8,128)(2,1)} %param.15) | copy-start | bytes 2752516
Sparse Core Ops, SparseCore 0:
  17.4 54.1 reduce-scatter.1
  73.3 73.3 all-gather.3
  148.5 65.6 all-gather.5

commit v2 on v1

--- a/solution.py
+++ b/solution.py
@@ -22,11 +22,11 @@
 
 
 def attend(queries, keys, values):
-    seq_rows = queries.shape[0]
+    seq_rows = queries.shape[0] + SPAN - 1
     heads_here = queries.shape[1]
     span_count = seq_rows // SPAN
     shifted = jnp.concatenate(
-        [queries[SPAN - 1 :], jnp.zeros((SPAN - 1, heads_here, HD), jnp.bfloat16)], axis=0
+        [queries, jnp.zeros((SPAN - 1, heads_here, HD), jnp.bfloat16)], axis=0
     )
     windows = shifted.reshape(span_count, SPAN, heads_here, HD)
     key_blocks = keys.reshape(span_count, KN * NTOK, heads_here, HD)
@@ -39,6 +39,36 @@
     mixed = mixed.astype(jnp.bfloat16).reshape(seq_rows, heads_here * HD)
     leading = jnp.zeros((SPAN - 1, heads_here * HD), jnp.bfloat16)
     return jnp.concatenate([leading, mixed[: seq_rows - SPAN + 1]], axis=0)
+
+
+def ring_hops(states, n):
+    to_right = [(i, (i + 1) % n) for i in range(n)]
+    to_left = [(i, (i - 1) % n) for i in range(n)]
+    going_right = states
+    going_left = states
+    right_hops = n // 2
+    left_hops = n - 1 - right_hops
+    steps = []
+    for hop in range(1, right_hops + 1):
+        step = {}
+        going_right = lax.ppermute(going_right, "tensor", to_right)
+        step[(n - hop) % n] = going_right
+        if hop <= left_hops:
+            going_left = lax.ppermute(going_left, "tensor", to_left)
+            step[hop] = going_left
+        steps.append(step)
+    return steps
+
+
+def ring_query(got, w_query, n):
+    width = got[0].shape[1]
+    me = lax.axis_index("tensor")
+    total = None
+    for offset in range(n):
+        rows = lax.dynamic_slice_in_dim(w_query, ((me + offset) % n) * width, width, 0)
+        term = jnp.dot(got[offset], rows, preferred_element_type=jnp.float32)
+        total = term if total is None else total + term
+    return total
 
 
 def shards(hidden_states, neighbour_ids, database, w_up, w_down, w_query, w_key, w_value):
@@ -77,18 +107,20 @@
         raw_float, lax.axis_index("tensor") * rows_here, rows_here, 1
     )
     encoded_own = (raw_own + summed).astype(jnp.bfloat16)
+    states = hidden_states[SPAN - 1 :]
+    steps = ring_hops(states, tensor_count)
+    got = {0: states}
+    for step in steps:
+        got.update(step)
+    early = [v for step in steps[: len(steps) // 2] for v in step.values()]
+    late = [v for step in steps[len(steps) // 2 :] for v in step.values()]
     asked = lax.all_to_all(requests, "dp", split_axis=0, concat_axis=0, tiled=True)
-    replies = lax.all_to_all(
-        encoded_own[asked], "dp", split_axis=0, concat_axis=0, tiled=True
-    )
+    served, _ = lax.optimization_barrier((encoded_own[asked], early))
+    replies = lax.all_to_all(served, "dp", split_axis=0, concat_axis=0, tiled=True)
     mine = replies.reshape(dp_count * capacity, rows_here, enc_width)[slots]
+    mine, _ = lax.optimization_barrier((mine, late))
     encoded = lax.all_gather(mine, "tensor", axis=1, tiled=True)
-    projected = jnp.dot(
-        lax.all_gather(hidden_states, "tensor", axis=1, tiled=True),
-        w_query,
-        preferred_element_type=jnp.float32,
-    )
-    queries = head_norm(projected)
+    queries = head_norm(ring_query(got, w_query, tensor_count))
     flat_encoded = encoded.reshape(-1, enc_width)
     keys = head_norm(jnp.dot(flat_encoded, w_key, preferred_element_type=jnp.float32))
     values = jnp.dot(flat_encoded, w_value, preferred_element_type=jnp.float32).astype(jnp.bfloat16)

time: 248 us -> 245 us (0.988)
  waiting for transfers between devices: 155 us -> 129 us
  starting transfers between devices: 16.4 us -> 31.4 us
  matrix products: 31.5 us -> 35.9 us
  local copies, waits for them, and re-layouts: 16.5 us -> 19.8 us
    ppermute x0 -> x7, waiting for transfers between devices: none -> 50.1 us  [the longest x4 27 us: ring_hops(): going_right = lax.ppermute(going_right, 'tensor', to_right)]
    all_gather x1 -> x0, waiting for transfers between devices: 35.6 us -> none  [shards(): lax.all_gather(hidden_states, 'tensor', axis=1, tiled=True)]
    all_to_all x1, waiting for transfers between devices: 25.2 us -> 6.11 us  [shards(): lax.all_to_all(served, 'dp', split_axis=0, concat_axis=0, tiled=True)]
    ppermute x0 -> x7, starting transfers between devices: none -> 12.6 us  [the longest x3 12.5 us: ring_hops(): going_left = lax.ppermute(going_left, 'tensor', to_left)]
    reduce_scatter x1, waiting for transfers between devices: 36.4 us -> 24.4 us  [shards(): lax.psum_scatter(partial.astype(jnp.bfloat16), 'tensor', scatter_dimensio...]
    all_gather x1, waiting for transfers between devices: 56.3 us -> 47.6 us  [shards(): encoded = lax.all_gather(mine, 'tensor', axis=1, tiled=True)]
    dot_general x1 -> x8, matrix products: 7.14 us -> 11.5 us  [ring_query(): term = jnp.dot(got[offset], rows, preferred_element_type=jnp.float32)]
    all_to_all x1, starting transfers between devices: 8.57 us -> 11.3 us  [shards(): lax.all_to_all(requests, 'dp', split_axis=0, concat_axis=0, tiled=True)]
  transfers between devices with their start and end apart: 5 -> 11, of which waited for: 5 -> 7; matrix products, arithmetic and copies ran while one was open for 10% -> 12% of each run, Pallas kernels for 0% -> 0%
where the time goes in v2:
time: 245 us; the launch traced here: 244 us
  waiting for transfers between devices  129 us (53%)
  matrix products  35.9 us (15%)
  starting transfers between devices  31.4 us (13%)
  local copies, waits for them, and re-layouts  19.8 us (8%)
  between operations  13.8 us (6%)
  other arithmetic  13.6 us (6%)
    all_gather x1, waiting for transfers between devices, shards(): encoded = lax.all_gather(mine, 'tensor', axis=1, tiled=True)  47.6 us
    ppermute x4, waiting for transfers between devices, ring_hops(): going_right = lax.ppermute(going_right, 'tensor', to_right)  27 us
    reduce_scatter x1, waiting for transfers between devices, shards(): lax.psum_scatter(partial.astype(jnp.bfloat16), 'tensor', scatter_dimensio...  24.4 us
    ppermute x3, waiting for transfers between devices, ring_hops(): going_left = lax.ppermute(going_left, 'tensor', to_left)  23.2 us
    ppermute x3, starting transfers between devices, ring_hops(): going_left = lax.ppermute(going_left, 'tensor', to_left)  12.5 us
    dot_general x8, matrix products, ring_query(): term = jnp.dot(got[offset], rows, preferred_element_type=jnp.float32)  11.5 us
    all_to_all x1, starting transfers between devices, shards(): lax.all_to_all(requests, 'dp', split_axis=0, concat_axis=0, tiled=True)  11.3 us
    dot_general x1, matrix products, shards(): jnp.einsum('btf,fe->bte', active, w_down, preferred_element_type=jnp.floa...  7.7 us
  transfers between devices with their start and end apart: 11, of which 7 were waited for; matrix products, arithmetic and copies ran while one was open for 12% of the time, Pallas kernels for 0%

profile of v2, /device:TPU:1, one launch (start us, length us, event | category | flops | bytes accessed | tf_op | source)
XLA Modules:
  0.0 243.9 jit_solution(13602797089264161143)
XLA Ops:
  6.5 3.0 %multiply_reduce_fusion = f32[16,128]{1,0:T(8,128)S(1)} fusion(bf16[16,128,896]{2,1,0:T(8,128)(2,1)} %param.10), kind=kLoop, calls=%fused_computation.3 | loop fusion | flops 5502976 | bytes 3678208 | tf_op jit(solution)/shard_map/reduce_sum | solution.py:97
  9.6 7.7 %convolution_convert_fusion.1 = bf16[16,128,896]{2,1,0:T(8,128)(2,1)} fusion(f32[16,128]{1,0:T(8,128)S(1)} %add_rsqrt_fusion.2, bf16[16,128,896]{2,1,0:T(8,128)(2,1)} %param.10, bf16[448,896]{1,0:T(8,128)(2,1)S(1)} %copy-done.11, bf16[896,448]{0,1:T(8,128)(2,1)S(1)} %copy-done.12), kind=kOutput, calls=%fused_computation.26 | convolution fusion | flops 3303931904 | bytes 8953856 | tf_op jit(solution)/shard_map/btf,fe->bte/dot_general | solution.py:101
  19.4 6.4 %collective-permute-start.1 = (bf16[705,512]{1,0:T(8,128)(2,1)}, bf16[705,512]{1,0:T(8,128)(2,1)S(1)}, u32[]{:S(2)}, u32[]{:S(2)}) collective-permute-start(bf16[705,512]{1,0:T(8,128)(2,1)} %slice.6), channel_id=1, source_target_pairs={{0,7},{1,0},{2,1},{3,2},{4,3},{5,4},{6,5},{7,6},{8,15},{9,8},{10,9... | collective-permute-start | bytes 2165768 | tf_op jit(solution)/shard_map/ppermute | solution.py:57
  26.3 23.2 %collective-permute-done.1 = bf16[705,512]{1,0:T(8,128)(2,1)S(1)} collective-permute-done((bf16[705,512]{1,0:T(8,128)(2,1)}, bf16[705,512]{1,0:T(8,128)(2,1)S(1)}, u32[]{:S(2)}, u32[]{:S(2)}) %collective-permute-start.1) | collective-permute-done | bytes 721952 | tf_op jit(solution)/shard_map/ppermute | solution.py:57
  49.5 3.4 %collective-permute-start.3 = (bf16[705,512]{1,0:T(8,128)(2,1)S(1)}, bf16[705,512]{1,0:T(8,128)(2,1)}, u32[]{:S(2)}, u32[]{:S(2)}) collective-permute-start(bf16[705,512]{1,0:T(8,128)(2,1)S(1)} %collective-permute-done.1), channel_id=1, source_target_pairs={{0,7},{1,0},{2,1},{3,2},{4,3},{5,4},{6,5},{7,6},{8,15},{9,8},{10,9... | collective-permute-start | bytes 2165768 | tf_op jit(solution)/shard_map/ppermute | solution.py:57
  53.7 11.3 %all-to-all-start = ((s32[32,1,2]{2,1,0:T(1,128)}), s32[32,1,2]{2,1,0:T(1,128)S(1)}, u32[]{:S(2)}, u32[]{:S(2)}) async-start(s32[32,1,2]{2,1,0:T(1,128)} %bitcast.2), calls=%async_computation.1 | async-start | bytes 32768 | tf_op jit(solution)/shard_map/all_to_all | solution.py:117
  65.0 5.8 %convert_element_type.38 = f32[16,128,896]{2,1,0:T(8,128)} convert(bf16[16,128,896]{2,1,0:T(8,128)(2,1)} %param.10) | non-fusion elementwise | flops 1835008 | bytes 11010048 | tf_op jit(solution)/shard_map/convert_element_type | solution.py:95
  70.9 1.1 all-to-all-done
  72.3 24.4 %reduce-scatter.2.cloned.1.call-done = bf16[16,16,896]{2,1,0:T(8,128)(2,1)} async-done(((bf16[16,128,896]{2,1,0:T(8,128)(2,1)}), bf16[16,16,896]{2,1,0:T(8,128)(2,1)}) %reduce-scatter.2.cloned.1.call-update) | async-done | bytes 458768 | tf_op jit(solution)/shard_map/reduce_scatter | solution.py:103
  96.7 1.4 add_convert_fusion
  98.1 2.0 gather_fusion
  100.1 7.5 %all-to-all-start.1 = ((bf16[32,2,16,896]{3,2,1,0:T(8,128)(2,1)}), bf16[32,2,16,896]{3,2,1,0:T(8,128)(2,1)S(1)}, u32[]{:S(2)}, u32[]{:S(2)}) async-start(bf16[32,2,16,896]{3,2,1,0:T(8,128)(2,1)} %bitcast.4), calls=%async_computation.2 | async-start | bytes 3670016 | tf_op jit(solution)/shard_map/all_to_all | solution.py:119
  107.8 2.7 %collective-permute-start.5 = (bf16[705,512]{1,0:T(8,128)(2,1)}, bf16[705,512]{1,0:T(8,128)(2,1)}, u32[]{:S(2)}, u32[]{:S(2)}) collective-permute-start(bf16[705,512]{1,0:T(8,128)(2,1)} %collective-permute-done.3), channel_id=1, source_target_pairs={{0,7},{1,0},{2,1},{3,2},{4,3},{5,4},{6,5},{7,6},{8,15},{9,8},{10,9... | collective-permute-start | bytes 2165768 | tf_op jit(solution)/shard_map/ppermute | solution.py:57
  110.4 16.5 %collective-permute-done.4 = bf16[705,512]{1,0:T(8,128)(2,1)} collective-permute-done((bf16[705,512]{1,0:T(8,128)(2,1)}, bf16[705,512]{1,0:T(8,128)(2,1)}, u32[]{:S(2)}, u32[]{:S(2)}) %collective-permute-start.4) | collective-permute-done | bytes 721952 | tf_op jit(solution)/shard_map/ppermute | solution.py:54
  127.0 6.1 %all-to-all-done.1 = bf16[32,2,16,896]{3,2,1,0:T(8,128)(2,1)S(1)} async-done(((bf16[32,2,16,896]{3,2,1,0:T(8,128)(2,1)}), bf16[32,2,16,896]{3,2,1,0:T(8,128)(2,1)S(1)}, u32[]{:S(2)}, u32[]{:S(2)}) %all-to-all-start.1) | async-done | bytes 1835040 | tf_op jit(solution)/shard_map/all_to_all | solution.py:119
  133.2 1.5 gather_fusion.1
  134.7 10.5 %collective-permute-done.6 = bf16[705,512]{1,0:T(8,128)(2,1)S(1)} collective-permute-done((bf16[705,512]{1,0:T(8,128)(2,1)}, bf16[705,512]{1,0:T(8,128)(2,1)S(1)}, u32[]{:S(2)}, u32[]{:S(2)}) %collective-permute-start.6) | collective-permute-done | bytes 721952 | tf_op jit(solution)/shard_map/ppermute | solution.py:54
  145.3 2.3 copy.62
  147.6 2.0 fusion.49
  151.3 1.7 fusion.41
  152.9 1.7 convolution_add_fusion.2
  154.6 1.7 fusion.43
  156.3 1.7 convolution_add_fusion.1
  158.0 1.7 fusion.26
  159.8 1.7 reshape.237
  163.0 47.6 %all-gather.2.cloned.1.call-done = bf16[24,128,896]{2,1,0:T(8,128)(2,1)} async-done(((bf16[24,16,896]{2,1,0:T(8,128)(2,1)}), bf16[24,128,896]{2,1,0:T(8,128)(2,1)}) %all-gather.2.cloned.1.call-update) | async-done | bytes 5505040 | tf_op jit(solution)/shard_map/all_gather | solution.py:122
  210.6 7.3 %convolution_convert_fusion = bf16[3072,512]{1,0:T(8,128)(2,1)} fusion(bf16[3072,896]{1,0:T(8,128)(2,1)} %bitcast.54, bf16[896,512]{1,0:T(8,128)(2,1)S(1)} %copy-done), kind=kOutput, calls=%fused_computation.7 | convolution fusion | flops 2820145152 | bytes 9568256 | tf_op jit(solution)/shard_map/dot_general | solution.py:126
  218.0 5.7 %reshape_reshape.3 = bf16[12,256,4,128]{3,2,1,0:T(4,128)(2,1)} reshape(bf16[3072,512]{1,0:T(8,128)(2,1)} %convolution_convert_fusion) | data formatting | bytes 6291456 | tf_op jit(solution)/shard_map/reshape;reshape | solution.py:33
  223.6 6.5 %multiply_reduce_fusion.1 = (f32[3072,4]{0,1:T(4,128)S(1)}, f32[3072,4,128]{2,0,1:T(8,128)S(1)}) fusion(bf16[3072,896,1]{1,0,2:T(8,128)(2,1)} %bitcast.55, bf16[4,128,896]{2,1,0:T(8,128)(2,1)S(1)} %bitcast.53), kind=kOutput, calls=%fused_computation.5 | convolution fusion | flops 2821705728 | bytes 12763136 | tf_op jit(solution)/shard_map/dot_general | solution.py:125
  230.2 1.9 multiply_convert_fusion.1
  232.1 1.3 fusion.15
  234.0 1.2 fusion.31
  (67 shorter events, 9.7 us)
Async XLA Ops:
  6.5 204.1 %copy-start = (bf16[896,512]{1,0:T(8,128)(2,1)S(1)}, bf16[896,512]{1,0:T(8,128)(2,1)}, u32[]{:S(2)}) copy-start(bf16[896,512]{1,0:T(8,128)(2,1)} %param.15) | copy-start | bytes 2752516
  6.5 3.0 %copy-start.11 = (bf16[448,896]{1,0:T(8,128)(2,1)S(1)}, bf16[448,896]{1,0:T(8,128)(2,1)}, u32[]{:S(2)}) copy-start(bf16[448,896]{1,0:T(8,128)(2,1)} %param.12) | copy-start | bytes 2408452
  6.5 3.0 %copy-start.12 = (bf16[896,448]{0,1:T(8,128)(2,1)S(1)}, bf16[896,448]{0,1:T(8,128)(2,1)}, u32[]{:S(2)}) copy-start(bf16[896,448]{0,1:T(8,128)(2,1)} %param.11) | copy-start | bytes 2408452
  6.5 90.1 %reduce-scatter.2.cloned.1.call-start = ((), (), s32[]{:S(2)}) async-start(), calls=%async_computation.3 | async-start | bytes 4128768 | tf_op jit(solution)/shard_map/reduce_scatter | solution.py:103
  17.3 1.1 copy-start.9
  17.3 8.6 %copy-start.10 = (s32[12,2]{0,1:T(2,128)S(1)}, s32[12,2]{0,1:T(2,128)}, u32[]{:S(2)}) copy-start(s32[12,2]{0,1:T(2,128)} %param.9) | copy-start | bytes 292
  19.4 30.1 %collective-permute-start.1 = (bf16[705,512]{1,0:T(8,128)(2,1)}, bf16[705,512]{1,0:T(8,128)(2,1)S(1)}, u32[]{:S(2)}, u32[]{:S(2)}) collective-permute-start(bf16[705,512]{1,0:T(8,128)(2,1)} %slice.6), channel_id=1, source_target_pairs={{0,7},{1,0},{2,1},{3,2},{4,3},{5,4},{6,5},{7,6},{8,15},{9,8},{10,9... | collective-permute-start | bytes 2165768 | tf_op jit(solution)/shard_map/ppermute | solution.py:57
  25.8 27.1 %collective-permute-start = (bf16[705,512]{1,0:T(8,128)(2,1)}, bf16[705,512]{1,0:T(8,128)(2,1)S(1)}, u32[]{:S(2)}, u32[]{:S(2)}) collective-permute-start(bf16[705,512]{1,0:T(8,128)(2,1)} %slice.6), channel_id=1, source_target_pairs={{0,1},{1,2},{2,3},{3,4},{4,5},{5,6},{6,7},{7,0},{8,9},{9,10},{10,1... | collective-permute-start | bytes 2165768 | tf_op jit(solution)/shard_map/ppermute | solution.py:54
  49.5 21.4 %copy-start.5 = (bf16[705,512]{1,0:T(8,128)(2,1)}, bf16[705,512]{1,0:T(8,128)(2,1)S(1)}, u32[]{:S(2)}) copy-start(bf16[705,512]{1,0:T(8,128)(2,1)S(1)} %collective-permute-done.1) | copy-start | bytes 2165764
  49.5 50.6 %collective-permute-start.3 = (bf16[705,512]{1,0:T(8,128)(2,1)S(1)}, bf16[705,512]{1,0:T(8,128)(2,1)}, u32[]{:S(2)}, u32[]{:S(2)}) collective-permute-start(bf16[705,512]{1,0:T(8,128)(2,1)S(1)} %collective-permute-done.1), channel_id=1, source_target_pairs={{0,7},{1,0},{2,1},{3,2},{4,3},{5,4},{6,5},{7,6},{8,15},{9,8},{10,9... | collective-permute-start | bytes 2165768 | tf_op jit(solution)/shard_map/ppermute | solution.py:57
  52.9 18.0 %copy-start.7 = (bf16[705,512]{1,0:T(8,128)(2,1)}, bf16[705,512]{1,0:T(8,128)(2,1)S(1)}, u32[]{:S(2)}) copy-start(bf16[705,512]{1,0:T(8,128)(2,1)S(1)} %collective-permute-done) | copy-start | bytes 2165764
  52.9 47.2 %collective-permute-start.2 = (bf16[705,512]{1,0:T(8,128)(2,1)S(1)}, bf16[705,512]{1,0:T(8,128)(2,1)}, u32[]{:S(2)}, u32[]{:S(2)}) collective-permute-start(bf16[705,512]{1,0:T(8,128)(2,1)S(1)} %collective-permute-done), channel_id=1, source_target_pairs={{0,1},{1,2},{2,3},{3,4},{4,5},{5,6},{6,7},{7,0},{8,9},{9,10},{10,1... | collective-permute-start | bytes 2165768 | tf_op jit(solution)/shard_map/ppermute | solution.py:54
  53.7 18.3 %all-to-all-start = ((s32[32,1,2]{2,1,0:T(1,128)}), s32[32,1,2]{2,1,0:T(1,128)S(1)}, u32[]{:S(2)}, u32[]{:S(2)}) async-start(s32[32,1,2]{2,1,0:T(1,128)} %bitcast.2), calls=%async_computation.1 | async-start | bytes 32768 | tf_op jit(solution)/shard_map/all_to_all | solution.py:117
  100.1 33.1 %all-to-all-start.1 = ((bf16[32,2,16,896]{3,2,1,0:T(8,128)(2,1)}), bf16[32,2,16,896]{3,2,1,0:T(8,128)(2,1)S(1)}, u32[]{:S(2)}, u32[]{:S(2)}) async-start(bf16[32,2,16,896]{3,2,1,0:T(8,128)(2,1)} %bitcast.4), calls=%async_computation.2 | async-start | bytes 3670016 | tf_op jit(solution)/shard_map/all_to_all | solution.py:119
  107.6 103.0 %all-gather.2.cloned.1.call-start = ((), (), s32[]{:S(2)}) async-start(), calls=%async_computation.4 | async-start | bytes 6193152 | tf_op jit(solution)/shard_map/all_gather | solution.py:122
  107.7 19.2 %collective-permute-start.4 = (bf16[705,512]{1,0:T(8,128)(2,1)}, bf16[705,512]{1,0:T(8,128)(2,1)}, u32[]{:S(2)}, u32[]{:S(2)}) collective-permute-start(bf16[705,512]{1,0:T(8,128)(2,1)} %collective-permute-done.2), channel_id=1, source_target_pairs={{0,1},{1,2},{2,3},{3,4},{4,5},{5,6},{6,7},{7,0},{8,9},{9,10},{10,1... | collective-permute-start | bytes 2165768 | tf_op jit(solution)/shard_map/ppermute | solution.py:54
  107.8 26.9 %collective-permute-start.5 = (bf16[705,512]{1,0:T(8,128)(2,1)}, bf16[705,512]{1,0:T(8,128)(2,1)}, u32[]{:S(2)}, u32[]{:S(2)}) collective-permute-start(bf16[705,512]{1,0:T(8,128)(2,1)} %collective-permute-done.3), channel_id=1, source_target_pairs={{0,7},{1,0},{2,1},{3,2},{4,3},{5,4},{6,5},{7,6},{8,15},{9,8},{10,9... | collective-permute-start | bytes 2165768 | tf_op jit(solution)/shard_map/ppermute | solution.py:57
  126.9 18.2 %collective-permute-start.6 = (bf16[705,512]{1,0:T(8,128)(2,1)}, bf16[705,512]{1,0:T(8,128)(2,1)S(1)}, u32[]{:S(2)}, u32[]{:S(2)}) collective-permute-start(bf16[705,512]{1,0:T(8,128)(2,1)} %collective-permute-done.4), channel_id=1, source_target_pairs={{0,1},{1,2},{2,3},{3,4},{4,5},{5,6},{6,7},{7,0},{8,9},{9,10},{10,1... | collective-permute-start | bytes 2165768 | tf_op jit(solution)/shard_map/ppermute | solution.py:54
  145.3 4.3 %copy-start.8 = (bf16[705,512]{1,0:T(8,128)(2,1)S(1)}, bf16[705,512]{1,0:T(8,128)(2,1)}, u32[]{:S(2)}) copy-start(bf16[705,512]{1,0:T(8,128)(2,1)} %copy-done.7) | copy-start | bytes 2165764
  147.6 2.6 %copy-start.2 = (bf16[4096,512]{1,0:T(8,128)(2,1)S(1)}, bf16[4096,512]{1,0:T(8,128)(2,1)}, u32[]{:S(2)}) copy-start(bf16[4096,512]{1,0:T(8,128)(2,1)} %param.13) | copy-start | bytes 12582916
  147.6 3.1 %copy-start.6 = (bf16[705,512]{1,0:T(8,128)(2,1)S(1)}, bf16[705,512]{1,0:T(8,128)(2,1)}, u32[]{:S(2)}) copy-start(bf16[705,512]{1,0:T(8,128)(2,1)} %copy-done.5) | copy-start | bytes 2165764
  218.0 5.7 %copy-start.4 = (bf16[512,896]{1,0:T(8,128)(2,1)S(1)}, bf16[512,896]{1,0:T(8,128)(2,1)}, u32[]{:S(2)}) copy-start(bf16[512,896]{1,0:T(8,128)(2,1)} %copy.62) | copy-start | bytes 2752516
  232.1 1.9 copy-start.3
  234.0 3.1 %copy-start.1 = (bf16[896,512]{1,0:T(8,128)(2,1)S(1)}, bf16[896,512]{1,0:T(8,128)(2,1)}, u32[]{:S(2)}) copy-start(bf16[896,512]{1,0:T(8,128)(2,1)} %param.15) | copy-start | bytes 2752516
Sparse Core Ops, SparseCore 0:
  17.4 79.2 reduce-scatter.1
  145.3 65.2 all-gather.1

commit v3 on v2

--- a/solution.py
+++ b/solution.py
@@ -21,14 +21,10 @@
     return scaled.astype(jnp.bfloat16)
 
 
-def attend(queries, keys, values):
-    seq_rows = queries.shape[0] + SPAN - 1
-    heads_here = queries.shape[1]
-    span_count = seq_rows // SPAN
-    shifted = jnp.concatenate(
-        [queries, jnp.zeros((SPAN - 1, heads_here, HD), jnp.bfloat16)], axis=0
-    )
-    windows = shifted.reshape(span_count, SPAN, heads_here, HD)
+def attend(windows_flat, keys, values):
+    heads_here = windows_flat.shape[1]
+    span_count = windows_flat.shape[0] // SPAN
+    windows = windows_flat.reshape(span_count, SPAN, heads_here, HD)
     key_blocks = keys.reshape(span_count, KN * NTOK, heads_here, HD)
     value_blocks = values.reshape(span_count, KN * NTOK, heads_here, HD)
     scores = jnp.einsum("cqhd,ckhd->chqk", windows, key_blocks, preferred_element_type=jnp.float32)
@@ -36,10 +32,7 @@
     expo = jnp.exp(scores)
     weights = (expo / jnp.sum(expo, axis=-1, keepdims=True)).astype(jnp.bfloat16)
     mixed = jnp.einsum("chqk,ckhd->cqhd", weights, value_blocks, preferred_element_type=jnp.float32)
-    mixed = mixed.astype(jnp.bfloat16).reshape(seq_rows, heads_here * HD)
-    leading = jnp.zeros((SPAN - 1, heads_here * HD), jnp.bfloat16)
-    return jnp.concatenate([leading, mixed[: seq_rows - SPAN + 1]], axis=0)
-
+    return mixed.astype(jnp.bfloat16).reshape(span_count * SPAN, heads_here * HD)
 
 def ring_hops(states, n):
     to_right = [(i, (i + 1) % n) for i in range(n)]
@@ -100,32 +93,51 @@
     active = jax.nn.gelu(inner).astype(jnp.bfloat16)
     partial = jnp.einsum("btf,fe->bte", active, w_down, preferred_element_type=jnp.float32)
     rows_here = block_tokens // tensor_count
-    summed = lax.psum_scatter(
-        partial.astype(jnp.bfloat16), "tensor", scatter_dimension=1, tiled=True
-    ).astype(jnp.float32)
-    raw_own = lax.dynamic_slice_in_dim(
-        raw_float, lax.axis_index("tensor") * rows_here, rows_here, 1
-    )
-    encoded_own = (raw_own + summed).astype(jnp.bfloat16)
     states = hidden_states[SPAN - 1 :]
     steps = ring_hops(states, tensor_count)
     got = {0: states}
     for step in steps:
         got.update(step)
-    early = [v for step in steps[: len(steps) // 2] for v in step.values()]
+    first = list(steps[0].values())
+    middle = [v for step in steps[1 : len(steps) // 2] for v in step.values()]
     late = [v for step in steps[len(steps) // 2 :] for v in step.values()]
+    partial, _ = lax.optimization_barrier((partial.astype(jnp.bfloat16), first))
+    summed = lax.psum_scatter(partial, "tensor", scatter_dimension=1, tiled=True).astype(
+        jnp.float32
+    )
+    raw_own = lax.dynamic_slice_in_dim(
+        raw_float, lax.axis_index("tensor") * rows_here, rows_here, 1
+    )
+    encoded_own = (raw_own + summed).astype(jnp.bfloat16)
     asked = lax.all_to_all(requests, "dp", split_axis=0, concat_axis=0, tiled=True)
-    served, _ = lax.optimization_barrier((encoded_own[asked], early))
+    served, _ = lax.optimization_barrier((encoded_own[asked], middle))
     replies = lax.all_to_all(served, "dp", split_axis=0, concat_axis=0, tiled=True)
     mine = replies.reshape(dp_count * capacity, rows_here, enc_width)[slots]
     mine, _ = lax.optimization_barrier((mine, late))
-    encoded = lax.all_gather(mine, "tensor", axis=1, tiled=True)
     queries = head_norm(ring_query(got, w_query, tensor_count))
-    flat_encoded = encoded.reshape(-1, enc_width)
-    keys = head_norm(jnp.dot(flat_encoded, w_key, preferred_element_type=jnp.float32))
-    values = jnp.dot(flat_encoded, w_value, preferred_element_type=jnp.float32).astype(jnp.bfloat16)
-    values = values.reshape(flat_encoded.shape[0], -1, HD)
-    return attend(queries, keys, values)
+    halves = 2
+    block_share = request_count // halves
+    query_share = queries.shape[0] + SPAN - 1
+    query_share = query_share // halves
+    padded = jnp.concatenate(
+        [queries, jnp.zeros((SPAN - 1,) + queries.shape[1:], queries.dtype)], axis=0
+    )
+    mixed = []
+    for half in range(halves):
+        part = lax.all_gather(
+            mine[half * block_share : (half + 1) * block_share], "tensor", axis=1, tiled=True
+        )
+        flat_encoded = part.reshape(-1, enc_width)
+        keys = head_norm(jnp.dot(flat_encoded, w_key, preferred_element_type=jnp.float32))
+        values = jnp.dot(flat_encoded, w_value, preferred_element_type=jnp.float32).astype(
+            jnp.bfloat16
+        )
+        values = values.reshape(flat_encoded.shape[0], -1, HD)
+        mixed.append(attend(padded[half * query_share : (half + 1) * query_share], keys, values))
+    mixed = jnp.concatenate(mixed, axis=0)
+    heads_width = mixed.shape[1]
+    leading = jnp.zeros((SPAN - 1, heads_width), jnp.bfloat16)
+    return jnp.concatenate([leading, mixed[: mixed.shape[0] - SPAN + 1]], axis=0)
 
 
 def solution(mesh):

time: 245 us -> 246 us (level)
  matrix products: 35.9 us -> 46.1 us
  waiting for transfers between devices: 129 us -> 124 us
  local copies, waits for them, and re-layouts: 19.8 us -> 15.9 us
  starting transfers between devices: 31.4 us -> 28 us
  other arithmetic: 13.6 us -> 16.1 us
    ppermute x3, waiting for transfers between devices: 23.2 us -> 4.45 us  [ring_hops(): going_left = lax.ppermute(going_left, 'tensor', to_left)]
    reduce_scatter x1, waiting for transfers between devices: 24.4 us -> 36.6 us  [shards(): lax.psum_scatter(partial, 'tensor', scatter_dimension=1, tiled=True)]
    dot_general x8, matrix products: 11.5 us -> 16.5 us  [ring_query(): term = jnp.dot(got[offset], rows, preferred_element_type=jnp.float32)]
    ppermute x4, waiting for transfers between devices: 27 us -> 30.9 us  [ring_hops(): going_right = lax.ppermute(going_right, 'tensor', to_right)]
    dot_general x1 -> x2, matrix products: 6.5 us -> 10 us  [shards(): jnp.dot(flat_encoded, w_key, preferred_element_type=jnp.float32)]
    dot_general x1 -> x2, matrix products: 1.2 us -> 4.5 us  [attend(): jnp.einsum('chqk,ckhd->cqhd', weights, value_blocks, preferred_element_ty...]
    all_gather x1 -> x2, waiting for transfers between devices: 47.6 us -> 44.7 us  [shards(): lax.all_gather(mine[half * block_share:(half + 1) * block_share], 'tensor...]
    ppermute x3, starting transfers between devices: 12.5 us -> 9.7 us  [ring_hops(): going_left = lax.ppermute(going_left, 'tensor', to_left)]
  transfers between devices with their start and end apart: 11 -> 12, of which waited for: 7 -> 9; matrix products, arithmetic and copies ran while one was open for 12% -> 24% of each run, Pallas kernels for 0% -> 0%
where the time goes in v3:
time: 246 us; the launch traced here: 244 us
  waiting for transfers between devices  124 us (50%)
  matrix products  46.1 us (19%)
  starting transfers between devices  28 us (11%)
  other arithmetic  16.1 us (7%)
  local copies, waits for them, and re-layouts  15.9 us (6%)
  between operations  13.6 us (6%)
    all_gather x2, waiting for transfers between devices, shards(): lax.all_gather(mine[half * block_share:(half + 1) * block_share], 'tensor...  44.7 us
    reduce_scatter x1, waiting for transfers between devices, shards(): lax.psum_scatter(partial, 'tensor', scatter_dimension=1, tiled=True)  36.6 us
    ppermute x4, waiting for transfers between devices, ring_hops(): going_right = lax.ppermute(going_right, 'tensor', to_right)  30.9 us
    dot_general x8, matrix products, ring_query(): term = jnp.dot(got[offset], rows, preferred_element_type=jnp.float32)  16.5 us
    dot_general x2, matrix products, shards(): jnp.dot(flat_encoded, w_key, preferred_element_type=jnp.float32)  10 us
    ppermute x3, starting transfers between devices, ring_hops(): going_left = lax.ppermute(going_left, 'tensor', to_left)  9.7 us
    all_to_all x1, starting transfers between devices, shards(): lax.all_to_all(requests, 'dp', split_axis=0, concat_axis=0, tiled=True)  9.46 us
    dot_general x1, matrix products, shards(): jnp.einsum('btf,fe->bte', active, w_down, preferred_element_type=jnp.floa...  8.02 us
  transfers between devices with their start and end apart: 12, of which 9 were waited for; matrix products, arithmetic and copies ran while one was open for 24% of the time, Pallas kernels for 0%

profile of v3, /device:TPU:1, one launch (start us, length us, event | category | flops | bytes accessed | tf_op | source)
XLA Modules:
  0.0 243.6 jit_solution(12530647677442331185)
XLA Ops:
  6.5 2.2 slice.18
  8.8 6.4 %collective-permute-start.1 = (bf16[705,512]{1,0:T(8,128)(2,1)}, bf16[705,512]{1,0:T(8,128)(2,1)S(1)}, u32[]{:S(2)}, u32[]{:S(2)}) collective-permute-start(bf16[705,512]{1,0:T(8,128)(2,1)} %slice.18), channel_id=1, source_target_pairs={{0,7},{1,0},{2,1},{3,2},{4,3},{5,4},{6,5},{7,6},{8,15},{9,8},{10,9... | collective-permute-start | bytes 2165768 | tf_op jit(solution)/shard_map/ppermute | solution.py:50
  15.2 2.8 %multiply_reduce_fusion = f32[16,128]{1,0:T(8,128)S(1)} fusion(bf16[16,128,896]{2,1,0:T(8,128)(2,1)} %param.10), kind=kLoop, calls=%fused_computation.3 | loop fusion | flops 5502976 | bytes 3678208 | tf_op jit(solution)/shard_map/reduce_sum | solution.py:90
  18.0 8.0 %convolution_convert_fusion.2 = bf16[16,128,896]{2,1,0:T(8,128)(2,1)} fusion(f32[16,128]{1,0:T(8,128)S(1)} %add_rsqrt_fusion.3, bf16[16,128,896]{2,1,0:T(8,128)(2,1)} %param.10, bf16[448,896]{1,0:T(8,128)(2,1)} %param.12, bf16[896,448]{0,1:T(8,128)(2,1)} %param.11), kind=kOutput, calls=%fused_computation.22 | convolution fusion | flops 3303931904 | bytes 8953856 | tf_op jit(solution)/shard_map/btf,fe->bte/dot_general | solution.py:94
  26.0 4.4 %collective-permute-done.1 = bf16[705,512]{1,0:T(8,128)(2,1)S(1)} collective-permute-done((bf16[705,512]{1,0:T(8,128)(2,1)}, bf16[705,512]{1,0:T(8,128)(2,1)S(1)}, u32[]{:S(2)}, u32[]{:S(2)}) %collective-permute-start.1) | collective-permute-done | bytes 721952 | tf_op jit(solution)/shard_map/ppermute | solution.py:50
  30.5 3.0 %collective-permute-done = bf16[705,512]{1,0:T(8,128)(2,1)S(1)} collective-permute-done((bf16[705,512]{1,0:T(8,128)(2,1)}, bf16[705,512]{1,0:T(8,128)(2,1)S(1)}, u32[]{:S(2)}, u32[]{:S(2)}) %collective-permute-start) | collective-permute-done | bytes 721952 | tf_op jit(solution)/shard_map/ppermute | solution.py:47
  36.4 9.5 %all-to-all-start = ((s32[32,1,2]{2,1,0:T(1,128)}), s32[32,1,2]{2,1,0:T(1,128)S(1)}, u32[]{:S(2)}, u32[]{:S(2)}) async-start(s32[32,1,2]{2,1,0:T(1,128)} %bitcast.2), calls=%async_computation.1 | async-start | bytes 32768 | tf_op jit(solution)/shard_map/all_to_all | solution.py:112
  45.9 5.8 %convert_element_type.53 = f32[16,128,896]{2,1,0:T(8,128)} convert(bf16[16,128,896]{2,1,0:T(8,128)(2,1)} %param.10) | non-fusion elementwise | flops 1835008 | bytes 11010048 | tf_op jit(solution)/shard_map/convert_element_type | solution.py:88
  53.1 36.6 %reduce-scatter.2.cloned.1.call-done = bf16[16,16,896]{2,1,0:T(8,128)(2,1)} async-done(((bf16[16,128,896]{2,1,0:T(8,128)(2,1)}), bf16[16,16,896]{2,1,0:T(8,128)(2,1)}) %reduce-scatter.2.cloned.1.call-update) | async-done | bytes 458768 | tf_op jit(solution)/shard_map/reduce_scatter | solution.py:105
  91.1 2.0 gather_fusion
  93.1 7.6 %all-to-all-start.1 = ((bf16[32,2,16,896]{3,2,1,0:T(8,128)(2,1)}), bf16[32,2,16,896]{3,2,1,0:T(8,128)(2,1)S(1)}, u32[]{:S(2)}, u32[]{:S(2)}) async-start(bf16[32,2,16,896]{3,2,1,0:T(8,128)(2,1)} %bitcast.4), calls=%async_computation.2 | async-start | bytes 3670016 | tf_op jit(solution)/shard_map/all_to_all | solution.py:114
  100.8 2.7 %collective-permute-start.5 = (bf16[705,512]{1,0:T(8,128)(2,1)}, bf16[705,512]{1,0:T(8,128)(2,1)}, u32[]{:S(2)}, u32[]{:S(2)}) collective-permute-start(bf16[705,512]{1,0:T(8,128)(2,1)} %collective-permute-done.3), channel_id=1, source_target_pairs={{0,7},{1,0},{2,1},{3,2},{4,3},{5,4},{6,5},{7,6},{8,15},{9,8},{10,9... | collective-permute-start | bytes 2165768 | tf_op jit(solution)/shard_map/ppermute | solution.py:50
  103.5 16.5 %collective-permute-done.4 = bf16[705,512]{1,0:T(8,128)(2,1)} collective-permute-done((bf16[705,512]{1,0:T(8,128)(2,1)}, bf16[705,512]{1,0:T(8,128)(2,1)}, u32[]{:S(2)}, u32[]{:S(2)}) %collective-permute-start.4) | collective-permute-done | bytes 721952 | tf_op jit(solution)/shard_map/ppermute | solution.py:47
  120.1 6.1 %all-to-all-done.1 = bf16[32,2,16,896]{3,2,1,0:T(8,128)(2,1)S(1)} async-done(((bf16[32,2,16,896]{3,2,1,0:T(8,128)(2,1)}), bf16[32,2,16,896]{3,2,1,0:T(8,128)(2,1)S(1)}, u32[]{:S(2)}, u32[]{:S(2)}) %all-to-all-start.1) | async-done | bytes 1835040 | tf_op jit(solution)/shard_map/all_to_all | solution.py:114
  126.9 11.4 %collective-permute-done.6 = bf16[705,512]{1,0:T(8,128)(2,1)} collective-permute-done((bf16[705,512]{1,0:T(8,128)(2,1)}, bf16[705,512]{1,0:T(8,128)(2,1)}, u32[]{:S(2)}, u32[]{:S(2)}) %collective-permute-start.6) | collective-permute-done | bytes 721952 | tf_op jit(solution)/shard_map/ppermute | solution.py:47
  144.3 2.7 %convolution_add_fusion.3 = f32[512,705]{0,1:T(8,128)} fusion(f32[512,705]{0,1:T(8,128)S(1)} %fusion.66, bf16[705,512]{1,0:T(8,128)(2,1)S(1)} %copy-done.4, bf16[4096,512]{1,0:T(8,128)(2,1)} %param.13, s32[]{:T(128)S(6)} %select_n.127), kind=kOutput, calls=%fused_computation.45 | convolution fusion | flops 369984000 | bytes 4133892 | tf_op jit(solution)/shard_map/dot_general | solution.py:62
  147.0 1.9 fusion.58
  149.0 1.9 convolution_add_fusion.2
  150.9 1.8 fusion.60
  152.7 1.8 convolution_add_fusion.1
  154.5 3.1 %fusion.33 = f32[705,512]{1,0:T(8,128)} fusion(f32[512,705]{0,1:T(8,128)S(1)} %fusion.56, f32[512,705]{0,1:T(8,128)S(1)} %fusion.58, f32[512,705]{0,1:T(8,128)S(1)} %fusion.60, f32[512,705]{0,1:T(8,128)S(1)} %convolution_add_fusion.1, bf16[705,512]{1,0:T(8,128)(2,1)} %collective-permute-done.6, bf16[4096,512]{1,0:T(8,128)(2,1)} %param.13, s32[]{:T(128)S(6)} %select_n.133), kind=kOutput, calls=%fused_computation.49 | convolution fusion | flops 371066880 | bytes 8472580 | tf_op jit(solution)/shard_map/dot_general | solution.py:62
  160.9 17.2 %all-gather.3.cloned.1.call-done = bf16[12,128,896]{2,1,0:T(8,128)(2,1)} async-done(((bf16[12,16,896]{2,1,0:T(8,128)(2,1)}), bf16[12,128,896]{2,1,0:T(8,128)(2,1)}) %all-gather.3.cloned.1.call-update) | async-done | bytes 2752528 | tf_op jit(solution)/shard_map/all_gather | solution.py:127
  178.0 3.6 %convolution_convert_fusion.1 = bf16[1536,512]{1,0:T(8,128)(2,1)S(1)} fusion(bf16[1536,896]{1,0:T(8,128)(2,1)} %bitcast.73, bf16[896,512]{1,0:T(8,128)(2,1)S(1)} %copy-done), kind=kOutput, calls=%fused_computation.21 | convolution fusion | flops 1410072576 | bytes 5242880 | tf_op jit(solution)/shard_map/dot_general | solution.py:132
  181.6 1.9 reshape_reshape.6
  183.5 4.4 %multiply_reduce_fusion.2 = (f32[1536,4]{0,1:T(4,128)S(1)}, f32[1536,4,128]{2,0,1:T(8,128)S(1)}) fusion(bf16[1536,896,1]{1,0,2:T(8,128)(2,1)} %bitcast.74, bf16[4,128,896]{2,1,0:T(8,128)(2,1)} %bitcast.71), kind=kOutput, calls=%fused_computation.19 | convolution fusion | flops 1410852864 | bytes 6840320 | tf_op jit(solution)/shard_map/dot_general | solution.py:131
  189.8 2.6 %fusion.44 = bf16[6,64,4,128]{3,1,2,0:T(8,128)(2,1)} fusion(bf16[6,256,4,128]{3,2,1,0:T(4,128)(2,1)} %reshape_reshape.6, f32[6,4,64,256]{3,2,1,0:T(8,128)S(1)} %multiply_exponential_fusion.1), kind=kOutput, calls=%fused_computation.56 | convolution fusion | flops 101648128 | bytes 3538944 | tf_op jit(solution)/shard_map/chqk,ckhd->cqhd/dot_general | solution.py:34
  193.7 27.5 %all-gather.5.cloned.1.call-done = bf16[12,128,896]{2,1,0:T(8,128)(2,1)} async-done(((bf16[12,16,896]{2,1,0:T(8,128)(2,1)}), bf16[12,128,896]{2,1,0:T(8,128)(2,1)}) %all-gather.5.cloned.1.call-update) | async-done | bytes 2752528 | tf_op jit(solution)/shard_map/all_gather | solution.py:127
  221.3 5.6 %multiply_reduce_fusion.1 = (f32[1536,4]{0,1:T(4,128)S(1)}, f32[1536,4,128]{2,0,1:T(8,128)}) fusion(bf16[1536,896,1]{1,0,2:T(8,128)(2,1)} %bitcast.75, bf16[4,128,896]{2,1,0:T(8,128)(2,1)} %bitcast.72), kind=kOutput, calls=%fused_computation.17 | convolution fusion | flops 1410852864 | bytes 6840320 | tf_op jit(solution)/shard_map/dot_general | solution.py:131
  226.9 1.8 convolution_convert_fusion
  228.7 1.9 reshape_reshape.7
  230.6 2.4 multiply_convert_fusion.2
  233.7 1.9 fusion.41
  (72 shorter events, 21.2 us)
Async XLA Ops:
  6.5 171.5 %copy-start = (bf16[896,512]{1,0:T(8,128)(2,1)S(1)}, bf16[896,512]{1,0:T(8,128)(2,1)}, u32[]{:S(2)}) copy-start(bf16[896,512]{1,0:T(8,128)(2,1)} %param.15) | copy-start | bytes 2752516
  6.5 83.2 %reduce-scatter.2.cloned.1.call-start = ((), (), s32[]{:S(2)}) async-start(), calls=%async_computation.3 | async-start | bytes 4128768 | tf_op jit(solution)/shard_map/reduce_scatter | solution.py:105
  8.8 21.7 %collective-permute-start.1 = (bf16[705,512]{1,0:T(8,128)(2,1)}, bf16[705,512]{1,0:T(8,128)(2,1)S(1)}, u32[]{:S(2)}, u32[]{:S(2)}) collective-permute-start(bf16[705,512]{1,0:T(8,128)(2,1)} %slice.18), channel_id=1, source_target_pairs={{0,7},{1,0},{2,1},{3,2},{4,3},{5,4},{6,5},{7,6},{8,15},{9,8},{10,9... | collective-permute-start | bytes 2165768 | tf_op jit(solution)/shard_map/ppermute | solution.py:50
  15.2 18.3 %collective-permute-start = (bf16[705,512]{1,0:T(8,128)(2,1)}, bf16[705,512]{1,0:T(8,128)(2,1)S(1)}, u32[]{:S(2)}, u32[]{:S(2)}) collective-permute-start(bf16[705,512]{1,0:T(8,128)(2,1)} %slice.18), channel_id=1, source_target_pairs={{0,1},{1,2},{2,3},{3,4},{4,5},{5,6},{6,7},{7,0},{8,9},{9,10},{10,1... | collective-permute-start | bytes 2165768 | tf_op jit(solution)/shard_map/ppermute | solution.py:47
  26.0 7.5 %copy-start.8 = (s32[12,2]{0,1:T(2,128)S(1)}, s32[12,2]{0,1:T(2,128)}, u32[]{:S(2)}) copy-start(s32[12,2]{0,1:T(2,128)} %param.9) | copy-start | bytes 292
  30.5 3.6 %copy-start.3 = (bf16[705,512]{1,0:T(8,128)(2,1)}, bf16[705,512]{1,0:T(8,128)(2,1)S(1)}, u32[]{:S(2)}) copy-start(bf16[705,512]{1,0:T(8,128)(2,1)S(1)} %collective-permute-done.1) | copy-start | bytes 2165764
  33.5 1.2 copy-start.5
  34.0 59.1 %collective-permute-start.3 = (bf16[705,512]{1,0:T(8,128)(2,1)S(1)}, bf16[705,512]{1,0:T(8,128)(2,1)}, u32[]{:S(2)}, u32[]{:S(2)}) collective-permute-start(bf16[705,512]{1,0:T(8,128)(2,1)S(1)} %collective-permute-done.1), channel_id=1, source_target_pairs={{0,7},{1,0},{2,1},{3,2},{4,3},{5,4},{6,5},{7,6},{8,15},{9,8},{10,9... | collective-permute-start | bytes 2165768 | tf_op jit(solution)/shard_map/ppermute | solution.py:50
  34.7 58.4 %collective-permute-start.2 = (bf16[705,512]{1,0:T(8,128)(2,1)S(1)}, bf16[705,512]{1,0:T(8,128)(2,1)}, u32[]{:S(2)}, u32[]{:S(2)}) collective-permute-start(bf16[705,512]{1,0:T(8,128)(2,1)S(1)} %collective-permute-done), channel_id=1, source_target_pairs={{0,1},{1,2},{2,3},{3,4},{4,5},{5,6},{6,7},{7,0},{8,9},{9,10},{10,1... | collective-permute-start | bytes 2165768 | tf_op jit(solution)/shard_map/ppermute | solution.py:47
  36.4 16.4 %all-to-all-start = ((s32[32,1,2]{2,1,0:T(1,128)}), s32[32,1,2]{2,1,0:T(1,128)S(1)}, u32[]{:S(2)}, u32[]{:S(2)}) async-start(s32[32,1,2]{2,1,0:T(1,128)} %bitcast.2), calls=%async_computation.1 | async-start | bytes 32768 | tf_op jit(solution)/shard_map/all_to_all | solution.py:112
  93.1 33.1 %all-to-all-start.1 = ((bf16[32,2,16,896]{3,2,1,0:T(8,128)(2,1)}), bf16[32,2,16,896]{3,2,1,0:T(8,128)(2,1)S(1)}, u32[]{:S(2)}, u32[]{:S(2)}) async-start(bf16[32,2,16,896]{3,2,1,0:T(8,128)(2,1)} %bitcast.4), calls=%async_computation.2 | async-start | bytes 3670016 | tf_op jit(solution)/shard_map/all_to_all | solution.py:114
  100.7 77.4 %all-gather.3.cloned.1.call-start = ((), (), s32[]{:S(2)}) async-start(), calls=%async_computation.4 | async-start | bytes 3096576 | tf_op jit(solution)/shard_map/all_gather | solution.py:127
  100.7 19.2 %collective-permute-start.4 = (bf16[705,512]{1,0:T(8,128)(2,1)}, bf16[705,512]{1,0:T(8,128)(2,1)}, u32[]{:S(2)}, u32[]{:S(2)}) collective-permute-start(bf16[705,512]{1,0:T(8,128)(2,1)} %collective-permute-done.2), channel_id=1, source_target_pairs={{0,1},{1,2},{2,3},{3,4},{4,5},{5,6},{6,7},{7,0},{8,9},{9,10},{10,1... | collective-permute-start | bytes 2165768 | tf_op jit(solution)/shard_map/ppermute | solution.py:47
  100.8 26.1 %collective-permute-start.5 = (bf16[705,512]{1,0:T(8,128)(2,1)}, bf16[705,512]{1,0:T(8,128)(2,1)}, u32[]{:S(2)}, u32[]{:S(2)}) collective-permute-start(bf16[705,512]{1,0:T(8,128)(2,1)} %collective-permute-done.3), channel_id=1, source_target_pairs={{0,7},{1,0},{2,1},{3,2},{4,3},{5,4},{6,5},{7,6},{8,15},{9,8},{10,9... | collective-permute-start | bytes 2165768 | tf_op jit(solution)/shard_map/ppermute | solution.py:50
  120.0 18.3 %collective-permute-start.6 = (bf16[705,512]{1,0:T(8,128)(2,1)}, bf16[705,512]{1,0:T(8,128)(2,1)}, u32[]{:S(2)}, u32[]{:S(2)}) collective-permute-start(bf16[705,512]{1,0:T(8,128)(2,1)} %collective-permute-done.4), channel_id=1, source_target_pairs={{0,1},{1,2},{2,3},{3,4},{4,5},{5,6},{6,7},{7,0},{8,9},{9,10},{10,1... | collective-permute-start | bytes 2165768 | tf_op jit(solution)/shard_map/ppermute | solution.py:47
  126.9 12.7 %copy-start.2 = (bf16[896,512]{1,0:T(8,128)(2,1)S(1)}, bf16[896,512]{1,0:T(8,128)(2,1)}, u32[]{:S(2)}) copy-start(bf16[896,512]{1,0:T(8,128)(2,1)} %param.14) | copy-start | bytes 2752516
  126.9 14.1 %copy-start.7 = (bf16[768,512]{1,0:T(8,128)(2,1)S(1)}, bf16[768,512]{1,0:T(8,128)(2,1)}, u32[]{:S(2)}) copy-start(bf16[768,512]{1,0:T(8,128)(2,1)} %param.8) | copy-start | bytes 2359300
  139.3 82.0 %all-gather.5.cloned.1.call-start = ((), (), s32[]{:S(2)}) async-start(), calls=%async_computation.5 | async-start | bytes 3096576 | tf_op jit(solution)/shard_map/all_gather | solution.py:127
  140.9 1.7 copy-start.6
  142.6 1.7 copy-start.4
  147.0 1.9 copy-start.1
  221.3 5.7 %copy-start.9 = (bf16[12,128,896]{2,1,0:T(8,128)(2,1)S(1)}, bf16[12,128,896]{2,1,0:T(8,128)(2,1)}, u32[]{:S(2)}) copy-start(bf16[12,128,896]{2,1,0:T(8,128)(2,1)} %all-gather.5.cloned.1.call-done) | copy-start | bytes 8257540
Sparse Core Ops, SparseCore 0:
  33.6 56.0 reduce-scatter.1
  139.4 38.6 all-gather.2
  179.8 41.3 all-gather.4

commit v4 on v3

--- a/solution.py
+++ b/solution.py
@@ -85,55 +85,54 @@
     slot_match = slots[None, :] == jnp.arange(dp_count * capacity, dtype=jnp.int32)[:, None]
     requests = jnp.sum(jnp.where(slot_match, local_rows[None, :], 0), axis=1)
     requests = requests.reshape(dp_count, capacity)
+    pieces = dp_count
+    me_dp = lax.axis_index("dp")
+    up_piece = lax.dynamic_slice_in_dim(w_up, me_dp * (w_up.shape[0] // pieces), w_up.shape[0] // pieces, 0)
+    down_piece = lax.dynamic_slice_in_dim(
+        w_down, me_dp * (w_down.shape[0] // pieces), w_down.shape[0] // pieces, 0
+    )
+    up_all = lax.all_gather(lax.all_gather(up_piece, "tensor"), "dp")
+    down_all = lax.all_gather(lax.all_gather(down_piece, "tensor"), "dp")
+    rows_here = block_tokens // tensor_count
     raw_float = database.astype(jnp.float32)
+    raw_own = lax.dynamic_slice_in_dim(
+        raw_float, lax.axis_index("tensor") * rows_here, rows_here, 1
+    )
     normed = (
-        raw_float * lax.rsqrt(jnp.mean(raw_float * raw_float, axis=-1, keepdims=True) + EPSILON)
+        raw_own * lax.rsqrt(jnp.mean(raw_own * raw_own, axis=-1, keepdims=True) + EPSILON)
     ).astype(jnp.bfloat16)
-    inner = jnp.einsum("bte,ef->btf", normed, w_up, preferred_element_type=jnp.float32)
-    active = jax.nn.gelu(inner).astype(jnp.bfloat16)
-    partial = jnp.einsum("btf,fe->bte", active, w_down, preferred_element_type=jnp.float32)
-    rows_here = block_tokens // tensor_count
     states = hidden_states[SPAN - 1 :]
     steps = ring_hops(states, tensor_count)
     got = {0: states}
     for step in steps:
         got.update(step)
-    first = list(steps[0].values())
-    middle = [v for step in steps[1 : len(steps) // 2] for v in step.values()]
+    early = [v for step in steps[: len(steps) // 2] for v in step.values()]
     late = [v for step in steps[len(steps) // 2 :] for v in step.values()]
-    partial, _ = lax.optimization_barrier((partial.astype(jnp.bfloat16), first))
-    summed = lax.psum_scatter(partial, "tensor", scatter_dimension=1, tiled=True).astype(
-        jnp.float32
-    )
-    raw_own = lax.dynamic_slice_in_dim(
-        raw_float, lax.axis_index("tensor") * rows_here, rows_here, 1
-    )
+    normed, _ = lax.optimization_barrier((normed, early))
+    flat_normed = normed.reshape(shard_blocks * rows_here, pieces, enc_width // pieces)
+    inner = jnp.einsum("ncr,cgrh->ngh", flat_normed, up_all, preferred_element_type=jnp.float32)
+    active = jax.nn.gelu(inner).astype(jnp.bfloat16)
+    active = active.reshape(active.shape[0], tensor_count, pieces, -1)
+    partials = jnp.einsum("ngcr,cgre->gne", active, down_all, preferred_element_type=jnp.float32)
+    summed = jnp.sum(partials.astype(jnp.bfloat16).astype(jnp.float32), axis=0)
+    summed = summed.reshape(shard_blocks, rows_here, enc_width)
     encoded_own = (raw_own + summed).astype(jnp.bfloat16)
     asked = lax.all_to_all(requests, "dp", split_axis=0, concat_axis=0, tiled=True)
-    served, _ = lax.optimization_barrier((encoded_own[asked], middle))
+    served, _ = lax.optimization_barrier((encoded_own[asked], late))
     replies = lax.all_to_all(served, "dp", split_axis=0, concat_axis=0, tiled=True)
     mine = replies.reshape(dp_count * capacity, rows_here, enc_width)[slots]
-    mine, _ = lax.optimization_barrier((mine, late))
     queries = head_norm(ring_query(got, w_query, tensor_count))
-    halves = 2
-    block_share = request_count // halves
-    query_share = queries.shape[0] + SPAN - 1
-    query_share = query_share // halves
     padded = jnp.concatenate(
         [queries, jnp.zeros((SPAN - 1,) + queries.shape[1:], queries.dtype)], axis=0
     )
-    mixed = []
-    for half in range(halves):
-        part = lax.all_gather(
-            mine[half * block_share : (half + 1) * block_share], "tensor", axis=1, tiled=True
-        )
-        flat_encoded = part.reshape(-1, enc_width)
-        keys = head_norm(jnp.dot(flat_encoded, w_key, preferred_element_type=jnp.float32))
-        values = jnp.dot(flat_encoded, w_value, preferred_element_type=jnp.float32).astype(
-            jnp.bfloat16
-        )
-        values = values.reshape(flat_encoded.shape[0], -1, HD)
-        mixed.append(attend(padded[half * query_share : (half + 1) * query_share], keys, values))
+    encoded = lax.all_gather(mine, "tensor", axis=1, tiled=True)
+    flat_encoded = encoded.reshape(-1, enc_width)
+    keys = head_norm(jnp.dot(flat_encoded, w_key, preferred_element_type=jnp.float32))
+    values = jnp.dot(flat_encoded, w_value, preferred_element_type=jnp.float32).astype(
+        jnp.bfloat16
+    )
+    values = values.reshape(flat_encoded.shape[0], -1, HD)
+    mixed = [attend(padded, keys, values)]
     mixed = jnp.concatenate(mixed, axis=0)
     heads_width = mixed.shape[1]
     leading = jnp.zeros((SPAN - 1, heads_width), jnp.bfloat16)

time: 246 us -> 298 us (1.21)
  blocking collectives: 0 us -> 42 us
  local copies, waits for them, and re-layouts: 15.9 us -> 31.8 us
  starting transfers between devices: 28 us -> 41.3 us
  waiting for transfers between devices: 124 us -> 116 us
  other arithmetic: 16.1 us -> 9.35 us
  matrix products: 46.1 us -> 43 us
    all_gather x0 -> x2, blocking collectives: none -> 42 us  [the longest x1 23.3 us: shards(): up_all = lax.all_gather(lax.all_gather(up_piece, 'tensor'), 'dp')]
    reduce_scatter x1 -> x0, waiting for transfers between devices: 36.6 us -> none  [shards(): lax.psum_scatter(partial, 'tensor', scatter_dimension=1, tiled=True)]
    all_gather x2 -> x3, waiting for transfers between devices: 44.7 us -> 67.7 us  [the longest x1 46.8 us: shards(): encoded = lax.all_gather(mine, 'tensor', axis=1, tiled=True)]
    ppermute x4, waiting for transfers between devices: 30.9 us -> 9.13 us  [ring_hops(): going_right = lax.ppermute(going_right, 'tensor', to_right)]
    all_to_all x1, waiting for transfers between devices: 6.11 us -> 25.1 us  [shards(): lax.all_to_all(served, 'dp', split_axis=0, concat_axis=0, tiled=True)]
    all_to_all x1, starting transfers between devices: 9.46 us -> 27 us  [shards(): lax.all_to_all(requests, 'dp', split_axis=0, concat_axis=0, tiled=True)]
    reshape x1 -> x2, local copies, waits for them, and re-layouts: 0.11 us -> 8.32 us  [shards(): normed.reshape(shard_blocks * rows_here, pieces, enc_width // pieces)]
    ppermute x3, waiting for transfers between devices: 4.45 us -> 12.4 us  [ring_hops(): going_left = lax.ppermute(going_left, 'tensor', to_left)]
  transfers between devices with their start and end apart: 12 -> 12, of which waited for: 9 -> 6; matrix products, arithmetic and copies ran while one was open for 24% -> 17% of each run, Pallas kernels for 0% -> 0%
where the time goes in v4:
time: 298 us; the launch traced here: 297 us
  waiting for transfers between devices  116 us (39%)
  matrix products  43 us (14%)
  blocking collectives  42 us (14%)
  starting transfers between devices  41.3 us (14%)
  local copies, waits for them, and re-layouts  31.8 us (11%)
  between operations  13.6 us (5%)
  other arithmetic  9.35 us (3%)
    all_gather x1, waiting for transfers between devices, shards(): encoded = lax.all_gather(mine, 'tensor', axis=1, tiled=True)  46.8 us
    all_to_all x1, starting transfers between devices, shards(): lax.all_to_all(requests, 'dp', split_axis=0, concat_axis=0, tiled=True)  27 us
    all_to_all x1, waiting for transfers between devices, shards(): lax.all_to_all(served, 'dp', split_axis=0, concat_axis=0, tiled=True)  25.1 us
    all_gather x1, blocking collectives, shards(): up_all = lax.all_gather(lax.all_gather(up_piece, 'tensor'), 'dp')  23.3 us
    all_gather x1, waiting for transfers between devices, shards(): down_all = lax.all_gather(lax.all_gather(down_piece, 'tensor'), 'dp')  20.9 us
    all_gather x1, blocking collectives, shards(): down_all = lax.all_gather(lax.all_gather(down_piece, 'tensor'), 'dp')  18.7 us
    ppermute x3, waiting for transfers between devices, ring_hops(): going_left = lax.ppermute(going_left, 'tensor', to_left)  12.4 us
    dot_general x8, matrix products, ring_query(): term = jnp.dot(got[offset], rows, preferred_element_type=jnp.float32)  11.5 us
  transfers between devices with their start and end apart: 12, of which 6 were waited for; matrix products, arithmetic and copies ran while one was open for 17% of the time, Pallas kernels for 0%

profile of v4, /device:TPU:1, one launch (start us, length us, event | category | flops | bytes accessed | tf_op | source)
XLA Modules:
  0.0 297.0 jit_solution(3649769576130073630)
XLA Ops:
  7.8 23.3 %all-gather.5 = bf16[8,28,448]{2,1,0:T(8,128)(2,1)S(1)} all-gather(bf16[1,28,448]{2,1,0:T(8,128)(2,1)S(1)} %bitcast.67), channel_id=2, replica_groups=mesh['dp'=32,'tensor'=8] {'tensor'}, dimensions={0}, use_global_device_ids=true | all-gather | bytes 225792 | tf_op jit(solution)/shard_map/all_gather | solution.py:94
  32.8 18.7 %all-gather.6 = bf16[8,14,896]{2,1,0:T(8,128)(2,1)S(1)} all-gather(bf16[1,14,896]{2,1,0:T(8,128)(2,1)S(1)} %dynamic-slice_bitcast_fusion), channel_id=4, replica_groups=mesh['dp'=32,'tensor'=8] {'tensor'}, dimensions={0}, use_global_device_ids=true | all-gather | bytes 225792 | tf_op jit(solution)/shard_map/all_gather | solution.py:95
  54.2 2.1 collective-permute-start.1
  56.3 9.1 %collective-permute-done = bf16[705,512]{1,0:T(8,128)(2,1)S(1)} collective-permute-done((bf16[705,512]{1,0:T(8,128)(2,1)S(1)}, bf16[705,512]{1,0:T(8,128)(2,1)S(1)}, u32[]{:S(2)}, u32[]{:S(2)}) %collective-permute-start) | collective-permute-done | bytes 721952 | tf_op jit(solution)/shard_map/ppermute | solution.py:47
  66.7 27.0 %all-to-all-start = ((s32[32,1,2]{2,1,0:T(1,128)}), s32[32,1,2]{2,1,0:T(1,128)S(1)}, u32[]{:S(2)}, u32[]{:S(2)}) async-start(s32[32,1,2]{2,1,0:T(1,128)} %bitcast.11), calls=%async_computation | async-start | bytes 32768 | tf_op jit(solution)/shard_map/all_to_all | solution.py:120
  95.0 3.0 %collective-permute-start.3 = (bf16[705,512]{1,0:T(8,128)(2,1)S(1)}, bf16[705,512]{1,0:T(8,128)(2,1)}, u32[]{:S(2)}, u32[]{:S(2)}) collective-permute-start(bf16[705,512]{1,0:T(8,128)(2,1)S(1)} %collective-permute-done.1), channel_id=1, source_target_pairs={{0,7},{1,0},{2,1},{3,2},{4,3},{5,4},{6,5},{7,6},{8,15},{9,8},{10,9... | collective-permute-start | bytes 2165768 | tf_op jit(solution)/shard_map/ppermute | solution.py:50
  99.2 1.5 all-to-all-done
  101.0 12.4 %collective-permute-done.3 = bf16[705,512]{1,0:T(8,128)(2,1)} collective-permute-done((bf16[705,512]{1,0:T(8,128)(2,1)S(1)}, bf16[705,512]{1,0:T(8,128)(2,1)}, u32[]{:S(2)}, u32[]{:S(2)}) %collective-permute-start.3) | collective-permute-done | bytes 721952 | tf_op jit(solution)/shard_map/ppermute | solution.py:50
  113.4 5.3 %reshape.242 = bf16[256,32,28]{2,1,0:T(8,128)(2,1)S(1)} reshape(bf16[16,16,896]{2,1,0:T(8,128)(2,1)S(1)} %fusion.38) | data formatting | bytes 917504 | tf_op jit(solution)/shard_map/reshape | solution.py:112
  118.8 3.0 %copy.94 = bf16[256,32,28]{0,1,2:T(8,128)(2,1)} copy(bf16[256,32,28]{2,1,0:T(8,128)(2,1)S(1)} %reshape.242) | data formatting | bytes 917504 | tf_op jit(solution)/shard_map/reshape | solution.py:112
  121.8 3.5 %collective-permute-start.5 = (bf16[705,512]{1,0:T(8,128)(2,1)}, bf16[705,512]{1,0:T(8,128)(2,1)}, u32[]{:S(2)}, u32[]{:S(2)}) collective-permute-start(bf16[705,512]{1,0:T(8,128)(2,1)} %collective-permute-done.3), channel_id=1, source_target_pairs={{0,7},{1,0},{2,1},{3,2},{4,3},{5,4},{6,5},{7,6},{8,15},{9,8},{10,9... | collective-permute-start | bytes 2165768 | tf_op jit(solution)/shard_map/ppermute | solution.py:50
  125.3 8.6 %fusion.11 = bf16[256,8,448]{0,2,1:T(8,128)(2,1)S(1)} fusion(bf16[32,8,28,448]{3,1,0,2:T(8,128)(2,1)} %bitcast.68, bf16[256,32,28]{0,1,2:T(8,128)(2,1)} %copy.94), kind=kOutput, calls=%fused_computation.19 | convolution fusion | flops 1652424704 | bytes 8716288 | tf_op jit(solution)/shard_map/ncr,cgrh->ngh/dot_general | solution.py:113
  134.9 20.9 %all-gather.13.cloned.1.call-done = bf16[256,14,896]{2,0,1:T(8,128)(2,1)} async-done(((bf16[8,14,896]{2,0,1:T(8,128)(2,1)}), bf16[256,14,896]{2,0,1:T(8,128)(2,1)}) %all-gather.13.cloned.1.call-update) | async-done | bytes 6422544 | tf_op jit(solution)/shard_map/all_gather | solution.py:95
  155.8 6.7 %convert_reduce_fusion = f32[256,896]{1,0:T(8,128)S(1)} fusion(bf16[32,8,14,896]{3,1,0,2:T(8,128)(2,1)} %bitcast.69, bf16[256,8,32,14]{0,1,3,2:T(8,128)(2,1)S(1)} %bitcast.63), kind=kOutput, calls=%fused_computation.5 | convolution fusion | flops 1649442816 | bytes 9175040 | tf_op jit(solution)/shard_map/ngcr,cgre->gne/dot_general | solution.py:116
  163.6 2.0 gather_fusion
  165.6 4.7 %all-to-all-start.1 = ((bf16[32,2,16,896]{3,2,1,0:T(8,128)(2,1)}), bf16[32,2,16,896]{3,2,1,0:T(8,128)(2,1)S(1)}, u32[]{:S(2)}, u32[]{:S(2)}) async-start(bf16[32,2,16,896]{3,2,1,0:T(8,128)(2,1)} %bitcast.13), calls=%async_computation.1 | async-start | bytes 3670016 | tf_op jit(solution)/shard_map/all_to_all | solution.py:122
  170.7 25.1 %all-to-all-done.1 = bf16[32,2,16,896]{3,2,1,0:T(8,128)(2,1)S(1)} async-done(((bf16[32,2,16,896]{3,2,1,0:T(8,128)(2,1)}), bf16[32,2,16,896]{3,2,1,0:T(8,128)(2,1)S(1)}, u32[]{:S(2)}, u32[]{:S(2)}) %all-to-all-start.1) | async-done | bytes 1835040 | tf_op jit(solution)/shard_map/all_to_all | solution.py:122
  195.8 1.5 gather_fusion.1
  197.5 2.3 copy.114
  199.8 2.0 fusion.50
  203.5 1.7 fusion.42
  205.2 1.7 convolution_add_fusion.2
  206.8 1.7 fusion.44
  208.5 1.7 convolution_add_fusion.1
  210.2 1.8 fusion.27
  211.9 1.8 reshape.249
  215.2 46.8 %all-gather.15.cloned.1.call-done = bf16[24,128,896]{2,1,0:T(8,128)(2,1)} async-done(((bf16[24,16,896]{2,1,0:T(8,128)(2,1)}), bf16[24,128,896]{2,1,0:T(8,128)(2,1)}) %all-gather.15.cloned.1.call-update) | async-done | bytes 5505040 | tf_op jit(solution)/shard_map/all_gather | solution.py:128
  262.0 8.7 %multiply_reduce_fusion = (f32[3072,4]{0,1:T(4,128)S(1)}, f32[3072,4,128]{2,0,1:T(8,128)}) fusion(bf16[3072,896,1]{1,0,2:T(8,128)(2,1)} %bitcast.70, bf16[4,128,896]{2,1,0:T(8,128)(2,1)S(1)} %bitcast.65), kind=kOutput, calls=%fused_computation.9 | convolution fusion | flops 2821705728 | bytes 12763136 | tf_op jit(solution)/shard_map/dot_general | solution.py:130
  270.8 4.8 %convolution_convert_fusion = bf16[3072,512]{1,0:T(8,128)(2,1)} fusion(bf16[3072,896]{1,0:T(8,128)(2,1)S(1)} %bitcast.71, bf16[896,512]{1,0:T(8,128)(2,1)S(1)} %copy-done), kind=kOutput, calls=%fused_computation.11 | convolution fusion | flops 2820145152 | bytes 9568256 | tf_op jit(solution)/shard_map/dot_general | solution.py:131
  275.5 5.5 %reshape_reshape.3 = bf16[12,256,4,128]{3,2,1,0:T(4,128)(2,1)} reshape(bf16[3072,512]{1,0:T(8,128)(2,1)} %convolution_convert_fusion) | data formatting | bytes 6291456 | tf_op jit(solution)/shard_map/reshape;reshape | solution.py:29
  281.1 4.4 %multiply_convert_fusion = bf16[3072,4,128]{2,0,1:T(8,128)(2,1)S(1)} fusion(f32[3072,4,128]{2,0,1:T(8,128)} %get-tuple-element.12, f32[3072,4]{0,1:T(4,128)S(1)} %add_rsqrt_fusion), kind=kLoop, calls=%fused_computation.8 | loop fusion | flops 3145728 | bytes 9486336 | tf_op jit(solution)/shard_map/convert_element_type | solution.py:21
  285.5 1.3 fusion.16
  (75 shorter events, 19.0 us)
Async XLA Ops:
  6.5 264.2 %copy-start = (bf16[896,512]{1,0:T(8,128)(2,1)S(1)}, bf16[896,512]{1,0:T(8,128)(2,1)}, u32[]{:S(2)}) copy-start(bf16[896,512]{1,0:T(8,128)(2,1)} %param.15) | copy-start | bytes 2752516
  6.5 58.9 %copy-start.8 = (s32[12,2]{0,1:T(2,128)S(1)}, s32[12,2]{0,1:T(2,128)}, u32[]{:S(2)}) copy-start(s32[12,2]{0,1:T(2,128)} %param.9) | copy-start | bytes 292
  6.5 118.8 %all-gather.11.cloned.1.call-start = ((), (), s32[]{:S(2)}) async-start(), calls=%async_computation.2 | async-start | bytes 7569408 | tf_op jit(solution)/shard_map/all_gather | solution.py:94
  31.9 123.9 %all-gather.13.cloned.1.call-start = ((), (), s32[]{:S(2)}) async-start(), calls=%async_computation.3 | async-start | bytes 6623232 | tf_op jit(solution)/shard_map/all_gather | solution.py:95
  53.5 11.9 %collective-permute-start = (bf16[705,512]{1,0:T(8,128)(2,1)S(1)}, bf16[705,512]{1,0:T(8,128)(2,1)S(1)}, u32[]{:S(2)}, u32[]{:S(2)}) collective-permute-start(bf16[705,512]{1,0:T(8,128)(2,1)S(1)} %slice.6), channel_id=1, source_target_pairs={{0,1},{1,2},{2,3},{3,4},{4,5},{5,6},{6,7},{7,0},{8,9},{9,10},{10,1... | collective-permute-start | bytes 2165768 | tf_op jit(solution)/shard_map/ppermute | solution.py:47
  54.2 40.8 %collective-permute-start.1 = (bf16[705,512]{1,0:T(8,128)(2,1)S(1)}, bf16[705,512]{1,0:T(8,128)(2,1)S(1)}, u32[]{:S(2)}, u32[]{:S(2)}) collective-permute-start(bf16[705,512]{1,0:T(8,128)(2,1)S(1)} %slice.6), channel_id=1, source_target_pairs={{0,7},{1,0},{2,1},{3,2},{4,3},{5,4},{6,5},{7,6},{8,15},{9,8},{10,9... | collective-permute-start | bytes 2165768 | tf_op jit(solution)/shard_map/ppermute | solution.py:50
  65.4 35.6 %copy-start.4 = (bf16[705,512]{1,0:T(8,128)(2,1)}, bf16[705,512]{1,0:T(8,128)(2,1)S(1)}, u32[]{:S(2)}) copy-start(bf16[705,512]{1,0:T(8,128)(2,1)S(1)} %collective-permute-done) | copy-start | bytes 2165764
  65.4 32.6 %collective-permute-start.2 = (bf16[705,512]{1,0:T(8,128)(2,1)S(1)}, bf16[705,512]{1,0:T(8,128)(2,1)}, u32[]{:S(2)}, u32[]{:S(2)}) collective-permute-start(bf16[705,512]{1,0:T(8,128)(2,1)S(1)} %collective-permute-done), channel_id=1, source_target_pairs={{0,1},{1,2},{2,3},{3,4},{4,5},{5,6},{6,7},{7,0},{8,9},{9,10},{10,1... | collective-permute-start | bytes 2165768 | tf_op jit(solution)/shard_map/ppermute | solution.py:47
  66.7 34.0 %all-to-all-start = ((s32[32,1,2]{2,1,0:T(1,128)}), s32[32,1,2]{2,1,0:T(1,128)S(1)}, u32[]{:S(2)}, u32[]{:S(2)}) async-start(s32[32,1,2]{2,1,0:T(1,128)} %bitcast.11), calls=%async_computation | async-start | bytes 32768 | tf_op jit(solution)/shard_map/all_to_all | solution.py:120
  95.0 6.1 %copy-start.6 = (bf16[705,512]{1,0:T(8,128)(2,1)}, bf16[705,512]{1,0:T(8,128)(2,1)S(1)}, u32[]{:S(2)}) copy-start(bf16[705,512]{1,0:T(8,128)(2,1)S(1)} %collective-permute-done.1) | copy-start | bytes 2165764
  95.0 18.5 %collective-permute-start.3 = (bf16[705,512]{1,0:T(8,128)(2,1)S(1)}, bf16[705,512]{1,0:T(8,128)(2,1)}, u32[]{:S(2)}, u32[]{:S(2)}) collective-permute-start(bf16[705,512]{1,0:T(8,128)(2,1)S(1)} %collective-permute-done.1), channel_id=1, source_target_pairs={{0,7},{1,0},{2,1},{3,2},{4,3},{5,4},{6,5},{7,6},{8,15},{9,8},{10,9... | collective-permute-start | bytes 2165768 | tf_op jit(solution)/shard_map/ppermute | solution.py:50
  98.0 27.3 %collective-permute-start.4 = (bf16[705,512]{1,0:T(8,128)(2,1)}, bf16[705,512]{1,0:T(8,128)(2,1)}, u32[]{:S(2)}, u32[]{:S(2)}) collective-permute-start(bf16[705,512]{1,0:T(8,128)(2,1)} %collective-permute-done.2), channel_id=1, source_target_pairs={{0,1},{1,2},{2,3},{3,4},{4,5},{5,6},{6,7},{7,0},{8,9},{9,10},{10,1... | collective-permute-start | bytes 2165768 | tf_op jit(solution)/shard_map/ppermute | solution.py:47
  121.8 43.9 %collective-permute-start.5 = (bf16[705,512]{1,0:T(8,128)(2,1)}, bf16[705,512]{1,0:T(8,128)(2,1)}, u32[]{:S(2)}, u32[]{:S(2)}) collective-permute-start(bf16[705,512]{1,0:T(8,128)(2,1)} %collective-permute-done.3), channel_id=1, source_target_pairs={{0,7},{1,0},{2,1},{3,2},{4,3},{5,4},{6,5},{7,6},{8,15},{9,8},{10,9... | collective-permute-start | bytes 2165768 | tf_op jit(solution)/shard_map/ppermute | solution.py:50
  125.3 40.3 %collective-permute-start.6 = (bf16[705,512]{1,0:T(8,128)(2,1)}, bf16[705,512]{1,0:T(8,128)(2,1)S(1)}, u32[]{:S(2)}, u32[]{:S(2)}) collective-permute-start(bf16[705,512]{1,0:T(8,128)(2,1)} %collective-permute-done.4), channel_id=1, source_target_pairs={{0,1},{1,2},{2,3},{3,4},{4,5},{5,6},{6,7},{7,0},{8,9},{9,10},{10,1... | collective-permute-start | bytes 2165768 | tf_op jit(solution)/shard_map/ppermute | solution.py:47
  165.6 30.2 %all-to-all-start.1 = ((bf16[32,2,16,896]{3,2,1,0:T(8,128)(2,1)}), bf16[32,2,16,896]{3,2,1,0:T(8,128)(2,1)S(1)}, u32[]{:S(2)}, u32[]{:S(2)}) async-start(bf16[32,2,16,896]{3,2,1,0:T(8,128)(2,1)} %bitcast.13), calls=%async_computation.1 | async-start | bytes 3670016 | tf_op jit(solution)/shard_map/all_to_all | solution.py:122
  170.3 91.7 %all-gather.15.cloned.1.call-start = ((), (), s32[]{:S(2)}) async-start(), calls=%async_computation.4 | async-start | bytes 6193152 | tf_op jit(solution)/shard_map/all_gather | solution.py:128
  197.5 4.3 %copy-start.5 = (bf16[705,512]{1,0:T(8,128)(2,1)S(1)}, bf16[705,512]{1,0:T(8,128)(2,1)}, u32[]{:S(2)}) copy-start(bf16[705,512]{1,0:T(8,128)(2,1)} %copy-done.4) | copy-start | bytes 2165764
  199.8 2.6 copy-start.1
  199.8 3.1 %copy-start.7 = (bf16[705,512]{1,0:T(8,128)(2,1)S(1)}, bf16[705,512]{1,0:T(8,128)(2,1)}, u32[]{:S(2)}) copy-start(bf16[705,512]{1,0:T(8,128)(2,1)} %copy-done.6) | copy-start | bytes 2165764
  214.6 47.4 %copy-start.3 = (bf16[512,896]{1,0:T(8,128)(2,1)S(1)}, bf16[512,896]{1,0:T(8,128)(2,1)}, u32[]{:S(2)}) copy-start(bf16[512,896]{1,0:T(8,128)(2,1)} %copy.114) | copy-start | bytes 2752516
  262.0 8.7 %copy-start.9 = (bf16[24,128,896]{2,1,0:T(8,128)(2,1)S(1)}, bf16[24,128,896]{2,1,0:T(8,128)(2,1)}, u32[]{:S(2)}) copy-start(bf16[24,128,896]{2,1,0:T(8,128)(2,1)} %all-gather.15.cloned.1.call-done) | copy-start | bytes 16515076
  285.5 1.9 copy-start.2
Sparse Core Ops, SparseCore 0:
  32.0 66.9 all-gather.10
  101.6 54.1 all-gather.12
  197.5 64.4 all-gather.14

commit v5 on v1

--- a/solution.py
+++ b/solution.py
@@ -22,24 +22,28 @@
 
 
 def attend(queries, keys, values):
-    seq_rows = queries.shape[0]
-    heads_here = queries.shape[1]
+    heads_here = queries.shape[0]
+    seq_rows = queries.shape[1] + SPAN - 1
     span_count = seq_rows // SPAN
     shifted = jnp.concatenate(
-        [queries[SPAN - 1 :], jnp.zeros((SPAN - 1, heads_here, HD), jnp.bfloat16)], axis=0
+        [queries, jnp.zeros((heads_here, SPAN - 1, HD), jnp.bfloat16)], axis=1
     )
-    windows = shifted.reshape(span_count, SPAN, heads_here, HD)
-    key_blocks = keys.reshape(span_count, KN * NTOK, heads_here, HD)
-    value_blocks = values.reshape(span_count, KN * NTOK, heads_here, HD)
-    scores = jnp.einsum("cqhd,ckhd->chqk", windows, key_blocks, preferred_element_type=jnp.float32)
+    windows = shifted.reshape(heads_here, span_count, SPAN, HD)
+    key_blocks = keys.reshape(heads_here, span_count, KN * NTOK, HD)
+    value_blocks = values.reshape(heads_here, span_count, KN * NTOK, HD)
+    scores = jnp.einsum("hcqd,hckd->hcqk", windows, key_blocks, preferred_element_type=jnp.float32)
     scores = scores * (LOGIT_SCALE / math.sqrt(HD))
     expo = jnp.exp(scores)
     weights = (expo / jnp.sum(expo, axis=-1, keepdims=True)).astype(jnp.bfloat16)
-    mixed = jnp.einsum("chqk,ckhd->cqhd", weights, value_blocks, preferred_element_type=jnp.float32)
+    mixed = jnp.einsum("hcqk,hckd->cqhd", weights, value_blocks, preferred_element_type=jnp.float32)
     mixed = mixed.astype(jnp.bfloat16).reshape(seq_rows, heads_here * HD)
     leading = jnp.zeros((SPAN - 1, heads_here * HD), jnp.bfloat16)
     return jnp.concatenate([leading, mixed[: seq_rows - SPAN + 1]], axis=0)
 
+
+def head_norm_major(projected):
+    scaled = projected * lax.rsqrt(jnp.mean(projected * projected, axis=-1, keepdims=True) + EPSILON)
+    return scaled.astype(jnp.bfloat16)
 
 def shards(hidden_states, neighbour_ids, database, w_up, w_down, w_query, w_key, w_value):
     dp_count = lax.axis_size("dp")
@@ -83,18 +87,30 @@
     )
     mine = replies.reshape(dp_count * capacity, rows_here, enc_width)[slots]
     encoded = lax.all_gather(mine, "tensor", axis=1, tiled=True)
+    heads_here = w_query.shape[1] // HD
     projected = jnp.dot(
-        lax.all_gather(hidden_states, "tensor", axis=1, tiled=True),
+        lax.all_gather(hidden_states[SPAN - 1 :], "tensor", axis=1, tiled=True),
         w_query,
         preferred_element_type=jnp.float32,
     )
-    queries = head_norm(projected)
+    queries = head_norm_major(projected.reshape(projected.shape[0], heads_here, HD))
+    queries = jnp.transpose(queries, (1, 0, 2))
     flat_encoded = encoded.reshape(-1, enc_width)
-    keys = head_norm(jnp.dot(flat_encoded, w_key, preferred_element_type=jnp.float32))
-    values = jnp.dot(flat_encoded, w_value, preferred_element_type=jnp.float32).astype(jnp.bfloat16)
-    values = values.reshape(flat_encoded.shape[0], -1, HD)
+    keys = head_norm_major(
+        jnp.einsum(
+            "ke,ehd->hkd",
+            flat_encoded,
+            w_key.reshape(enc_width, heads_here, HD),
+            preferred_element_type=jnp.float32,
+        )
+    )
+    values = jnp.einsum(
+        "ke,ehd->hkd",
+        flat_encoded,
+        w_value.reshape(enc_width, heads_here, HD),
+        preferred_element_type=jnp.float32,
+    ).astype(jnp.bfloat16)
     return attend(queries, keys, values)
-
 
 def solution(mesh):
     in_specs = (

time: 248 us -> 234 us (0.944)
  waiting for transfers between devices: 155 us -> 149 us
  local copies, waits for them, and re-layouts: 16.5 us -> 10.6 us
    another operation x1 -> x0, local copies, waits for them, and re-layouts: 5.54 us -> none  [attend(): value_blocks = values.reshape(span_count, KN * NTOK, heads_here, HD)]
    all_gather x1, waiting for transfers between devices: 35.6 us -> 32.8 us  [shards(): lax.all_gather(hidden_states[SPAN - 1:], 'tensor', axis=1, tiled=True)]
  transfers between devices with their start and end apart: 5 -> 5, of which waited for: 5 -> 5; matrix products, arithmetic and copies ran while one was open for 10% -> 11% of each run, Pallas kernels for 0% -> 0%
where the time goes in v5:
time: 234 us
  waiting for transfers between devices  149 us (64%)
  matrix products  29.4 us (13%)
  starting transfers between devices  16.3 us (7%)
  other arithmetic  14.8 us (6%)
  between operations  13.3 us (6%)
  local copies, waits for them, and re-layouts  10.6 us (5%)
    all_gather x1, waiting for transfers between devices, shards(): encoded = lax.all_gather(mine, 'tensor', axis=1, tiled=True)  54.7 us
    reduce_scatter x1, waiting for transfers between devices, shards(): lax.psum_scatter(partial.astype(jnp.bfloat16), 'tensor', scatter_dimensio...  34.9 us
    all_gather x1, waiting for transfers between devices, shards(): lax.all_gather(hidden_states[SPAN - 1:], 'tensor', axis=1, tiled=True)  32.8 us
    all_to_all x1, waiting for transfers between devices, shards(): lax.all_to_all(encoded_own[asked], 'dp', split_axis=0, concat_axis=0, til...  25.4 us
    all_to_all x1, starting transfers between devices, shards(): lax.all_to_all(requests, 'dp', split_axis=0, concat_axis=0, tiled=True)  8.57 us
    dot_general x1, matrix products, shards(): jnp.dot(lax.all_gather(hidden_states[SPAN - 1:], 'tensor', axis=1, tiled=...  8.24 us
    dot_general x1, matrix products, shards(): jnp.einsum('btf,fe->bte', active, w_down, preferred_element_type=jnp.floa...  7.71 us
    all_to_all x1, starting transfers between devices, shards(): lax.all_to_all(encoded_own[asked], 'dp', split_axis=0, concat_axis=0, til...  7.59 us
  transfers between devices with their start and end apart: 5, of which 5 were waited for; matrix products, arithmetic and copies ran while one was open for 11% of the time, Pallas kernels for 0%

profile of v5, /device:TPU:1, one launch (start us, length us, event | category | flops | bytes accessed | tf_op | source)
XLA Modules:
  0.0 233.5 jit_solution(7370419812442654083)
XLA Ops:
  6.5 3.0 %multiply_reduce_fusion = f32[16,128]{1,0:T(8,128)S(1)} fusion(bf16[16,128,896]{2,1,0:T(8,128)(2,1)} %param.10), kind=kLoop, calls=%fused_computation.3 | loop fusion | flops 5502976 | bytes 3678208 | tf_op jit(solution)/shard_map/reduce_sum | solution.py:71
  9.6 7.7 %convolution_convert_fusion.1 = bf16[16,128,896]{2,1,0:T(8,128)(2,1)} fusion(f32[16,128]{1,0:T(8,128)S(1)} %add_rsqrt_fusion.2, bf16[16,128,896]{2,1,0:T(8,128)(2,1)} %param.10, bf16[448,896]{1,0:T(8,128)(2,1)S(1)} %copy-done.5, bf16[896,448]{0,1:T(8,128)(2,1)S(1)} %copy-done.6), kind=kOutput, calls=%fused_computation.26 | convolution fusion | flops 3303931904 | bytes 8953856 | tf_op jit(solution)/shard_map/btf,fe->bte/dot_general | solution.py:75
  17.3 1.1 copy-done.1
  18.4 1.0 slice.6
  19.5 0.1 copy.62
  19.7 0.3 fusion.32
  20.1 0.7 all_to_all.11
  20.8 8.6 %all-to-all-start = ((s32[32,1,2]{2,1,0:T(1,128)}), s32[32,1,2]{2,1,0:T(1,128)S(1)}, u32[]{:S(2)}, u32[]{:S(2)}) async-start(s32[32,1,2]{2,1,0:T(1,128)} %bitcast.2), calls=%async_computation.1 | async-start | bytes 32768 | tf_op jit(solution)/shard_map/all_to_all | solution.py:84
  29.4 5.8 %convert_element_type.41 = f32[16,128,896]{2,1,0:T(8,128)} convert(bf16[16,128,896]{2,1,0:T(8,128)(2,1)} %param.10) | non-fusion elementwise | flops 1835008 | bytes 11010048 | tf_op jit(solution)/shard_map/convert_element_type | solution.py:69
  35.2 1.2 all-to-all-done
  36.5 0.1 reshape.253
  36.6 34.9 %reduce-scatter.2.cloned.1.call-done = bf16[16,16,896]{2,1,0:T(8,128)(2,1)} async-done(((bf16[16,128,896]{2,1,0:T(8,128)(2,1)}), bf16[16,16,896]{2,1,0:T(8,128)(2,1)}) %reduce-scatter.2.cloned.1.call-update) | async-done | bytes 458768 | tf_op jit(solution)/shard_map/reduce_scatter | solution.py:77
  71.6 1.4 add_convert_fusion
  73.0 2.0 gather_fusion
  75.0 7.6 %all-to-all-start.1 = ((bf16[32,2,16,896]{3,2,1,0:T(8,128)(2,1)}), bf16[32,2,16,896]{3,2,1,0:T(8,128)(2,1)S(1)}, u32[]{:S(2)}, u32[]{:S(2)}) async-start(bf16[32,2,16,896]{3,2,1,0:T(8,128)(2,1)} %bitcast.4), calls=%async_computation.2 | async-start | bytes 3670016 | tf_op jit(solution)/shard_map/all_to_all | solution.py:85
  82.7 25.4 %all-to-all-done.1 = bf16[32,2,16,896]{3,2,1,0:T(8,128)(2,1)S(1)} async-done(((bf16[32,2,16,896]{3,2,1,0:T(8,128)(2,1)}), bf16[32,2,16,896]{3,2,1,0:T(8,128)(2,1)S(1)}, u32[]{:S(2)}, u32[]{:S(2)}) %all-to-all-start.1) | async-done | bytes 1835040 | tf_op jit(solution)/shard_map/all_to_all | solution.py:85
  108.1 1.5 gather_fusion.1
  109.7 32.8 %all-gather.4.cloned.1.call-done = bf16[705,4096]{1,0:T(8,128)(2,1)} async-done(((bf16[705,512]{1,0:T(8,128)(2,1)}), bf16[705,4096]{1,0:T(8,128)(2,1)}) %all-gather.4.cloned.1.call-update) | async-done | bytes 5775376 | tf_op jit(solution)/shard_map/all_gather | solution.py:92
  142.5 8.2 %fusion.48 = f32[705,512]{1,0:T(8,128)} fusion(bf16[705,4096]{1,0:T(8,128)(2,1)} %all-gather.4.cloned.1.call-done, bf16[4096,512]{1,0:T(8,128)(2,1)} %param.13), kind=kOutput, calls=%fused_computation.76 | convolution fusion | flops 2956984320 | bytes 11413504 | tf_op jit(solution)/shard_map/dot_general | solution.py:91
  150.7 1.7 reshape.246
  152.5 0.8 multiply_reduce_fusion.1
  153.3 1.7 fusion.41
  155.0 0.1 copy.75
  155.2 54.7 %all-gather.6.cloned.1.call-done = bf16[24,128,896]{2,1,0:T(8,128)(2,1)} async-done(((bf16[24,16,896]{2,1,0:T(8,128)(2,1)}), bf16[24,128,896]{2,1,0:T(8,128)(2,1)}) %all-gather.6.cloned.1.call-update) | async-done | bytes 5505040 | tf_op jit(solution)/shard_map/all_gather | solution.py:89
  209.9 6.3 %convolution_convert_fusion = bf16[3072,4,128]{2,0,1:T(8,128)(2,1)S(1)} fusion(bf16[3072,896,1]{1,0,2:T(8,128)(2,1)} %bitcast.71, bf16[896,512]{1,0:T(8,128)(2,1)S(1)} %copy-done.4), kind=kOutput, calls=%fused_computation.9 | convolution fusion | flops 2820145152 | bytes 9568256 | tf_op jit(solution)/shard_map/ke,ehd->hkd/dot_general | solution.py:107
  216.3 4.4 %fusion = (f32[4,3072]{1,0:T(4,128)S(1)}, f32[3072,4,128]{2,0,1:T(8,128)S(1)}) fusion(bf16[3072,896,1]{1,0,2:T(8,128)(2,1)S(1)} %bitcast.72, bf16[896,512]{1,0:T(8,128)(2,1)S(1)} %copy-done), kind=kOutput, calls=%fused_computation.6 | convolution fusion | flops 2821705728 | bytes 12763136 | tf_op jit(solution)/shard_map/ke,ehd->hkd/dot_general | solution.py:100
  220.7 1.9 fusion.1
  222.7 1.3 fusion.15
  224.0 1.1 fusion.27
  225.1 0.6 copy.74
  225.8 0.1 copy.103
  226.0 1.1 concatenate.7
  (35 shorter events, 0.8 us)
Async XLA Ops:
  6.5 209.7 %copy-start = (bf16[896,512]{1,0:T(8,128)(2,1)S(1)}, bf16[896,512]{1,0:T(8,128)(2,1)}, u32[]{:S(2)}) copy-start(bf16[896,512]{1,0:T(8,128)(2,1)} %param.14) | copy-start | bytes 2752516
  6.5 3.0 %copy-start.5 = (bf16[448,896]{1,0:T(8,128)(2,1)S(1)}, bf16[448,896]{1,0:T(8,128)(2,1)}, u32[]{:S(2)}) copy-start(bf16[448,896]{1,0:T(8,128)(2,1)} %param.12) | copy-start | bytes 2408452
  6.5 3.0 %copy-start.6 = (bf16[896,448]{0,1:T(8,128)(2,1)S(1)}, bf16[896,448]{0,1:T(8,128)(2,1)}, u32[]{:S(2)}) copy-start(bf16[896,448]{0,1:T(8,128)(2,1)} %param.11) | copy-start | bytes 2408452
  6.5 65.0 %reduce-scatter.2.cloned.1.call-start = ((), (), s32[]{:S(2)}) async-start(), calls=%async_computation.3 | async-start | bytes 4128768 | tf_op jit(solution)/shard_map/reduce_scatter | solution.py:77
  17.3 1.1 copy-start.1
  17.3 2.2 copy-start.2
  17.3 125.2 %all-gather.4.cloned.1.call-start = ((), (), s32[]{:S(2)}) async-start(), calls=%async_computation.4 | async-start | bytes 6561792 | tf_op jit(solution)/shard_map/all_gather | solution.py:92
  20.8 15.5 %all-to-all-start = ((s32[32,1,2]{2,1,0:T(1,128)}), s32[32,1,2]{2,1,0:T(1,128)S(1)}, u32[]{:S(2)}, u32[]{:S(2)}) async-start(s32[32,1,2]{2,1,0:T(1,128)} %bitcast.2), calls=%async_computation.1 | async-start | bytes 32768 | tf_op jit(solution)/shard_map/all_to_all | solution.py:84
  75.0 33.1 %all-to-all-start.1 = ((bf16[32,2,16,896]{3,2,1,0:T(8,128)(2,1)}), bf16[32,2,16,896]{3,2,1,0:T(8,128)(2,1)S(1)}, u32[]{:S(2)}, u32[]{:S(2)}) async-start(bf16[32,2,16,896]{3,2,1,0:T(8,128)(2,1)} %bitcast.4), calls=%async_computation.2 | async-start | bytes 3670016 | tf_op jit(solution)/shard_map/all_to_all | solution.py:85
  82.6 127.3 %all-gather.6.cloned.1.call-start = ((), (), s32[]{:S(2)}) async-start(), calls=%async_computation.5 | async-start | bytes 6193152 | tf_op jit(solution)/shard_map/all_gather | solution.py:89
  152.4 57.5 %copy-start.4 = (bf16[896,512]{1,0:T(8,128)(2,1)S(1)}, bf16[896,512]{1,0:T(8,128)(2,1)}, u32[]{:S(2)}) copy-start(bf16[896,512]{1,0:T(8,128)(2,1)} %param.15) | copy-start | bytes 2752516
  209.9 6.4 %copy-start.3 = (bf16[24,128,896]{2,1,0:T(8,128)(2,1)S(1)}, bf16[24,128,896]{2,1,0:T(8,128)(2,1)}, u32[]{:S(2)}) copy-start(bf16[24,128,896]{2,1,0:T(8,128)(2,1)} %all-gather.6.cloned.1.call-done) | copy-start | bytes 16515076
Sparse Core Ops, SparseCore 0:
  17.4 54.1 reduce-scatter.1
  73.4 69.0 all-gather.3
  144.3 65.6 all-gather.5

commit v6 on v5

--- a/solution.py
+++ b/solution.py
@@ -45,6 +45,36 @@
     scaled = projected * lax.rsqrt(jnp.mean(projected * projected, axis=-1, keepdims=True) + EPSILON)
     return scaled.astype(jnp.bfloat16)
 
+def ring_hops(states, n):
+    to_right = [(i, (i + 1) % n) for i in range(n)]
+    to_left = [(i, (i - 1) % n) for i in range(n)]
+    going_right = states
+    going_left = states
+    right_hops = n // 2
+    left_hops = n - 1 - right_hops
+    steps = []
+    for hop in range(1, right_hops + 1):
+        step = {}
+        going_right = lax.ppermute(going_right, "tensor", to_right)
+        step[(n - hop) % n] = going_right
+        if hop <= left_hops:
+            going_left = lax.ppermute(going_left, "tensor", to_left)
+            step[hop] = going_left
+        steps.append(step)
+    return steps
+
+
+def ring_query(got, w_query, n):
+    width = got[0].shape[1]
+    me = lax.axis_index("tensor")
+    total = None
+    for offset in range(n):
+        rows = lax.dynamic_slice_in_dim(w_query, ((me + offset) % n) * width, width, 0)
+        term = jnp.dot(got[offset], rows, preferred_element_type=jnp.float32)
+        total = term if total is None else total + term
+    return total
+
+
 def shards(hidden_states, neighbour_ids, database, w_up, w_down, w_query, w_key, w_value):
     dp_count = lax.axis_size("dp")
     tensor_count = lax.axis_size("tensor")
@@ -74,24 +104,33 @@
     active = jax.nn.gelu(inner).astype(jnp.bfloat16)
     partial = jnp.einsum("btf,fe->bte", active, w_down, preferred_element_type=jnp.float32)
     rows_here = block_tokens // tensor_count
+    states = hidden_states[SPAN - 1 :]
+    head_rows = SPAN
+    head_got = {0: states[:head_rows]}
+    for step in ring_hops(states[:head_rows], tensor_count):
+        head_got.update(step)
     summed = lax.psum_scatter(
         partial.astype(jnp.bfloat16), "tensor", scatter_dimension=1, tiled=True
-    ).astype(jnp.float32)
+    )
+    states_rest, summed = lax.optimization_barrier((states[head_rows:], summed))
+    summed = summed.astype(jnp.float32)
     raw_own = lax.dynamic_slice_in_dim(
         raw_float, lax.axis_index("tensor") * rows_here, rows_here, 1
     )
     encoded_own = (raw_own + summed).astype(jnp.bfloat16)
     asked = lax.all_to_all(requests, "dp", split_axis=0, concat_axis=0, tiled=True)
-    replies = lax.all_to_all(
-        encoded_own[asked], "dp", split_axis=0, concat_axis=0, tiled=True
-    )
+    served, head_got = lax.optimization_barrier((encoded_own[asked], head_got))
+    replies = lax.all_to_all(served, "dp", split_axis=0, concat_axis=0, tiled=True)
     mine = replies.reshape(dp_count * capacity, rows_here, enc_width)[slots]
     encoded = lax.all_gather(mine, "tensor", axis=1, tiled=True)
     heads_here = w_query.shape[1] // HD
-    projected = jnp.dot(
-        lax.all_gather(hidden_states[SPAN - 1 :], "tensor", axis=1, tiled=True),
-        w_query,
-        preferred_element_type=jnp.float32,
+    states_rest = lax.all_gather(states_rest, "tensor", axis=1, tiled=True)
+    projected = jnp.concatenate(
+        [
+            ring_query(head_got, w_query, tensor_count),
+            jnp.dot(states_rest, w_query, preferred_element_type=jnp.float32),
+        ],
+        axis=0,
     )
     queries = head_norm_major(projected.reshape(projected.shape[0], heads_here, HD))
     queries = jnp.transpose(queries, (1, 0, 2))

time: 234 us -> 233 us (level)
  waiting for transfers between devices: 149 us -> 130 us
  starting transfers between devices: 16.3 us -> 25.3 us
  matrix products: 29.4 us -> 37.2 us
    all_gather x1, waiting for transfers between devices: 32.8 us -> 0.02 us  [shards(): states_rest = lax.all_gather(states_rest, 'tensor', axis=1, tiled=True)]
    reduce_scatter x1, waiting for transfers between devices: 34.9 us -> 52.1 us  [shards(): lax.psum_scatter(partial.astype(jnp.bfloat16), 'tensor', scatter_dimensio...]
    all_gather x1, waiting for transfers between devices: 54.7 us -> 41.3 us  [shards(): encoded = lax.all_gather(mine, 'tensor', axis=1, tiled=True)]
    ppermute x0 -> x7, waiting for transfers between devices: none -> 10.2 us  [the longest x4 10.2 us: ring_hops(): going_right = lax.ppermute(going_right, 'tensor', to_right)]
    ppermute x0 -> x7, starting transfers between devices: none -> 8.35 us  [the longest x3 8.24 us: ring_hops(): going_left = lax.ppermute(going_left, 'tensor', to_left)]
    dot_general x1 -> x9, matrix products: 8.24 us -> 16.2 us  [the longest x8 10 us: ring_query(): term = jnp.dot(got[offset], rows, preferred_element_type=jnp.float32)]
    dot_general x1, matrix products: 6.34 us -> 3.64 us  [shards(): jnp.einsum('ke,ehd->hkd', flat_encoded, w_value.reshape(enc_width, heads_...]
    dot_general x1, matrix products: 4.4 us -> 6.86 us  [shards(): jnp.einsum('ke,ehd->hkd', flat_encoded, w_key.reshape(enc_width, heads_he...]
  transfers between devices with their start and end apart: 5 -> 12, of which waited for: 5 -> 7; matrix products, arithmetic and copies ran while one was open for 11% -> 15% of each run, Pallas kernels for 0% -> 0%
where the time goes in v6:
time: 233 us
  waiting for transfers between devices  130 us (56%)
  matrix products  37.2 us (16%)
  starting transfers between devices  25.3 us (11%)
  other arithmetic  16 us (7%)
  between operations  13.6 us (6%)
  local copies, waits for them, and re-layouts  10.7 us (5%)
    reduce_scatter x1, waiting for transfers between devices, shards(): lax.psum_scatter(partial.astype(jnp.bfloat16), 'tensor', scatter_dimensio...  52.1 us
    all_gather x1, waiting for transfers between devices, shards(): encoded = lax.all_gather(mine, 'tensor', axis=1, tiled=True)  41.3 us
    all_to_all x1, waiting for transfers between devices, shards(): lax.all_to_all(served, 'dp', split_axis=0, concat_axis=0, tiled=True)  25.2 us
    ppermute x4, waiting for transfers between devices, ring_hops(): going_right = lax.ppermute(going_right, 'tensor', to_right)  10.2 us
    dot_general x8, matrix products, ring_query(): term = jnp.dot(got[offset], rows, preferred_element_type=jnp.float32)  10 us
    all_to_all x1, starting transfers between devices, shards(): lax.all_to_all(served, 'dp', split_axis=0, concat_axis=0, tiled=True)  8.5 us
    ppermute x3, starting transfers between devices, ring_hops(): going_left = lax.ppermute(going_left, 'tensor', to_left)  8.24 us
    all_to_all x1, starting transfers between devices, shards(): lax.all_to_all(requests, 'dp', split_axis=0, concat_axis=0, tiled=True)  8.15 us
  transfers between devices with their start and end apart: 12, of which 7 were waited for; matrix products, arithmetic and copies ran while one was open for 15% of the time, Pallas kernels for 0%

profile of v6, /device:TPU:1, one launch (start us, length us, event | category | flops | bytes accessed | tf_op | source)
XLA Modules:
  0.0 232.6 jit_solution(15547182018745896545)
XLA Ops:
  6.5 3.0 %multiply_reduce_fusion = f32[16,128]{1,0:T(8,128)S(1)} fusion(bf16[16,128,896]{2,1,0:T(8,128)(2,1)} %param.10), kind=kLoop, calls=%fused_computation.3 | loop fusion | flops 5502976 | bytes 3678208 | tf_op jit(solution)/shard_map/reduce_sum | solution.py:101
  9.6 7.7 %convolution_convert_fusion.1 = bf16[16,128,896]{2,1,0:T(8,128)(2,1)} fusion(f32[16,128]{1,0:T(8,128)S(1)} %add_rsqrt_fusion.2, bf16[16,128,896]{2,1,0:T(8,128)(2,1)} %param.10, bf16[448,896]{1,0:T(8,128)(2,1)S(1)} %copy-done.7, bf16[896,448]{0,1:T(8,128)(2,1)S(1)} %copy-done.8), kind=kOutput, calls=%fused_computation.26 | convolution fusion | flops 3303931904 | bytes 8953856 | tf_op jit(solution)/shard_map/btf,fe->bte/dot_general | solution.py:105
  19.5 52.1 %reduce-scatter.2.cloned.1.call-done = bf16[16,16,896]{2,1,0:T(8,128)(2,1)} async-done(((bf16[16,128,896]{2,1,0:T(8,128)(2,1)}), bf16[16,16,896]{2,1,0:T(8,128)(2,1)}) %reduce-scatter.2.cloned.1.call-update) | async-done | bytes 458768 | tf_op jit(solution)/shard_map/reduce_scatter | solution.py:112
  71.7 2.7 %collective-permute-start = (bf16[64,512]{1,0:T(8,128)(2,1)S(1)}, bf16[64,512]{1,0:T(8,128)(2,1)S(1)}, u32[]{:S(2)}, u32[]{:S(2)}) collective-permute-start(bf16[64,512]{1,0:T(8,128)(2,1)S(1)} %slice.14), channel_id=1, source_target_pairs={{0,7},{1,0},{2,1},{3,2},{4,3},{5,4},{6,5},{7,6},{8,15},{9,8},{10,9... | collective-permute-start | bytes 196616 | tf_op jit(solution)/shard_map/ppermute | solution.py:61
  75.7 8.2 %all-to-all-start = ((s32[32,1,2]{2,1,0:T(1,128)}), s32[32,1,2]{2,1,0:T(1,128)S(1)}, u32[]{:S(2)}, u32[]{:S(2)}) async-start(s32[32,1,2]{2,1,0:T(1,128)} %bitcast.2), calls=%async_computation.1 | async-start | bytes 32768 | tf_op jit(solution)/shard_map/all_to_all | solution.py:121
  83.9 5.9 %convert_element_type.41 = f32[16,128,896]{2,1,0:T(8,128)} convert(bf16[16,128,896]{2,1,0:T(8,128)(2,1)} %param.10) | non-fusion elementwise | flops 1835008 | bytes 11010048 | tf_op jit(solution)/shard_map/convert_element_type | solution.py:99
  91.1 2.7 %collective-permute-start.1 = (bf16[64,512]{1,0:T(8,128)(2,1)S(1)}, bf16[64,512]{1,0:T(8,128)(2,1)S(1)}, u32[]{:S(2)}, u32[]{:S(2)}) collective-permute-start(bf16[64,512]{1,0:T(8,128)(2,1)S(1)} %collective-permute-done), channel_id=1, source_target_pairs={{0,7},{1,0},{2,1},{3,2},{4,3},{5,4},{6,5},{7,6},{8,15},{9,8},{10,9... | collective-permute-start | bytes 196616 | tf_op jit(solution)/shard_map/ppermute | solution.py:61
  93.8 3.7 %collective-permute-done.4 = bf16[64,512]{1,0:T(8,128)(2,1)S(1)} collective-permute-done((bf16[64,512]{1,0:T(8,128)(2,1)S(1)}, bf16[64,512]{1,0:T(8,128)(2,1)S(1)}, u32[]{:S(2)}, u32[]{:S(2)}) %collective-permute-start.4) | collective-permute-done | bytes 65568 | tf_op jit(solution)/shard_map/ppermute | solution.py:58
  97.5 2.8 %collective-permute-start.2 = (bf16[64,512]{1,0:T(8,128)(2,1)S(1)}, bf16[64,512]{1,0:T(8,128)(2,1)S(1)}, u32[]{:S(2)}, u32[]{:S(2)}) collective-permute-start(bf16[64,512]{1,0:T(8,128)(2,1)S(1)} %collective-permute-done.1), channel_id=1, source_target_pairs={{0,7},{1,0},{2,1},{3,2},{4,3},{5,4},{6,5},{7,6},{8,15},{9,8},{10,9... | collective-permute-start | bytes 196616 | tf_op jit(solution)/shard_map/ppermute | solution.py:61
  100.3 3.6 %collective-permute-done.5 = bf16[64,512]{1,0:T(8,128)(2,1)S(1)} collective-permute-done((bf16[64,512]{1,0:T(8,128)(2,1)S(1)}, bf16[64,512]{1,0:T(8,128)(2,1)S(1)}, u32[]{:S(2)}, u32[]{:S(2)}) %collective-permute-start.5) | collective-permute-done | bytes 65568 | tf_op jit(solution)/shard_map/ppermute | solution.py:58
  103.9 1.3 add_convert_fusion
  105.2 2.0 gather_fusion
  107.2 3.0 %collective-permute-done.6 = bf16[64,512]{1,0:T(8,128)(2,1)S(1)} collective-permute-done((bf16[64,512]{1,0:T(8,128)(2,1)S(1)}, bf16[64,512]{1,0:T(8,128)(2,1)S(1)}, u32[]{:S(2)}, u32[]{:S(2)}) %collective-permute-start.6) | collective-permute-done | bytes 65568 | tf_op jit(solution)/shard_map/ppermute | solution.py:58
  110.1 8.5 %all-to-all-start.1 = ((bf16[32,2,16,896]{3,2,1,0:T(8,128)(2,1)}), bf16[32,2,16,896]{3,2,1,0:T(8,128)(2,1)S(1)}, u32[]{:S(2)}, u32[]{:S(2)}) async-start(bf16[32,2,16,896]{3,2,1,0:T(8,128)(2,1)} %bitcast.4), calls=%async_computation.2 | async-start | bytes 3670016 | tf_op jit(solution)/shard_map/all_to_all | solution.py:123
  119.0 25.2 %all-to-all-done.1 = bf16[32,2,16,896]{3,2,1,0:T(8,128)(2,1)S(1)} async-done(((bf16[32,2,16,896]{3,2,1,0:T(8,128)(2,1)}), bf16[32,2,16,896]{3,2,1,0:T(8,128)(2,1)S(1)}, u32[]{:S(2)}, u32[]{:S(2)}) %all-to-all-start.1) | async-done | bytes 1835040 | tf_op jit(solution)/shard_map/all_to_all | solution.py:123
  144.2 1.5 gather_fusion.1
  145.8 1.2 fusion.48
  147.1 1.2 fusion.50
  148.3 1.2 fusion.52
  149.6 1.2 fusion.54
  150.8 1.2 fusion.56
  152.1 1.2 fusion.58
  153.3 1.3 fusion.60
  154.6 1.3 fusion.37
  155.9 6.2 %fusion.77 = f32[641,512]{1,0:T(8,128)S(1)} fusion(bf16[641,4096]{1,0:T(8,128)(2,1)} %all-gather.4.cloned.1.call-done, bf16[4096,512]{1,0:T(8,128)(2,1)} %param.13), kind=kOutput, calls=%fused_computation.107 | convolution fusion | flops 2688548864 | bytes 10758144 | tf_op jit(solution)/shard_map/dot_general | solution.py:131
  163.3 1.8 reshape.246
  166.0 1.7 fusion.47
  167.8 41.3 %all-gather.6.cloned.1.call-done = bf16[24,128,896]{2,1,0:T(8,128)(2,1)} async-done(((bf16[24,16,896]{2,1,0:T(8,128)(2,1)}), bf16[24,128,896]{2,1,0:T(8,128)(2,1)}) %all-gather.6.cloned.1.call-update) | async-done | bytes 5505040 | tf_op jit(solution)/shard_map/all_gather | solution.py:125
  209.2 6.9 %fusion = (f32[4,3072]{1,0:T(4,128)S(1)}, f32[3072,4,128]{2,0,1:T(8,128)S(1)}) fusion(bf16[3072,896,1]{1,0,2:T(8,128)(2,1)} %bitcast.79, bf16[896,512]{1,0:T(8,128)(2,1)S(1)} %copy-done), kind=kOutput, calls=%fused_computation.6 | convolution fusion | flops 2821705728 | bytes 12763136 | tf_op jit(solution)/shard_map/ke,ehd->hkd/dot_general | solution.py:139
  216.1 3.6 %convolution_convert_fusion = bf16[3072,4,128]{2,0,1:T(8,128)(2,1)S(1)} fusion(bf16[3072,896,1]{1,0,2:T(8,128)(2,1)S(1)} %bitcast.80, bf16[896,512]{1,0:T(8,128)(2,1)S(1)} %copy-done.6), kind=kOutput, calls=%fused_computation.9 | convolution fusion | flops 2820145152 | bytes 9568256 | tf_op jit(solution)/shard_map/ke,ehd->hkd/dot_general | solution.py:146
  219.7 1.9 fusion.1
  221.7 1.3 fusion.15
  (63 shorter events, 10.6 us)
Async XLA Ops:
  6.5 202.6 %copy-start = (bf16[896,512]{1,0:T(8,128)(2,1)S(1)}, bf16[896,512]{1,0:T(8,128)(2,1)}, u32[]{:S(2)}) copy-start(bf16[896,512]{1,0:T(8,128)(2,1)} %param.14) | copy-start | bytes 2752516
  6.5 3.0 %copy-start.8 = (bf16[896,448]{0,1:T(8,128)(2,1)S(1)}, bf16[896,448]{0,1:T(8,128)(2,1)}, u32[]{:S(2)}) copy-start(bf16[896,448]{0,1:T(8,128)(2,1)} %param.11) | copy-start | bytes 2408452
  6.5 3.0 %copy-start.7 = (bf16[448,896]{1,0:T(8,128)(2,1)S(1)}, bf16[448,896]{1,0:T(8,128)(2,1)}, u32[]{:S(2)}) copy-start(bf16[448,896]{1,0:T(8,128)(2,1)} %param.12) | copy-start | bytes 2408452
  6.5 65.0 %reduce-scatter.2.cloned.1.call-start = ((), (), s32[]{:S(2)}) async-start(), calls=%async_computation.3 | async-start | bytes 4128768 | tf_op jit(solution)/shard_map/reduce_scatter | solution.py:112
  17.3 1.1 copy-start.2
  17.3 57.1 %copy-start.4 = (s32[12,2]{0,1:T(2,128)S(1)}, s32[12,2]{0,1:T(2,128)}, u32[]{:S(2)}) copy-start(s32[12,2]{0,1:T(2,128)} %param.9) | copy-start | bytes 292
  17.3 138.6 %all-gather.4.cloned.1.call-start = ((), (), s32[]{:S(2)}) async-start(), calls=%async_computation.4 | async-start | bytes 5971968 | tf_op jit(solution)/shard_map/all_gather | solution.py:127
  71.6 19.2 %collective-permute-start.3 = (bf16[64,512]{1,0:T(8,128)(2,1)S(1)}, bf16[64,512]{1,0:T(8,128)(2,1)S(1)}, u32[]{:S(2)}, u32[]{:S(2)}) collective-permute-start(bf16[64,512]{1,0:T(8,128)(2,1)S(1)} %slice.14), channel_id=1, source_target_pairs={{0,1},{1,2},{2,3},{3,4},{4,5},{5,6},{6,7},{7,0},{8,9},{9,10},{10,1... | collective-permute-start | bytes 196616 | tf_op jit(solution)/shard_map/ppermute | solution.py:58
  71.7 19.4 %collective-permute-start = (bf16[64,512]{1,0:T(8,128)(2,1)S(1)}, bf16[64,512]{1,0:T(8,128)(2,1)S(1)}, u32[]{:S(2)}, u32[]{:S(2)}) collective-permute-start(bf16[64,512]{1,0:T(8,128)(2,1)S(1)} %slice.14), channel_id=1, source_target_pairs={{0,7},{1,0},{2,1},{3,2},{4,3},{5,4},{6,5},{7,6},{8,15},{9,8},{10,9... | collective-permute-start | bytes 196616 | tf_op jit(solution)/shard_map/ppermute | solution.py:61
  75.7 15.1 %all-to-all-start = ((s32[32,1,2]{2,1,0:T(1,128)}), s32[32,1,2]{2,1,0:T(1,128)S(1)}, u32[]{:S(2)}, u32[]{:S(2)}) async-start(s32[32,1,2]{2,1,0:T(1,128)} %bitcast.2), calls=%async_computation.1 | async-start | bytes 32768 | tf_op jit(solution)/shard_map/all_to_all | solution.py:121
  83.9 20.0 %copy-start.3 = (bf16[16,16,896]{2,1,0:T(8,128)(2,1)S(1)}, bf16[16,16,896]{2,1,0:T(8,128)(2,1)}, u32[]{:S(2)}) copy-start(bf16[16,16,896]{2,1,0:T(8,128)(2,1)} %reduce-scatter.2.cloned.1.call-done) | copy-start | bytes 1376260
  90.8 6.6 %collective-permute-start.4 = (bf16[64,512]{1,0:T(8,128)(2,1)S(1)}, bf16[64,512]{1,0:T(8,128)(2,1)S(1)}, u32[]{:S(2)}, u32[]{:S(2)}) collective-permute-start(bf16[64,512]{1,0:T(8,128)(2,1)S(1)} %collective-permute-done.3), channel_id=1, source_target_pairs={{0,1},{1,2},{2,3},{3,4},{4,5},{5,6},{6,7},{7,0},{8,9},{9,10},{10,1... | collective-permute-start | bytes 196616 | tf_op jit(solution)/shard_map/ppermute | solution.py:58
  91.1 6.4 %collective-permute-start.1 = (bf16[64,512]{1,0:T(8,128)(2,1)S(1)}, bf16[64,512]{1,0:T(8,128)(2,1)S(1)}, u32[]{:S(2)}, u32[]{:S(2)}) collective-permute-start(bf16[64,512]{1,0:T(8,128)(2,1)S(1)} %collective-permute-done), channel_id=1, source_target_pairs={{0,7},{1,0},{2,1},{3,2},{4,3},{5,4},{6,5},{7,6},{8,15},{9,8},{10,9... | collective-permute-start | bytes 196616 | tf_op jit(solution)/shard_map/ppermute | solution.py:61
  97.5 6.4 %collective-permute-start.5 = (bf16[64,512]{1,0:T(8,128)(2,1)S(1)}, bf16[64,512]{1,0:T(8,128)(2,1)S(1)}, u32[]{:S(2)}, u32[]{:S(2)}) collective-permute-start(bf16[64,512]{1,0:T(8,128)(2,1)S(1)} %collective-permute-done.4), channel_id=1, source_target_pairs={{0,1},{1,2},{2,3},{3,4},{4,5},{5,6},{6,7},{7,0},{8,9},{9,10},{10,1... | collective-permute-start | bytes 196616 | tf_op jit(solution)/shard_map/ppermute | solution.py:58
  97.5 9.7 %collective-permute-start.2 = (bf16[64,512]{1,0:T(8,128)(2,1)S(1)}, bf16[64,512]{1,0:T(8,128)(2,1)S(1)}, u32[]{:S(2)}, u32[]{:S(2)}) collective-permute-start(bf16[64,512]{1,0:T(8,128)(2,1)S(1)} %collective-permute-done.1), channel_id=1, source_target_pairs={{0,7},{1,0},{2,1},{3,2},{4,3},{5,4},{6,5},{7,6},{8,15},{9,8},{10,9... | collective-permute-start | bytes 196616 | tf_op jit(solution)/shard_map/ppermute | solution.py:61
  103.9 6.3 %collective-permute-start.6 = (bf16[64,512]{1,0:T(8,128)(2,1)S(1)}, bf16[64,512]{1,0:T(8,128)(2,1)S(1)}, u32[]{:S(2)}, u32[]{:S(2)}) collective-permute-start(bf16[64,512]{1,0:T(8,128)(2,1)S(1)} %collective-permute-done.5), channel_id=1, source_target_pairs={{0,1},{1,2},{2,3},{3,4},{4,5},{5,6},{6,7},{7,0},{8,9},{9,10},{10,1... | collective-permute-start | bytes 196616 | tf_op jit(solution)/shard_map/ppermute | solution.py:58
  110.1 34.0 %all-to-all-start.1 = ((bf16[32,2,16,896]{3,2,1,0:T(8,128)(2,1)}), bf16[32,2,16,896]{3,2,1,0:T(8,128)(2,1)S(1)}, u32[]{:S(2)}, u32[]{:S(2)}) async-start(bf16[32,2,16,896]{3,2,1,0:T(8,128)(2,1)} %bitcast.4), calls=%async_computation.2 | async-start | bytes 3670016 | tf_op jit(solution)/shard_map/all_to_all | solution.py:123
  118.7 90.5 %all-gather.6.cloned.1.call-start = ((), (), s32[]{:S(2)}) async-start(), calls=%async_computation.5 | async-start | bytes 6193152 | tf_op jit(solution)/shard_map/all_gather | solution.py:125
  209.2 6.9 %copy-start.5 = (bf16[24,128,896]{2,1,0:T(8,128)(2,1)S(1)}, bf16[24,128,896]{2,1,0:T(8,128)(2,1)}, u32[]{:S(2)}) copy-start(bf16[24,128,896]{2,1,0:T(8,128)(2,1)} %all-gather.6.cloned.1.call-done) | copy-start | bytes 16515076
  209.2 6.9 %copy-start.6 = (bf16[896,512]{1,0:T(8,128)(2,1)S(1)}, bf16[896,512]{1,0:T(8,128)(2,1)}, u32[]{:S(2)}) copy-start(bf16[896,512]{1,0:T(8,128)(2,1)} %param.15) | copy-start | bytes 2752516
  223.0 3.0 %copy-start.1 = (bf16[896,512]{1,0:T(8,128)(2,1)S(1)}, bf16[896,512]{1,0:T(8,128)(2,1)}, u32[]{:S(2)}) copy-start(bf16[896,512]{1,0:T(8,128)(2,1)} %param.14) | copy-start | bytes 2752516
Sparse Core Ops, SparseCore 0:
  17.4 54.1 reduce-scatter.1
  73.4 68.3 all-gather.3
  145.8 63.3 all-gather.5

commit v7 on v5

--- a/solution.py
+++ b/solution.py
@@ -74,9 +74,13 @@
     active = jax.nn.gelu(inner).astype(jnp.bfloat16)
     partial = jnp.einsum("btf,fe->bte", active, w_down, preferred_element_type=jnp.float32)
     rows_here = block_tokens // tensor_count
-    summed = lax.psum_scatter(
-        partial.astype(jnp.bfloat16), "tensor", scatter_dimension=1, tiled=True
-    ).astype(jnp.float32)
+    states = hidden_states[SPAN - 1 :]
+    head_rows = 2 * SPAN
+    states_head = lax.all_gather(states[:head_rows], "tensor", axis=1, tiled=True)
+    partial, states_head = lax.optimization_barrier((partial.astype(jnp.bfloat16), states_head))
+    summed = lax.psum_scatter(partial, "tensor", scatter_dimension=1, tiled=True)
+    states_rest, summed = lax.optimization_barrier((states[head_rows:], summed))
+    summed = summed.astype(jnp.float32)
     raw_own = lax.dynamic_slice_in_dim(
         raw_float, lax.axis_index("tensor") * rows_here, rows_here, 1
     )
@@ -88,10 +92,13 @@
     mine = replies.reshape(dp_count * capacity, rows_here, enc_width)[slots]
     encoded = lax.all_gather(mine, "tensor", axis=1, tiled=True)
     heads_here = w_query.shape[1] // HD
-    projected = jnp.dot(
-        lax.all_gather(hidden_states[SPAN - 1 :], "tensor", axis=1, tiled=True),
-        w_query,
-        preferred_element_type=jnp.float32,
+    states_rest = lax.all_gather(states_rest, "tensor", axis=1, tiled=True)
+    projected = jnp.concatenate(
+        [
+            jnp.dot(states_head, w_query, preferred_element_type=jnp.float32),
+            jnp.dot(states_rest, w_query, preferred_element_type=jnp.float32),
+        ],
+        axis=0,
     )
     queries = head_norm_major(projected.reshape(projected.shape[0], heads_here, HD))
     queries = jnp.transpose(queries, (1, 0, 2))

time: 234 us -> 255 us (1.090)
  waiting for transfers between devices: 149 us -> 170 us
    reduce_scatter x1, waiting for transfers between devices: 34.9 us -> 55.3 us  [shards(): lax.psum_scatter(partial, 'tensor', scatter_dimension=1, tiled=True)]
    dot_general x1 -> x2, matrix products: 8.24 us -> 9.21 us  [the longest x1 5.94 us: shards(): jnp.dot(states_rest, w_query, preferred_element_type=jnp.float32)]
    all_gather x1 -> x2, waiting for transfers between devices: 32.8 us -> 32.4 us  [the longest x1 27.4 us: shards(): lax.all_gather(states[:head_rows], 'tensor', axis=1, tiled=True)]
  transfers between devices with their start and end apart: 5 -> 6, of which waited for: 5 -> 6; matrix products, arithmetic and copies ran while one was open for 11% -> 15% of each run, Pallas kernels for 0% -> 0%
where the time goes in v7:
time: 255 us
  waiting for transfers between devices  170 us (67%)
  matrix products  30.4 us (12%)
  other arithmetic  15.8 us (6%)
  starting transfers between devices  14.1 us (6%)
  between operations  13.4 us (5%)
  local copies, waits for them, and re-layouts  11.3 us (4%)
    all_gather x1, waiting for transfers between devices, shards(): encoded = lax.all_gather(mine, 'tensor', axis=1, tiled=True)  55.6 us
    reduce_scatter x1, waiting for transfers between devices, shards(): lax.psum_scatter(partial, 'tensor', scatter_dimension=1, tiled=True)  55.3 us
    all_gather x1, waiting for transfers between devices, shards(): lax.all_gather(states[:head_rows], 'tensor', axis=1, tiled=True)  27.4 us
    all_to_all x1, waiting for transfers between devices, shards(): lax.all_to_all(encoded_own[asked], 'dp', split_axis=0, concat_axis=0, til...  25.4 us
    dot_general x1, matrix products, shards(): jnp.einsum('btf,fe->bte', active, w_down, preferred_element_type=jnp.floa...  7.69 us
    all_to_all x1, starting transfers between devices, shards(): lax.all_to_all(requests, 'dp', split_axis=0, concat_axis=0, tiled=True)  7.6 us
    all_to_all x1, starting transfers between devices, shards(): lax.all_to_all(encoded_own[asked], 'dp', split_axis=0, concat_axis=0, til...  6.35 us
    dot_general x1, matrix products, shards(): jnp.einsum('ke,ehd->hkd', flat_encoded, w_value.reshape(enc_width, heads_...  6.34 us
  transfers between devices with their start and end apart: 6, of which 6 were waited for; matrix products, arithmetic and copies ran while one was open for 15% of the time, Pallas kernels for 0%

profile of v7, /device:TPU:1, one launch (start us, length us, event | category | flops | bytes accessed | tf_op | source)
XLA Modules:
  0.0 254.7 jit_solution(8146495737433301493)
XLA Ops:
  6.5 1.7 slice.13
  8.4 2.8 %multiply_reduce_fusion = f32[16,128]{1,0:T(8,128)S(1)} fusion(bf16[16,128,896]{2,1,0:T(8,128)(2,1)} %param.10), kind=kLoop, calls=%fused_computation.3 | loop fusion | flops 5502976 | bytes 3678208 | tf_op jit(solution)/shard_map/reduce_sum | solution.py:71
  11.2 7.7 %convolution_convert_fusion.1 = bf16[16,128,896]{2,1,0:T(8,128)(2,1)} fusion(f32[16,128]{1,0:T(8,128)S(1)} %add_rsqrt_fusion.2, bf16[16,128,896]{2,1,0:T(8,128)(2,1)} %param.10, bf16[448,896]{1,0:T(8,128)(2,1)S(1)} %copy-done.6, bf16[896,448]{0,1:T(8,128)(2,1)S(1)} %copy-done.7), kind=kOutput, calls=%fused_computation.26 | convolution fusion | flops 3303931904 | bytes 8953856 | tf_op jit(solution)/shard_map/btf,fe->bte/dot_general | solution.py:75
  18.9 27.4 %all-gather.5.cloned.1.call-done = bf16[128,4096]{1,0:T(8,128)(2,1)} async-done(((bf16[128,512]{1,0:T(8,128)(2,1)}), bf16[128,4096]{1,0:T(8,128)(2,1)}) %all-gather.5.cloned.1.call-update) | async-done | bytes 1048592 | tf_op jit(solution)/shard_map/all_gather | solution.py:79
  46.4 1.0 slice.12
  47.4 55.3 %reduce-scatter.2.cloned.1.call-done = bf16[16,16,896]{2,1,0:T(8,128)(2,1)} async-done(((bf16[16,128,896]{2,1,0:T(8,128)(2,1)}), bf16[16,16,896]{2,1,0:T(8,128)(2,1)}) %reduce-scatter.2.cloned.1.call-update) | async-done | bytes 458768 | tf_op jit(solution)/shard_map/reduce_scatter | solution.py:81
  102.9 0.3 fusion.32
  103.3 0.7 all_to_all.11
  104.0 7.6 %all-to-all-start = ((s32[32,1,2]{2,1,0:T(1,128)}), s32[32,1,2]{2,1,0:T(1,128)S(1)}, u32[]{:S(2)}, u32[]{:S(2)}) async-start(s32[32,1,2]{2,1,0:T(1,128)} %bitcast.2), calls=%async_computation.1 | async-start | bytes 32768 | tf_op jit(solution)/shard_map/all_to_all | solution.py:88
  111.7 5.8 %convert_element_type.41 = f32[16,128,896]{2,1,0:T(8,128)} convert(bf16[16,128,896]{2,1,0:T(8,128)(2,1)} %param.10) | non-fusion elementwise | flops 1835008 | bytes 11010048 | tf_op jit(solution)/shard_map/convert_element_type | solution.py:69
  117.5 1.0 all-to-all-done
  118.9 1.3 add_convert_fusion
  120.1 2.0 gather_fusion
  122.1 6.3 %all-to-all-start.1 = ((bf16[32,2,16,896]{3,2,1,0:T(8,128)(2,1)}), bf16[32,2,16,896]{3,2,1,0:T(8,128)(2,1)S(1)}, u32[]{:S(2)}, u32[]{:S(2)}) async-start(bf16[32,2,16,896]{3,2,1,0:T(8,128)(2,1)} %bitcast.4), calls=%async_computation.2 | async-start | bytes 3670016 | tf_op jit(solution)/shard_map/all_to_all | solution.py:89
  128.7 25.4 %all-to-all-done.1 = bf16[32,2,16,896]{3,2,1,0:T(8,128)(2,1)S(1)} async-done(((bf16[32,2,16,896]{3,2,1,0:T(8,128)(2,1)}), bf16[32,2,16,896]{3,2,1,0:T(8,128)(2,1)S(1)}, u32[]{:S(2)}, u32[]{:S(2)}) %all-to-all-start.1) | async-done | bytes 1835040 | tf_op jit(solution)/shard_map/all_to_all | solution.py:89
  154.0 1.5 gather_fusion.1
  155.5 3.3 %fusion.48 = f32[128,512]{1,0:T(8,128)S(1)} fusion(bf16[128,4096]{1,0:T(8,128)(2,1)} %all-gather.5.cloned.1.call-done, bf16[4096,512]{1,0:T(8,128)(2,1)} %param.13), kind=kOutput, calls=%fused_computation.77 | convolution fusion | flops 536870912 | bytes 5505024 | tf_op jit(solution)/shard_map/dot_general | solution.py:98
  158.8 5.0 %all-gather.7.cloned.1.call-done = bf16[577,4096]{1,0:T(8,128)(2,1)} async-done(((bf16[577,512]{1,0:T(8,128)(2,1)}), bf16[577,4096]{1,0:T(8,128)(2,1)}) %all-gather.7.cloned.1.call-update) | async-done | bytes 4726800 | tf_op jit(solution)/shard_map/all_gather | solution.py:95
  163.8 5.9 %fusion.49 = f32[577,512]{1,0:T(8,128)S(1)} fusion(bf16[577,4096]{1,0:T(8,128)(2,1)} %all-gather.7.cloned.1.call-done, bf16[4096,512]{1,0:T(8,128)(2,1)} %param.13), kind=kOutput, calls=%fused_computation.78 | convolution fusion | flops 2420113408 | bytes 10102784 | tf_op jit(solution)/shard_map/dot_general | solution.py:99
  169.7 1.2 pad_maximum_fusion
  171.0 1.7 reshape.246
  172.7 0.8 multiply_reduce_fusion.1
  173.6 1.7 fusion.41
  175.5 55.6 %all-gather.9.cloned.1.call-done = bf16[24,128,896]{2,1,0:T(8,128)(2,1)} async-done(((bf16[24,16,896]{2,1,0:T(8,128)(2,1)}), bf16[24,128,896]{2,1,0:T(8,128)(2,1)}) %all-gather.9.cloned.1.call-update) | async-done | bytes 5505040 | tf_op jit(solution)/shard_map/all_gather | solution.py:93
  231.1 6.3 %convolution_convert_fusion = bf16[3072,4,128]{2,0,1:T(8,128)(2,1)S(1)} fusion(bf16[3072,896,1]{1,0,2:T(8,128)(2,1)} %bitcast.73, bf16[896,512]{1,0:T(8,128)(2,1)S(1)} %copy-done.5), kind=kOutput, calls=%fused_computation.9 | convolution fusion | flops 2820145152 | bytes 9568256 | tf_op jit(solution)/shard_map/ke,ehd->hkd/dot_general | solution.py:114
  237.5 4.4 %fusion = (f32[4,3072]{1,0:T(4,128)S(1)}, f32[3072,4,128]{2,0,1:T(8,128)S(1)}) fusion(bf16[3072,896,1]{1,0,2:T(8,128)(2,1)S(1)} %bitcast.74, bf16[896,512]{1,0:T(8,128)(2,1)S(1)} %copy-done), kind=kOutput, calls=%fused_computation.6 | convolution fusion | flops 2821705728 | bytes 12763136 | tf_op jit(solution)/shard_map/ke,ehd->hkd/dot_general | solution.py:107
  241.9 1.9 fusion.1
  243.8 1.3 fusion.15
  245.1 1.1 fusion.27
  246.3 0.6 copy.74
  246.9 0.1 copy.103
  247.1 1.1 concatenate.11
  (43 shorter events, 1.2 us)
Async XLA Ops:
  6.5 230.9 %copy-start = (bf16[896,512]{1,0:T(8,128)(2,1)S(1)}, bf16[896,512]{1,0:T(8,128)(2,1)}, u32[]{:S(2)}) copy-start(bf16[896,512]{1,0:T(8,128)(2,1)} %param.14) | copy-start | bytes 2752516
  6.5 4.7 %copy-start.6 = (bf16[448,896]{1,0:T(8,128)(2,1)S(1)}, bf16[448,896]{1,0:T(8,128)(2,1)}, u32[]{:S(2)}) copy-start(bf16[448,896]{1,0:T(8,128)(2,1)} %param.12) | copy-start | bytes 2408452
  6.5 4.7 %copy-start.7 = (bf16[896,448]{0,1:T(8,128)(2,1)S(1)}, bf16[896,448]{0,1:T(8,128)(2,1)}, u32[]{:S(2)}) copy-start(bf16[896,448]{0,1:T(8,128)(2,1)} %param.11) | copy-start | bytes 2408452
  6.5 39.8 %all-gather.5.cloned.1.call-start = ((), (), s32[]{:S(2)}) async-start(), calls=%async_computation.3 | async-start | bytes 1179648 | tf_op jit(solution)/shard_map/all_gather | solution.py:79
  8.3 94.4 %reduce-scatter.2.cloned.1.call-start = ((), (), s32[]{:S(2)}) async-start(), calls=%async_computation.4 | async-start | bytes 4128768 | tf_op jit(solution)/shard_map/reduce_scatter | solution.py:81
  18.9 27.5 %copy-start.1 = (bf16[768,512]{1,0:T(8,128)(2,1)S(1)}, bf16[768,512]{1,0:T(8,128)(2,1)}, u32[]{:S(2)}) copy-start(bf16[768,512]{1,0:T(8,128)(2,1)} %param.8) | copy-start | bytes 2359300
  18.9 83.8 %copy-start.3 = (s32[12,2]{0,1:T(2,128)S(1)}, s32[12,2]{0,1:T(2,128)}, u32[]{:S(2)}) copy-start(s32[12,2]{0,1:T(2,128)} %param.9) | copy-start | bytes 292
  46.4 117.4 %all-gather.7.cloned.1.call-start = ((), (), s32[]{:S(2)}) async-start(), calls=%async_computation.5 | async-start | bytes 5382144 | tf_op jit(solution)/shard_map/all_gather | solution.py:95
  104.0 14.5 %all-to-all-start = ((s32[32,1,2]{2,1,0:T(1,128)}), s32[32,1,2]{2,1,0:T(1,128)S(1)}, u32[]{:S(2)}, u32[]{:S(2)}) async-start(s32[32,1,2]{2,1,0:T(1,128)} %bitcast.2), calls=%async_computation.1 | async-start | bytes 32768 | tf_op jit(solution)/shard_map/all_to_all | solution.py:88
  111.7 7.2 %copy-start.2 = (bf16[16,16,896]{2,1,0:T(8,128)(2,1)S(1)}, bf16[16,16,896]{2,1,0:T(8,128)(2,1)}, u32[]{:S(2)}) copy-start(bf16[16,16,896]{2,1,0:T(8,128)(2,1)} %reduce-scatter.2.cloned.1.call-done) | copy-start | bytes 1376260
  122.1 31.9 %all-to-all-start.1 = ((bf16[32,2,16,896]{3,2,1,0:T(8,128)(2,1)}), bf16[32,2,16,896]{3,2,1,0:T(8,128)(2,1)S(1)}, u32[]{:S(2)}, u32[]{:S(2)}) async-start(bf16[32,2,16,896]{3,2,1,0:T(8,128)(2,1)} %bitcast.4), calls=%async_computation.2 | async-start | bytes 3670016 | tf_op jit(solution)/shard_map/all_to_all | solution.py:89
  128.5 102.6 %all-gather.9.cloned.1.call-start = ((), (), s32[]{:S(2)}) async-start(), calls=%async_computation.6 | async-start | bytes 6193152 | tf_op jit(solution)/shard_map/all_gather | solution.py:93
  172.7 58.4 %copy-start.5 = (bf16[896,512]{1,0:T(8,128)(2,1)S(1)}, bf16[896,512]{1,0:T(8,128)(2,1)}, u32[]{:S(2)}) copy-start(bf16[896,512]{1,0:T(8,128)(2,1)} %param.15) | copy-start | bytes 2752516
  231.1 6.4 %copy-start.4 = (bf16[24,128,896]{2,1,0:T(8,128)(2,1)S(1)}, bf16[24,128,896]{2,1,0:T(8,128)(2,1)}, u32[]{:S(2)}) copy-start(bf16[24,128,896]{2,1,0:T(8,128)(2,1)} %all-gather.9.cloned.1.call-done) | copy-start | bytes 16515076
Sparse Core Ops, SparseCore 0:
  9.1 37.1 all-gather.4
  48.9 53.7 reduce-scatter.1
  104.5 59.2 all-gather.6
  165.4 65.6 all-gather.8

commit v8 on v6

--- a/solution.py
+++ b/solution.py
@@ -21,7 +21,7 @@
     return scaled.astype(jnp.bfloat16)
 
 
-def attend(queries, keys, values):
+def attend(queries, keys, key_scale, values):
     heads_here = queries.shape[0]
     seq_rows = queries.shape[1] + SPAN - 1
     span_count = seq_rows // SPAN
@@ -30,9 +30,10 @@
     )
     windows = shifted.reshape(heads_here, span_count, SPAN, HD)
     key_blocks = keys.reshape(heads_here, span_count, KN * NTOK, HD)
+    key_scale = key_scale.reshape(heads_here, span_count, 1, KN * NTOK)
     value_blocks = values.reshape(heads_here, span_count, KN * NTOK, HD)
     scores = jnp.einsum("hcqd,hckd->hcqk", windows, key_blocks, preferred_element_type=jnp.float32)
-    scores = scores * (LOGIT_SCALE / math.sqrt(HD))
+    scores = scores * key_scale * (LOGIT_SCALE / math.sqrt(HD))
     expo = jnp.exp(scores)
     weights = (expo / jnp.sum(expo, axis=-1, keepdims=True)).astype(jnp.bfloat16)
     mixed = jnp.einsum("hcqk,hckd->cqhd", weights, value_blocks, preferred_element_type=jnp.float32)
@@ -135,21 +136,21 @@
     queries = head_norm_major(projected.reshape(projected.shape[0], heads_here, HD))
     queries = jnp.transpose(queries, (1, 0, 2))
     flat_encoded = encoded.reshape(-1, enc_width)
-    keys = head_norm_major(
-        jnp.einsum(
-            "ke,ehd->hkd",
-            flat_encoded,
-            w_key.reshape(enc_width, heads_here, HD),
-            preferred_element_type=jnp.float32,
-        )
+    keys = jnp.einsum(
+        "ke,ehd->hkd",
+        flat_encoded,
+        w_key.reshape(enc_width, heads_here, HD),
+        preferred_element_type=jnp.float32,
     )
+    key_scale = lax.rsqrt(jnp.mean(keys * keys, axis=-1) + EPSILON)
+    keys = keys.astype(jnp.bfloat16)
     values = jnp.einsum(
         "ke,ehd->hkd",
         flat_encoded,
         w_value.reshape(enc_width, heads_here, HD),
         preferred_element_type=jnp.float32,
     ).astype(jnp.bfloat16)
-    return attend(queries, keys, values)
+    return attend(queries, keys, key_scale, values)
 
 def solution(mesh):
     in_specs = (

time: 233 us -> 236 us (1.013)
  matrix products: 37.2 us -> 42.1 us
    dot_general x1, matrix products: 3.64 us -> 7.56 us  [shards(): jnp.einsum('ke,ehd->hkd', flat_encoded, w_value.reshape(enc_width, heads_...]
where the time goes in v8:
time: 236 us
  waiting for transfers between devices  130 us (55%)
  matrix products  42.1 us (18%)
  starting transfers between devices  25.3 us (11%)
  other arithmetic  14.1 us (6%)
  between operations  13.6 us (6%)
  local copies, waits for them, and re-layouts  10.7 us (5%)
    reduce_scatter x1, waiting for transfers between devices, shards(): lax.psum_scatter(partial.astype(jnp.bfloat16), 'tensor', scatter_dimensio...  52.1 us
    all_gather x1, waiting for transfers between devices, shards(): encoded = lax.all_gather(mine, 'tensor', axis=1, tiled=True)  41.3 us
    all_to_all x1, waiting for transfers between devices, shards(): lax.all_to_all(served, 'dp', split_axis=0, concat_axis=0, tiled=True)  25.2 us
    ppermute x4, waiting for transfers between devices, ring_hops(): going_right = lax.ppermute(going_right, 'tensor', to_right)  10.2 us
    dot_general x8, matrix products, ring_query(): term = jnp.dot(got[offset], rows, preferred_element_type=jnp.float32)  10 us
    all_to_all x1, starting transfers between devices, shards(): lax.all_to_all(served, 'dp', split_axis=0, concat_axis=0, tiled=True)  8.5 us
    ppermute x3, starting transfers between devices, ring_hops(): going_left = lax.ppermute(going_left, 'tensor', to_left)  8.24 us
    all_to_all x1, starting transfers between devices, shards(): lax.all_to_all(requests, 'dp', split_axis=0, concat_axis=0, tiled=True)  8.15 us
  transfers between devices with their start and end apart: 12, of which 7 were waited for; matrix products, arithmetic and copies ran while one was open for 15% of the time, Pallas kernels for 0%

profile of v8, /device:TPU:1, one launch (start us, length us, event | category | flops | bytes accessed | tf_op | source)
XLA Modules:
  0.0 235.6 jit_solution(5259191929711574739)
XLA Ops:
  6.5 3.0 %multiply_reduce_fusion = f32[16,128]{1,0:T(8,128)S(1)} fusion(bf16[16,128,896]{2,1,0:T(8,128)(2,1)} %param.10), kind=kLoop, calls=%fused_computation.3 | loop fusion | flops 5502976 | bytes 3678208 | tf_op jit(solution)/shard_map/reduce_sum | solution.py:102
  9.6 7.7 %convolution_convert_fusion.1 = bf16[16,128,896]{2,1,0:T(8,128)(2,1)} fusion(f32[16,128]{1,0:T(8,128)S(1)} %add_rsqrt_fusion.1, bf16[16,128,896]{2,1,0:T(8,128)(2,1)} %param.10, bf16[448,896]{1,0:T(8,128)(2,1)S(1)} %copy-done.6, bf16[896,448]{0,1:T(8,128)(2,1)S(1)} %copy-done.7), kind=kOutput, calls=%fused_computation.23 | convolution fusion | flops 3303931904 | bytes 8953856 | tf_op jit(solution)/shard_map/btf,fe->bte/dot_general | solution.py:106
  19.5 52.1 %reduce-scatter.2.cloned.1.call-done = bf16[16,16,896]{2,1,0:T(8,128)(2,1)} async-done(((bf16[16,128,896]{2,1,0:T(8,128)(2,1)}), bf16[16,16,896]{2,1,0:T(8,128)(2,1)}) %reduce-scatter.2.cloned.1.call-update) | async-done | bytes 458768 | tf_op jit(solution)/shard_map/reduce_scatter | solution.py:113
  71.7 2.7 %collective-permute-start = (bf16[64,512]{1,0:T(8,128)(2,1)S(1)}, bf16[64,512]{1,0:T(8,128)(2,1)S(1)}, u32[]{:S(2)}, u32[]{:S(2)}) collective-permute-start(bf16[64,512]{1,0:T(8,128)(2,1)S(1)} %slice.14), channel_id=1, source_target_pairs={{0,7},{1,0},{2,1},{3,2},{4,3},{5,4},{6,5},{7,6},{8,15},{9,8},{10,9... | collective-permute-start | bytes 196616 | tf_op jit(solution)/shard_map/ppermute | solution.py:62
  75.7 8.2 %all-to-all-start = ((s32[32,1,2]{2,1,0:T(1,128)}), s32[32,1,2]{2,1,0:T(1,128)S(1)}, u32[]{:S(2)}, u32[]{:S(2)}) async-start(s32[32,1,2]{2,1,0:T(1,128)} %bitcast.2), calls=%async_computation.1 | async-start | bytes 32768 | tf_op jit(solution)/shard_map/all_to_all | solution.py:122
  83.9 5.9 %convert_element_type.44 = f32[16,128,896]{2,1,0:T(8,128)} convert(bf16[16,128,896]{2,1,0:T(8,128)(2,1)} %param.10) | non-fusion elementwise | flops 1835008 | bytes 11010048 | tf_op jit(solution)/shard_map/convert_element_type | solution.py:100
  91.1 2.7 %collective-permute-start.1 = (bf16[64,512]{1,0:T(8,128)(2,1)S(1)}, bf16[64,512]{1,0:T(8,128)(2,1)S(1)}, u32[]{:S(2)}, u32[]{:S(2)}) collective-permute-start(bf16[64,512]{1,0:T(8,128)(2,1)S(1)} %collective-permute-done), channel_id=1, source_target_pairs={{0,7},{1,0},{2,1},{3,2},{4,3},{5,4},{6,5},{7,6},{8,15},{9,8},{10,9... | collective-permute-start | bytes 196616 | tf_op jit(solution)/shard_map/ppermute | solution.py:62
  93.8 3.7 %collective-permute-done.4 = bf16[64,512]{1,0:T(8,128)(2,1)S(1)} collective-permute-done((bf16[64,512]{1,0:T(8,128)(2,1)S(1)}, bf16[64,512]{1,0:T(8,128)(2,1)S(1)}, u32[]{:S(2)}, u32[]{:S(2)}) %collective-permute-start.4) | collective-permute-done | bytes 65568 | tf_op jit(solution)/shard_map/ppermute | solution.py:59
  97.5 2.8 %collective-permute-start.2 = (bf16[64,512]{1,0:T(8,128)(2,1)S(1)}, bf16[64,512]{1,0:T(8,128)(2,1)S(1)}, u32[]{:S(2)}, u32[]{:S(2)}) collective-permute-start(bf16[64,512]{1,0:T(8,128)(2,1)S(1)} %collective-permute-done.1), channel_id=1, source_target_pairs={{0,7},{1,0},{2,1},{3,2},{4,3},{5,4},{6,5},{7,6},{8,15},{9,8},{10,9... | collective-permute-start | bytes 196616 | tf_op jit(solution)/shard_map/ppermute | solution.py:62
  100.3 3.6 %collective-permute-done.5 = bf16[64,512]{1,0:T(8,128)(2,1)S(1)} collective-permute-done((bf16[64,512]{1,0:T(8,128)(2,1)S(1)}, bf16[64,512]{1,0:T(8,128)(2,1)S(1)}, u32[]{:S(2)}, u32[]{:S(2)}) %collective-permute-start.5) | collective-permute-done | bytes 65568 | tf_op jit(solution)/shard_map/ppermute | solution.py:59
  103.9 1.3 add_convert_fusion
  105.2 2.0 gather_fusion
  107.2 3.0 %collective-permute-done.6 = bf16[64,512]{1,0:T(8,128)(2,1)S(1)} collective-permute-done((bf16[64,512]{1,0:T(8,128)(2,1)S(1)}, bf16[64,512]{1,0:T(8,128)(2,1)S(1)}, u32[]{:S(2)}, u32[]{:S(2)}) %collective-permute-start.6) | collective-permute-done | bytes 65568 | tf_op jit(solution)/shard_map/ppermute | solution.py:59
  110.1 8.5 %all-to-all-start.1 = ((bf16[32,2,16,896]{3,2,1,0:T(8,128)(2,1)}), bf16[32,2,16,896]{3,2,1,0:T(8,128)(2,1)S(1)}, u32[]{:S(2)}, u32[]{:S(2)}) async-start(bf16[32,2,16,896]{3,2,1,0:T(8,128)(2,1)} %bitcast.4), calls=%async_computation.2 | async-start | bytes 3670016 | tf_op jit(solution)/shard_map/all_to_all | solution.py:124
  119.0 25.2 %all-to-all-done.1 = bf16[32,2,16,896]{3,2,1,0:T(8,128)(2,1)S(1)} async-done(((bf16[32,2,16,896]{3,2,1,0:T(8,128)(2,1)}), bf16[32,2,16,896]{3,2,1,0:T(8,128)(2,1)S(1)}, u32[]{:S(2)}, u32[]{:S(2)}) %all-to-all-start.1) | async-done | bytes 1835040 | tf_op jit(solution)/shard_map/all_to_all | solution.py:124
  144.2 1.5 gather_fusion.1
  145.8 1.2 fusion.58
  147.1 1.2 fusion.56
  148.3 1.2 fusion.54
  149.6 1.2 fusion.52
  150.8 1.2 fusion.50
  152.1 1.2 fusion.48
  153.3 1.3 fusion.46
  154.6 1.3 fusion.35
  155.9 6.2 %fusion.75 = f32[641,512]{1,0:T(8,128)S(1)} fusion(bf16[641,4096]{1,0:T(8,128)(2,1)} %all-gather.4.cloned.1.call-done, bf16[4096,512]{1,0:T(8,128)(2,1)} %param.13), kind=kOutput, calls=%fused_computation.104 | convolution fusion | flops 2688548864 | bytes 10758144 | tf_op jit(solution)/shard_map/dot_general | solution.py:132
  162.1 1.2 pad_maximum_fusion
  163.3 1.8 reshape.251
  166.0 1.7 fusion.45
  167.9 41.3 %all-gather.6.cloned.1.call-done = bf16[24,128,896]{2,1,0:T(8,128)(2,1)} async-done(((bf16[24,16,896]{2,1,0:T(8,128)(2,1)}), bf16[24,128,896]{2,1,0:T(8,128)(2,1)}) %all-gather.6.cloned.1.call-update) | async-done | bytes 5505040 | tf_op jit(solution)/shard_map/all_gather | solution.py:126
  209.2 7.6 %convolution_convert_fusion = bf16[3072,4,128]{2,0,1:T(8,128)(2,1)} fusion(bf16[3072,896,1]{1,0,2:T(8,128)(2,1)} %bitcast.76, bf16[896,512]{1,0:T(8,128)(2,1)S(1)} %copy-done.5), kind=kOutput, calls=%fused_computation.6 | convolution fusion | flops 2820145152 | bytes 9568256 | tf_op jit(solution)/shard_map/ke,ehd->hkd/dot_general | solution.py:147
  216.7 5.9 %multiply_reduce_fusion.1 = (f32[3072,4]{0,1:T(4,128)S(1)}, bf16[3072,4,128]{2,0,1:T(8,128)(2,1)}) fusion(bf16[3072,896,1]{1,0,2:T(8,128)(2,1)S(1)} %bitcast.77, bf16[896,512]{1,0:T(8,128)(2,1)S(1)} %copy-done), kind=kOutput, calls=%fused_computation.4 | convolution fusion | flops 2823278592 | bytes 9617408 | tf_op jit(solution)/shard_map/ke,ehd->hkd/dot_general | solution.py:139
  222.7 3.3 %fusion.13 = (f32[4,12,64]{2,1,0:T(8,128)S(1)}, f32[4,12,64,256]{3,2,1,0:T(8,128)S(1)}) fusion(f32[4,12,256]{2,1,0:T(8,128)S(1)} %rsqrt.33, bf16[4,12,64,128]{3,2,1,0:T(8,128)(2,1)S(1)} %bitcast.73, bf16[4,12,256,128]{3,2,1,0:T(8,128)(2,1)} %bitcast.72), kind=kOutput, calls=%fused_computation.22 | convolution fusion | flops 203682816 | bytes 7139328 | tf_op jit(solution)/shard_map/hcqd,hckd->hcqk/dot_general | solution.py:35
  (63 shorter events, 9.4 us)
Async XLA Ops:
  6.5 210.2 %copy-start = (bf16[896,512]{1,0:T(8,128)(2,1)S(1)}, bf16[896,512]{1,0:T(8,128)(2,1)}, u32[]{:S(2)}) copy-start(bf16[896,512]{1,0:T(8,128)(2,1)} %param.14) | copy-start | bytes 2752516
  6.5 3.0 %copy-start.6 = (bf16[448,896]{1,0:T(8,128)(2,1)S(1)}, bf16[448,896]{1,0:T(8,128)(2,1)}, u32[]{:S(2)}) copy-start(bf16[448,896]{1,0:T(8,128)(2,1)} %param.12) | copy-start | bytes 2408452
  6.5 3.0 %copy-start.7 = (bf16[896,448]{0,1:T(8,128)(2,1)S(1)}, bf16[896,448]{0,1:T(8,128)(2,1)}, u32[]{:S(2)}) copy-start(bf16[896,448]{0,1:T(8,128)(2,1)} %param.11) | copy-start | bytes 2408452
  6.5 65.0 %reduce-scatter.2.cloned.1.call-start = ((), (), s32[]{:S(2)}) async-start(), calls=%async_computation.3 | async-start | bytes 4128768 | tf_op jit(solution)/shard_map/reduce_scatter | solution.py:113
  17.3 1.1 copy-start.1
  17.3 57.1 %copy-start.3 = (s32[12,2]{0,1:T(2,128)S(1)}, s32[12,2]{0,1:T(2,128)}, u32[]{:S(2)}) copy-start(s32[12,2]{0,1:T(2,128)} %param.9) | copy-start | bytes 292
  17.3 138.6 %all-gather.4.cloned.1.call-start = ((), (), s32[]{:S(2)}) async-start(), calls=%async_computation.4 | async-start | bytes 5971968 | tf_op jit(solution)/shard_map/all_gather | solution.py:128
  71.6 19.2 %collective-permute-start.3 = (bf16[64,512]{1,0:T(8,128)(2,1)S(1)}, bf16[64,512]{1,0:T(8,128)(2,1)S(1)}, u32[]{:S(2)}, u32[]{:S(2)}) collective-permute-start(bf16[64,512]{1,0:T(8,128)(2,1)S(1)} %slice.14), channel_id=1, source_target_pairs={{0,1},{1,2},{2,3},{3,4},{4,5},{5,6},{6,7},{7,0},{8,9},{9,10},{10,1... | collective-permute-start | bytes 196616 | tf_op jit(solution)/shard_map/ppermute | solution.py:59
  71.7 19.4 %collective-permute-start = (bf16[64,512]{1,0:T(8,128)(2,1)S(1)}, bf16[64,512]{1,0:T(8,128)(2,1)S(1)}, u32[]{:S(2)}, u32[]{:S(2)}) collective-permute-start(bf16[64,512]{1,0:T(8,128)(2,1)S(1)} %slice.14), channel_id=1, source_target_pairs={{0,7},{1,0},{2,1},{3,2},{4,3},{5,4},{6,5},{7,6},{8,15},{9,8},{10,9... | collective-permute-start | bytes 196616 | tf_op jit(solution)/shard_map/ppermute | solution.py:62
  75.7 15.1 %all-to-all-start = ((s32[32,1,2]{2,1,0:T(1,128)}), s32[32,1,2]{2,1,0:T(1,128)S(1)}, u32[]{:S(2)}, u32[]{:S(2)}) async-start(s32[32,1,2]{2,1,0:T(1,128)} %bitcast.2), calls=%async_computation.1 | async-start | bytes 32768 | tf_op jit(solution)/shard_map/all_to_all | solution.py:122
  83.9 20.0 %copy-start.2 = (bf16[16,16,896]{2,1,0:T(8,128)(2,1)S(1)}, bf16[16,16,896]{2,1,0:T(8,128)(2,1)}, u32[]{:S(2)}) copy-start(bf16[16,16,896]{2,1,0:T(8,128)(2,1)} %reduce-scatter.2.cloned.1.call-done) | copy-start | bytes 1376260
  90.8 6.6 %collective-permute-start.4 = (bf16[64,512]{1,0:T(8,128)(2,1)S(1)}, bf16[64,512]{1,0:T(8,128)(2,1)S(1)}, u32[]{:S(2)}, u32[]{:S(2)}) collective-permute-start(bf16[64,512]{1,0:T(8,128)(2,1)S(1)} %collective-permute-done.3), channel_id=1, source_target_pairs={{0,1},{1,2},{2,3},{3,4},{4,5},{5,6},{6,7},{7,0},{8,9},{9,10},{10,1... | collective-permute-start | bytes 196616 | tf_op jit(solution)/shard_map/ppermute | solution.py:59
  91.1 6.4 %collective-permute-start.1 = (bf16[64,512]{1,0:T(8,128)(2,1)S(1)}, bf16[64,512]{1,0:T(8,128)(2,1)S(1)}, u32[]{:S(2)}, u32[]{:S(2)}) collective-permute-start(bf16[64,512]{1,0:T(8,128)(2,1)S(1)} %collective-permute-done), channel_id=1, source_target_pairs={{0,7},{1,0},{2,1},{3,2},{4,3},{5,4},{6,5},{7,6},{8,15},{9,8},{10,9... | collective-permute-start | bytes 196616 | tf_op jit(solution)/shard_map/ppermute | solution.py:62
  97.5 6.4 %collective-permute-start.5 = (bf16[64,512]{1,0:T(8,128)(2,1)S(1)}, bf16[64,512]{1,0:T(8,128)(2,1)S(1)}, u32[]{:S(2)}, u32[]{:S(2)}) collective-permute-start(bf16[64,512]{1,0:T(8,128)(2,1)S(1)} %collective-permute-done.4), channel_id=1, source_target_pairs={{0,1},{1,2},{2,3},{3,4},{4,5},{5,6},{6,7},{7,0},{8,9},{9,10},{10,1... | collective-permute-start | bytes 196616 | tf_op jit(solution)/shard_map/ppermute | solution.py:59
  97.5 9.7 %collective-permute-start.2 = (bf16[64,512]{1,0:T(8,128)(2,1)S(1)}, bf16[64,512]{1,0:T(8,128)(2,1)S(1)}, u32[]{:S(2)}, u32[]{:S(2)}) collective-permute-start(bf16[64,512]{1,0:T(8,128)(2,1)S(1)} %collective-permute-done.1), channel_id=1, source_target_pairs={{0,7},{1,0},{2,1},{3,2},{4,3},{5,4},{6,5},{7,6},{8,15},{9,8},{10,9... | collective-permute-start | bytes 196616 | tf_op jit(solution)/shard_map/ppermute | solution.py:62
  103.9 6.3 %collective-permute-start.6 = (bf16[64,512]{1,0:T(8,128)(2,1)S(1)}, bf16[64,512]{1,0:T(8,128)(2,1)S(1)}, u32[]{:S(2)}, u32[]{:S(2)}) collective-permute-start(bf16[64,512]{1,0:T(8,128)(2,1)S(1)} %collective-permute-done.5), channel_id=1, source_target_pairs={{0,1},{1,2},{2,3},{3,4},{4,5},{5,6},{6,7},{7,0},{8,9},{9,10},{10,1... | collective-permute-start | bytes 196616 | tf_op jit(solution)/shard_map/ppermute | solution.py:59
  110.1 34.0 %all-to-all-start.1 = ((bf16[32,2,16,896]{3,2,1,0:T(8,128)(2,1)}), bf16[32,2,16,896]{3,2,1,0:T(8,128)(2,1)S(1)}, u32[]{:S(2)}, u32[]{:S(2)}) async-start(bf16[32,2,16,896]{3,2,1,0:T(8,128)(2,1)} %bitcast.4), calls=%async_computation.2 | async-start | bytes 3670016 | tf_op jit(solution)/shard_map/all_to_all | solution.py:124
  118.7 90.5 %all-gather.6.cloned.1.call-start = ((), (), s32[]{:S(2)}) async-start(), calls=%async_computation.5 | async-start | bytes 6193152 | tf_op jit(solution)/shard_map/all_gather | solution.py:126
  165.1 44.1 %copy-start.5 = (bf16[896,512]{1,0:T(8,128)(2,1)S(1)}, bf16[896,512]{1,0:T(8,128)(2,1)}, u32[]{:S(2)}) copy-start(bf16[896,512]{1,0:T(8,128)(2,1)} %param.15) | copy-start | bytes 2752516
  209.2 7.6 %copy-start.4 = (bf16[24,128,896]{2,1,0:T(8,128)(2,1)S(1)}, bf16[24,128,896]{2,1,0:T(8,128)(2,1)}, u32[]{:S(2)}) copy-start(bf16[24,128,896]{2,1,0:T(8,128)(2,1)} %all-gather.6.cloned.1.call-done) | copy-start | bytes 16515076
  222.7 3.4 %copy-start.8 = (bf16[3072,4,128]{2,0,1:T(8,128)(2,1)S(1)}, bf16[3072,4,128]{2,0,1:T(8,128)(2,1)}, u32[]{:S(2)}) copy-start(bf16[3072,4,128]{2,0,1:T(8,128)(2,1)} %convolution_convert_fusion) | copy-start | bytes 9437188
Sparse Core Ops, SparseCore 0:
  17.4 54.1 reduce-scatter.1
  73.4 68.3 all-gather.3
  145.8 63.3 all-gather.5

commit v9 on v6

--- a/solution.py
+++ b/solution.py
@@ -112,15 +112,16 @@
     summed = lax.psum_scatter(
         partial.astype(jnp.bfloat16), "tensor", scatter_dimension=1, tiled=True
     )
-    states_rest, summed = lax.optimization_barrier((states[head_rows:], summed))
+    states_rest, summed, head_got = lax.optimization_barrier((states[head_rows:], summed, head_got))
     summed = summed.astype(jnp.float32)
     raw_own = lax.dynamic_slice_in_dim(
         raw_float, lax.axis_index("tensor") * rows_here, rows_here, 1
     )
     encoded_own = (raw_own + summed).astype(jnp.bfloat16)
     asked = lax.all_to_all(requests, "dp", split_axis=0, concat_axis=0, tiled=True)
-    served, head_got = lax.optimization_barrier((encoded_own[asked], head_got))
-    replies = lax.all_to_all(served, "dp", split_axis=0, concat_axis=0, tiled=True)
+    replies = lax.all_to_all(
+        encoded_own[asked], "dp", split_axis=0, concat_axis=0, tiled=True
+    )
     mine = replies.reshape(dp_count * capacity, rows_here, enc_width)[slots]
     encoded = lax.all_gather(mine, "tensor", axis=1, tiled=True)
     heads_here = w_query.shape[1] // HD

time: 233 us -> 231 us (level)
  waiting for transfers between devices: 130 us -> 127 us
    reduce_scatter x1, waiting for transfers between devices: 52.1 us -> 32 us  [shards(): lax.psum_scatter(partial.astype(jnp.bfloat16), 'tensor', scatter_dimensio...]
    all_gather x1, waiting for transfers between devices: 41.3 us -> 55.6 us  [shards(): encoded = lax.all_gather(mine, 'tensor', axis=1, tiled=True)]
    all_gather x1, waiting for transfers between devices: 0.02 us -> 3.02 us  [shards(): states_rest = lax.all_gather(states_rest, 'tensor', axis=1, tiled=True)]
    ppermute x4, starting transfers between devices: 0.11 us -> 2.54 us  [ring_hops(): going_right = lax.ppermute(going_right, 'tensor', to_right)]
  transfers between devices with their start and end apart: 12 -> 12, of which waited for: 7 -> 9; matrix products, arithmetic and copies ran while one was open for 15% -> 15% of each run, Pallas kernels for 0% -> 0%
where the time goes in v9:
time: 231 us
  waiting for transfers between devices  127 us (55%)
  matrix products  37.1 us (16%)
  starting transfers between devices  26.3 us (11%)
  other arithmetic  16 us (7%)
  between operations  13.6 us (6%)
  local copies, waits for them, and re-layouts  10.7 us (5%)
    all_gather x1, waiting for transfers between devices, shards(): encoded = lax.all_gather(mine, 'tensor', axis=1, tiled=True)  55.6 us
    reduce_scatter x1, waiting for transfers between devices, shards(): lax.psum_scatter(partial.astype(jnp.bfloat16), 'tensor', scatter_dimensio...  32 us
    all_to_all x1, waiting for transfers between devices, shards(): lax.all_to_all(encoded_own[asked], 'dp', split_axis=0, concat_axis=0, til...  25.2 us
    ppermute x4, waiting for transfers between devices, ring_hops(): going_right = lax.ppermute(going_right, 'tensor', to_right)  10.1 us
    dot_general x8, matrix products, ring_query(): term = jnp.dot(got[offset], rows, preferred_element_type=jnp.float32)  10 us
    ppermute x3, starting transfers between devices, ring_hops(): going_left = lax.ppermute(going_left, 'tensor', to_left)  9.54 us
    dot_general x1, matrix products, shards(): jnp.einsum('btf,fe->bte', active, w_down, preferred_element_type=jnp.floa...  7.71 us
    all_to_all x1, starting transfers between devices, shards(): lax.all_to_all(requests, 'dp', split_axis=0, concat_axis=0, tiled=True)  7.59 us
  transfers between devices with their start and end apart: 12, of which 9 were waited for; matrix products, arithmetic and copies ran while one was open for 15% of the time, Pallas kernels for 0%

profile of v9, /device:TPU:1, one launch (start us, length us, event | category | flops | bytes accessed | tf_op | source)
XLA Modules:
  0.0 230.6 jit_solution(312758131262861159)
XLA Ops:
  6.5 3.0 %multiply_reduce_fusion = f32[16,128]{1,0:T(8,128)S(1)} fusion(bf16[16,128,896]{2,1,0:T(8,128)(2,1)} %param.10), kind=kLoop, calls=%fused_computation.3 | loop fusion | flops 5502976 | bytes 3678208 | tf_op jit(solution)/shard_map/reduce_sum | solution.py:101
  9.6 7.7 %convolution_convert_fusion.1 = bf16[16,128,896]{2,1,0:T(8,128)(2,1)} fusion(f32[16,128]{1,0:T(8,128)S(1)} %add_rsqrt_fusion.2, bf16[16,128,896]{2,1,0:T(8,128)(2,1)} %param.10, bf16[448,896]{1,0:T(8,128)(2,1)S(1)} %copy-done.7, bf16[896,448]{0,1:T(8,128)(2,1)S(1)} %copy-done.8), kind=kOutput, calls=%fused_computation.26 | convolution fusion | flops 3303931904 | bytes 8953856 | tf_op jit(solution)/shard_map/btf,fe->bte/dot_general | solution.py:105
  18.4 2.5 %collective-permute-start.3 = (bf16[64,512]{1,0:T(8,128)(2,1)S(1)}, bf16[64,512]{1,0:T(8,128)(2,1)S(1)}, u32[]{:S(2)}, u32[]{:S(2)}) collective-permute-start(bf16[64,512]{1,0:T(8,128)(2,1)S(1)} %slice.14), channel_id=1, source_target_pairs={{0,1},{1,2},{2,3},{3,4},{4,5},{5,6},{6,7},{7,0},{8,9},{9,10},{10,1... | collective-permute-start | bytes 196616 | tf_op jit(solution)/shard_map/ppermute | solution.py:58
  21.0 4.0 %collective-permute-start = (bf16[64,512]{1,0:T(8,128)(2,1)S(1)}, bf16[64,512]{1,0:T(8,128)(2,1)S(1)}, u32[]{:S(2)}, u32[]{:S(2)}) collective-permute-start(bf16[64,512]{1,0:T(8,128)(2,1)S(1)} %slice.14), channel_id=1, source_target_pairs={{0,7},{1,0},{2,1},{3,2},{4,3},{5,4},{6,5},{7,6},{8,15},{9,8},{10,9... | collective-permute-start | bytes 196616 | tf_op jit(solution)/shard_map/ppermute | solution.py:61
  25.0 1.6 collective-permute-done.3
  26.6 2.8 %collective-permute-start.1 = (bf16[64,512]{1,0:T(8,128)(2,1)S(1)}, bf16[64,512]{1,0:T(8,128)(2,1)S(1)}, u32[]{:S(2)}, u32[]{:S(2)}) collective-permute-start(bf16[64,512]{1,0:T(8,128)(2,1)S(1)} %collective-permute-done), channel_id=1, source_target_pairs={{0,7},{1,0},{2,1},{3,2},{4,3},{5,4},{6,5},{7,6},{8,15},{9,8},{10,9... | collective-permute-start | bytes 196616 | tf_op jit(solution)/shard_map/ppermute | solution.py:61
  29.3 1.6 collective-permute-done.4
  30.9 2.8 %collective-permute-start.2 = (bf16[64,512]{1,0:T(8,128)(2,1)S(1)}, bf16[64,512]{1,0:T(8,128)(2,1)S(1)}, u32[]{:S(2)}, u32[]{:S(2)}) collective-permute-start(bf16[64,512]{1,0:T(8,128)(2,1)S(1)} %collective-permute-done.1), channel_id=1, source_target_pairs={{0,7},{1,0},{2,1},{3,2},{4,3},{5,4},{6,5},{7,6},{8,15},{9,8},{10,9... | collective-permute-start | bytes 196616 | tf_op jit(solution)/shard_map/ppermute | solution.py:61
  33.6 1.6 collective-permute-done.5
  36.3 5.4 %collective-permute-done.6 = bf16[64,512]{1,0:T(8,128)(2,1)S(1)} collective-permute-done((bf16[64,512]{1,0:T(8,128)(2,1)S(1)}, bf16[64,512]{1,0:T(8,128)(2,1)S(1)}, u32[]{:S(2)}, u32[]{:S(2)}) %collective-permute-start.6) | collective-permute-done | bytes 65568 | tf_op jit(solution)/shard_map/ppermute | solution.py:58
  41.7 32.0 %reduce-scatter.2.cloned.1.call-done = bf16[16,16,896]{2,1,0:T(8,128)(2,1)} async-done(((bf16[16,128,896]{2,1,0:T(8,128)(2,1)}), bf16[16,16,896]{2,1,0:T(8,128)(2,1)}) %reduce-scatter.2.cloned.1.call-update) | async-done | bytes 458768 | tf_op jit(solution)/shard_map/reduce_scatter | solution.py:112
  75.0 7.6 %all-to-all-start = ((s32[32,1,2]{2,1,0:T(1,128)}), s32[32,1,2]{2,1,0:T(1,128)S(1)}, u32[]{:S(2)}, u32[]{:S(2)}) async-start(s32[32,1,2]{2,1,0:T(1,128)} %bitcast.2), calls=%async_computation.1 | async-start | bytes 32768 | tf_op jit(solution)/shard_map/all_to_all | solution.py:121
  82.6 5.8 %convert_element_type.41 = f32[16,128,896]{2,1,0:T(8,128)} convert(bf16[16,128,896]{2,1,0:T(8,128)(2,1)} %param.10) | non-fusion elementwise | flops 1835008 | bytes 11010048 | tf_op jit(solution)/shard_map/convert_element_type | solution.py:99
  89.8 1.3 add_convert_fusion
  91.1 2.0 gather_fusion
  93.1 6.3 %all-to-all-start.1 = ((bf16[32,2,16,896]{3,2,1,0:T(8,128)(2,1)}), bf16[32,2,16,896]{3,2,1,0:T(8,128)(2,1)S(1)}, u32[]{:S(2)}, u32[]{:S(2)}) async-start(bf16[32,2,16,896]{3,2,1,0:T(8,128)(2,1)} %bitcast.4), calls=%async_computation.2 | async-start | bytes 3670016 | tf_op jit(solution)/shard_map/all_to_all | solution.py:122
  99.8 25.2 %all-to-all-done.1 = bf16[32,2,16,896]{3,2,1,0:T(8,128)(2,1)S(1)} async-done(((bf16[32,2,16,896]{3,2,1,0:T(8,128)(2,1)}), bf16[32,2,16,896]{3,2,1,0:T(8,128)(2,1)S(1)}, u32[]{:S(2)}, u32[]{:S(2)}) %all-to-all-start.1) | async-done | bytes 1835040 | tf_op jit(solution)/shard_map/all_to_all | solution.py:122
  125.0 1.5 gather_fusion.1
  127.9 1.3 fusion.50
  129.1 1.3 fusion.52
  131.6 1.2 fusion.56
  132.9 1.3 fusion.58
  135.4 1.3 fusion.37
  136.7 3.0 %all-gather.4.cloned.1.call-done = bf16[641,4096]{1,0:T(8,128)(2,1)} async-done(((bf16[641,512]{1,0:T(8,128)(2,1)}), bf16[641,4096]{1,0:T(8,128)(2,1)}) %all-gather.4.cloned.1.call-update) | async-done | bytes 5251088 | tf_op jit(solution)/shard_map/all_gather | solution.py:128
  139.7 6.1 %fusion.77 = f32[641,512]{1,0:T(8,128)S(1)} fusion(bf16[641,4096]{1,0:T(8,128)(2,1)} %all-gather.4.cloned.1.call-done, bf16[4096,512]{1,0:T(8,128)(2,1)} %param.13), kind=kOutput, calls=%fused_computation.107 | convolution fusion | flops 2688548864 | bytes 10758144 | tf_op jit(solution)/shard_map/dot_general | solution.py:132
  147.1 1.7 reshape.246
  149.7 1.7 fusion.47
  151.6 55.6 %all-gather.6.cloned.1.call-done = bf16[24,128,896]{2,1,0:T(8,128)(2,1)} async-done(((bf16[24,16,896]{2,1,0:T(8,128)(2,1)}), bf16[24,128,896]{2,1,0:T(8,128)(2,1)}) %all-gather.6.cloned.1.call-update) | async-done | bytes 5505040 | tf_op jit(solution)/shard_map/all_gather | solution.py:126
  207.2 6.9 %fusion = (f32[4,3072]{1,0:T(4,128)S(1)}, f32[3072,4,128]{2,0,1:T(8,128)S(1)}) fusion(bf16[3072,896,1]{1,0,2:T(8,128)(2,1)} %bitcast.79, bf16[896,512]{1,0:T(8,128)(2,1)S(1)} %copy-done), kind=kOutput, calls=%fused_computation.6 | convolution fusion | flops 2821705728 | bytes 12763136 | tf_op jit(solution)/shard_map/ke,ehd->hkd/dot_general | solution.py:140
  214.1 3.6 %convolution_convert_fusion = bf16[3072,4,128]{2,0,1:T(8,128)(2,1)S(1)} fusion(bf16[3072,896,1]{1,0,2:T(8,128)(2,1)S(1)} %bitcast.80, bf16[896,512]{1,0:T(8,128)(2,1)S(1)} %copy-done.6), kind=kOutput, calls=%fused_computation.9 | convolution fusion | flops 2820145152 | bytes 9568256 | tf_op jit(solution)/shard_map/ke,ehd->hkd/dot_general | solution.py:147
  217.8 1.9 fusion.1
  219.7 1.3 fusion.15
  (63 shorter events, 14.2 us)
Async XLA Ops:
  6.5 200.7 %copy-start = (bf16[896,512]{1,0:T(8,128)(2,1)S(1)}, bf16[896,512]{1,0:T(8,128)(2,1)}, u32[]{:S(2)}) copy-start(bf16[896,512]{1,0:T(8,128)(2,1)} %param.14) | copy-start | bytes 2752516
  6.5 3.0 %copy-start.8 = (bf16[896,448]{0,1:T(8,128)(2,1)S(1)}, bf16[896,448]{0,1:T(8,128)(2,1)}, u32[]{:S(2)}) copy-start(bf16[896,448]{0,1:T(8,128)(2,1)} %param.11) | copy-start | bytes 2408452
  6.5 3.0 %copy-start.7 = (bf16[448,896]{1,0:T(8,128)(2,1)S(1)}, bf16[448,896]{1,0:T(8,128)(2,1)}, u32[]{:S(2)}) copy-start(bf16[448,896]{1,0:T(8,128)(2,1)} %param.12) | copy-start | bytes 2408452
  6.5 67.1 %reduce-scatter.2.cloned.1.call-start = ((), (), s32[]{:S(2)}) async-start(), calls=%async_computation.3 | async-start | bytes 4128768 | tf_op jit(solution)/shard_map/reduce_scatter | solution.py:112
  17.3 1.1 copy-start.2
  17.3 56.4 %copy-start.4 = (s32[12,2]{0,1:T(2,128)S(1)}, s32[12,2]{0,1:T(2,128)}, u32[]{:S(2)}) copy-start(s32[12,2]{0,1:T(2,128)} %param.9) | copy-start | bytes 292
  17.3 122.4 %all-gather.4.cloned.1.call-start = ((), (), s32[]{:S(2)}) async-start(), calls=%async_computation.4 | async-start | bytes 5971968 | tf_op jit(solution)/shard_map/all_gather | solution.py:128
  18.4 8.1 %collective-permute-start.3 = (bf16[64,512]{1,0:T(8,128)(2,1)S(1)}, bf16[64,512]{1,0:T(8,128)(2,1)S(1)}, u32[]{:S(2)}, u32[]{:S(2)}) collective-permute-start(bf16[64,512]{1,0:T(8,128)(2,1)S(1)} %slice.14), channel_id=1, source_target_pairs={{0,1},{1,2},{2,3},{3,4},{4,5},{5,6},{6,7},{7,0},{8,9},{9,10},{10,1... | collective-permute-start | bytes 196616 | tf_op jit(solution)/shard_map/ppermute | solution.py:58
  21.0 5.6 %collective-permute-start = (bf16[64,512]{1,0:T(8,128)(2,1)S(1)}, bf16[64,512]{1,0:T(8,128)(2,1)S(1)}, u32[]{:S(2)}, u32[]{:S(2)}) collective-permute-start(bf16[64,512]{1,0:T(8,128)(2,1)S(1)} %slice.14), channel_id=1, source_target_pairs={{0,7},{1,0},{2,1},{3,2},{4,3},{5,4},{6,5},{7,6},{8,15},{9,8},{10,9... | collective-permute-start | bytes 196616 | tf_op jit(solution)/shard_map/ppermute | solution.py:61
  26.5 4.3 %collective-permute-start.4 = (bf16[64,512]{1,0:T(8,128)(2,1)S(1)}, bf16[64,512]{1,0:T(8,128)(2,1)S(1)}, u32[]{:S(2)}, u32[]{:S(2)}) collective-permute-start(bf16[64,512]{1,0:T(8,128)(2,1)S(1)} %collective-permute-done.3), channel_id=1, source_target_pairs={{0,1},{1,2},{2,3},{3,4},{4,5},{5,6},{6,7},{7,0},{8,9},{9,10},{10,1... | collective-permute-start | bytes 196616 | tf_op jit(solution)/shard_map/ppermute | solution.py:58
  26.6 4.3 %collective-permute-start.1 = (bf16[64,512]{1,0:T(8,128)(2,1)S(1)}, bf16[64,512]{1,0:T(8,128)(2,1)S(1)}, u32[]{:S(2)}, u32[]{:S(2)}) collective-permute-start(bf16[64,512]{1,0:T(8,128)(2,1)S(1)} %collective-permute-done), channel_id=1, source_target_pairs={{0,7},{1,0},{2,1},{3,2},{4,3},{5,4},{6,5},{7,6},{8,15},{9,8},{10,9... | collective-permute-start | bytes 196616 | tf_op jit(solution)/shard_map/ppermute | solution.py:61
  30.9 4.3 %collective-permute-start.5 = (bf16[64,512]{1,0:T(8,128)(2,1)S(1)}, bf16[64,512]{1,0:T(8,128)(2,1)S(1)}, u32[]{:S(2)}, u32[]{:S(2)}) collective-permute-start(bf16[64,512]{1,0:T(8,128)(2,1)S(1)} %collective-permute-done.4), channel_id=1, source_target_pairs={{0,1},{1,2},{2,3},{3,4},{4,5},{5,6},{6,7},{7,0},{8,9},{9,10},{10,1... | collective-permute-start | bytes 196616 | tf_op jit(solution)/shard_map/ppermute | solution.py:58
  30.9 5.4 %collective-permute-start.2 = (bf16[64,512]{1,0:T(8,128)(2,1)S(1)}, bf16[64,512]{1,0:T(8,128)(2,1)S(1)}, u32[]{:S(2)}, u32[]{:S(2)}) collective-permute-start(bf16[64,512]{1,0:T(8,128)(2,1)S(1)} %collective-permute-done.1), channel_id=1, source_target_pairs={{0,7},{1,0},{2,1},{3,2},{4,3},{5,4},{6,5},{7,6},{8,15},{9,8},{10,9... | collective-permute-start | bytes 196616 | tf_op jit(solution)/shard_map/ppermute | solution.py:61
  35.2 6.4 %collective-permute-start.6 = (bf16[64,512]{1,0:T(8,128)(2,1)S(1)}, bf16[64,512]{1,0:T(8,128)(2,1)S(1)}, u32[]{:S(2)}, u32[]{:S(2)}) collective-permute-start(bf16[64,512]{1,0:T(8,128)(2,1)S(1)} %collective-permute-done.5), channel_id=1, source_target_pairs={{0,1},{1,2},{2,3},{3,4},{4,5},{5,6},{6,7},{7,0},{8,9},{9,10},{10,1... | collective-permute-start | bytes 196616 | tf_op jit(solution)/shard_map/ppermute | solution.py:58
  75.0 14.5 %all-to-all-start = ((s32[32,1,2]{2,1,0:T(1,128)}), s32[32,1,2]{2,1,0:T(1,128)S(1)}, u32[]{:S(2)}, u32[]{:S(2)}) async-start(s32[32,1,2]{2,1,0:T(1,128)} %bitcast.2), calls=%async_computation.1 | async-start | bytes 32768 | tf_op jit(solution)/shard_map/all_to_all | solution.py:121
  82.6 7.2 %copy-start.3 = (bf16[16,16,896]{2,1,0:T(8,128)(2,1)S(1)}, bf16[16,16,896]{2,1,0:T(8,128)(2,1)}, u32[]{:S(2)}) copy-start(bf16[16,16,896]{2,1,0:T(8,128)(2,1)} %reduce-scatter.2.cloned.1.call-done) | copy-start | bytes 1376260
  93.1 31.9 %all-to-all-start.1 = ((bf16[32,2,16,896]{3,2,1,0:T(8,128)(2,1)}), bf16[32,2,16,896]{3,2,1,0:T(8,128)(2,1)S(1)}, u32[]{:S(2)}, u32[]{:S(2)}) async-start(bf16[32,2,16,896]{3,2,1,0:T(8,128)(2,1)} %bitcast.4), calls=%async_computation.2 | async-start | bytes 3670016 | tf_op jit(solution)/shard_map/all_to_all | solution.py:122
  99.5 107.7 %all-gather.6.cloned.1.call-start = ((), (), s32[]{:S(2)}) async-start(), calls=%async_computation.5 | async-start | bytes 6193152 | tf_op jit(solution)/shard_map/all_gather | solution.py:126
  207.2 6.9 %copy-start.5 = (bf16[24,128,896]{2,1,0:T(8,128)(2,1)S(1)}, bf16[24,128,896]{2,1,0:T(8,128)(2,1)}, u32[]{:S(2)}) copy-start(bf16[24,128,896]{2,1,0:T(8,128)(2,1)} %all-gather.6.cloned.1.call-done) | copy-start | bytes 16515076
  207.2 6.9 %copy-start.6 = (bf16[896,512]{1,0:T(8,128)(2,1)S(1)}, bf16[896,512]{1,0:T(8,128)(2,1)}, u32[]{:S(2)}) copy-start(bf16[896,512]{1,0:T(8,128)(2,1)} %param.15) | copy-start | bytes 2752516
  221.0 3.0 %copy-start.1 = (bf16[896,512]{1,0:T(8,128)(2,1)S(1)}, bf16[896,512]{1,0:T(8,128)(2,1)}, u32[]{:S(2)}) copy-start(bf16[896,512]{1,0:T(8,128)(2,1)} %param.14) | copy-start | bytes 2752516
Sparse Core Ops, SparseCore 0:
  17.4 56.2 reduce-scatter.1
  75.5 64.2 all-gather.3
  141.5 65.6 all-gather.5

commit v10 on v9

--- a/solution.py
+++ b/solution.py
@@ -105,7 +105,7 @@
     partial = jnp.einsum("btf,fe->bte", active, w_down, preferred_element_type=jnp.float32)
     rows_here = block_tokens // tensor_count
     states = hidden_states[SPAN - 1 :]
-    head_rows = SPAN
+    head_rows = 2 * SPAN
     head_got = {0: states[:head_rows]}
     for step in ring_hops(states[:head_rows], tensor_count):
         head_got.update(step)

time: 231 us -> 230 us (level)
    ppermute x4, waiting for transfers between devices: 10.1 us -> 18.4 us  [ring_hops(): going_right = lax.ppermute(going_right, 'tensor', to_right)]
    reduce_scatter x1, waiting for transfers between devices: 32 us -> 27.1 us  [shards(): lax.psum_scatter(partial.astype(jnp.bfloat16), 'tensor', scatter_dimensio...]
    all_gather x1, waiting for transfers between devices: 3.02 us -> 0.02 us  [shards(): states_rest = lax.all_gather(states_rest, 'tensor', axis=1, tiled=True)]
  transfers between devices with their start and end apart: 12 -> 12, of which waited for: 9 -> 8; matrix products, arithmetic and copies ran while one was open for 15% -> 15% of each run, Pallas kernels for 0% -> 0%
where the time goes in v10:
time: 230 us; the launch traced here: 229 us
  waiting for transfers between devices  125 us (54%)
  matrix products  37.1 us (16%)
  starting transfers between devices  26.4 us (11%)
  other arithmetic  16 us (7%)
  between operations  13.6 us (6%)
  local copies, waits for them, and re-layouts  10.6 us (5%)
    all_gather x1, waiting for transfers between devices, shards(): encoded = lax.all_gather(mine, 'tensor', axis=1, tiled=True)  53.3 us
    reduce_scatter x1, waiting for transfers between devices, shards(): lax.psum_scatter(partial.astype(jnp.bfloat16), 'tensor', scatter_dimensio...  27.1 us
    all_to_all x1, waiting for transfers between devices, shards(): lax.all_to_all(encoded_own[asked], 'dp', split_axis=0, concat_axis=0, til...  25.2 us
    ppermute x4, waiting for transfers between devices, ring_hops(): going_right = lax.ppermute(going_right, 'tensor', to_right)  18.4 us
    dot_general x8, matrix products, ring_query(): term = jnp.dot(got[offset], rows, preferred_element_type=jnp.float32)  10.3 us
    ppermute x3, starting transfers between devices, ring_hops(): going_left = lax.ppermute(going_left, 'tensor', to_left)  9.68 us
    dot_general x1, matrix products, shards(): jnp.einsum('btf,fe->bte', active, w_down, preferred_element_type=jnp.floa...  7.71 us
    all_to_all x1, starting transfers between devices, shards(): lax.all_to_all(requests, 'dp', split_axis=0, concat_axis=0, tiled=True)  7.59 us
  transfers between devices with their start and end apart: 12, of which 8 were waited for; matrix products, arithmetic and copies ran while one was open for 15% of the time, Pallas kernels for 0%

profile of v10, /device:TPU:1, one launch (start us, length us, event | category | flops | bytes accessed | tf_op | source)
XLA Modules:
  0.0 228.9 jit_solution(10558666336854750705)
XLA Ops:
  6.5 3.0 %multiply_reduce_fusion = f32[16,128]{1,0:T(8,128)S(1)} fusion(bf16[16,128,896]{2,1,0:T(8,128)(2,1)} %param.10), kind=kLoop, calls=%fused_computation.3 | loop fusion | flops 5502976 | bytes 3678208 | tf_op jit(solution)/shard_map/reduce_sum | solution.py:101
  9.6 7.7 %convolution_convert_fusion.1 = bf16[16,128,896]{2,1,0:T(8,128)(2,1)} fusion(f32[16,128]{1,0:T(8,128)S(1)} %add_rsqrt_fusion.2, bf16[16,128,896]{2,1,0:T(8,128)(2,1)} %param.10, bf16[448,896]{1,0:T(8,128)(2,1)S(1)} %copy-done.11, bf16[896,448]{0,1:T(8,128)(2,1)S(1)} %copy-done.12), kind=kOutput, calls=%fused_computation.26 | convolution fusion | flops 3303931904 | bytes 8953856 | tf_op jit(solution)/shard_map/btf,fe->bte/dot_general | solution.py:105
  18.4 2.5 %collective-permute-start.3 = (bf16[128,512]{1,0:T(8,128)(2,1)S(1)}, bf16[128,512]{1,0:T(8,128)(2,1)S(1)}, u32[]{:S(2)}, u32[]{:S(2)}) collective-permute-start(bf16[128,512]{1,0:T(8,128)(2,1)S(1)} %slice.14), channel_id=1, source_target_pairs={{0,1},{1,2},{2,3},{3,4},{4,5},{5,6},{6,7},{7,0},{8,9},{9,10},{10,1... | collective-permute-start | bytes 393224 | tf_op jit(solution)/shard_map/ppermute | solution.py:58
  21.0 4.0 %collective-permute-start = (bf16[128,512]{1,0:T(8,128)(2,1)S(1)}, bf16[128,512]{1,0:T(8,128)(2,1)S(1)}, u32[]{:S(2)}, u32[]{:S(2)}) collective-permute-start(bf16[128,512]{1,0:T(8,128)(2,1)S(1)} %slice.14), channel_id=1, source_target_pairs={{0,7},{1,0},{2,1},{3,2},{4,3},{5,4},{6,5},{7,6},{8,15},{9,8},{10,9... | collective-permute-start | bytes 393224 | tf_op jit(solution)/shard_map/ppermute | solution.py:61
  25.0 3.1 %collective-permute-done.3 = bf16[128,512]{1,0:T(8,128)(2,1)S(1)} collective-permute-done((bf16[128,512]{1,0:T(8,128)(2,1)S(1)}, bf16[128,512]{1,0:T(8,128)(2,1)S(1)}, u32[]{:S(2)}, u32[]{:S(2)}) %collective-permute-start.3) | collective-permute-done | bytes 131104 | tf_op jit(solution)/shard_map/ppermute | solution.py:58
  28.1 2.7 %collective-permute-start.1 = (bf16[128,512]{1,0:T(8,128)(2,1)S(1)}, bf16[128,512]{1,0:T(8,128)(2,1)S(1)}, u32[]{:S(2)}, u32[]{:S(2)}) collective-permute-start(bf16[128,512]{1,0:T(8,128)(2,1)S(1)} %collective-permute-done), channel_id=1, source_target_pairs={{0,7},{1,0},{2,1},{3,2},{4,3},{5,4},{6,5},{7,6},{8,15},{9,8},{10,9... | collective-permute-start | bytes 393224 | tf_op jit(solution)/shard_map/ppermute | solution.py:61
  30.8 2.3 %collective-permute-done.4 = bf16[128,512]{1,0:T(8,128)(2,1)S(1)} collective-permute-done((bf16[128,512]{1,0:T(8,128)(2,1)S(1)}, bf16[128,512]{1,0:T(8,128)(2,1)S(1)}, u32[]{:S(2)}, u32[]{:S(2)}) %collective-permute-start.4) | collective-permute-done | bytes 131104 | tf_op jit(solution)/shard_map/ppermute | solution.py:58
  33.1 3.0 %collective-permute-start.2 = (bf16[128,512]{1,0:T(8,128)(2,1)S(1)}, bf16[128,512]{1,0:T(8,128)(2,1)S(1)}, u32[]{:S(2)}, u32[]{:S(2)}) collective-permute-start(bf16[128,512]{1,0:T(8,128)(2,1)S(1)} %collective-permute-done.1), channel_id=1, source_target_pairs={{0,7},{1,0},{2,1},{3,2},{4,3},{5,4},{6,5},{7,6},{8,15},{9,8},{10,9... | collective-permute-start | bytes 393224 | tf_op jit(solution)/shard_map/ppermute | solution.py:61
  36.1 5.4 %collective-permute-done.5 = bf16[128,512]{1,0:T(8,128)(2,1)S(1)} collective-permute-done((bf16[128,512]{1,0:T(8,128)(2,1)S(1)}, bf16[128,512]{1,0:T(8,128)(2,1)S(1)}, u32[]{:S(2)}, u32[]{:S(2)}) %collective-permute-start.5) | collective-permute-done | bytes 131104 | tf_op jit(solution)/shard_map/ppermute | solution.py:58
  42.5 7.5 %collective-permute-done.6 = bf16[128,512]{1,0:T(8,128)(2,1)S(1)} collective-permute-done((bf16[128,512]{1,0:T(8,128)(2,1)S(1)}, bf16[128,512]{1,0:T(8,128)(2,1)S(1)}, u32[]{:S(2)}, u32[]{:S(2)}) %collective-permute-start.6) | collective-permute-done | bytes 131104 | tf_op jit(solution)/shard_map/ppermute | solution.py:58
  50.0 27.1 %reduce-scatter.2.cloned.1.call-done = bf16[16,16,896]{2,1,0:T(8,128)(2,1)} async-done(((bf16[16,128,896]{2,1,0:T(8,128)(2,1)}), bf16[16,16,896]{2,1,0:T(8,128)(2,1)}) %reduce-scatter.2.cloned.1.call-update) | async-done | bytes 458768 | tf_op jit(solution)/shard_map/reduce_scatter | solution.py:112
  78.5 7.6 %all-to-all-start = ((s32[32,1,2]{2,1,0:T(1,128)}), s32[32,1,2]{2,1,0:T(1,128)S(1)}, u32[]{:S(2)}, u32[]{:S(2)}) async-start(s32[32,1,2]{2,1,0:T(1,128)} %bitcast.2), calls=%async_computation.1 | async-start | bytes 32768 | tf_op jit(solution)/shard_map/all_to_all | solution.py:121
  86.1 5.8 %convert_element_type.41 = f32[16,128,896]{2,1,0:T(8,128)} convert(bf16[16,128,896]{2,1,0:T(8,128)(2,1)} %param.10) | non-fusion elementwise | flops 1835008 | bytes 11010048 | tf_op jit(solution)/shard_map/convert_element_type | solution.py:99
  93.3 1.3 add_convert_fusion
  94.6 2.0 gather_fusion
  96.6 6.4 %all-to-all-start.1 = ((bf16[32,2,16,896]{3,2,1,0:T(8,128)(2,1)}), bf16[32,2,16,896]{3,2,1,0:T(8,128)(2,1)S(1)}, u32[]{:S(2)}, u32[]{:S(2)}) async-start(bf16[32,2,16,896]{3,2,1,0:T(8,128)(2,1)} %bitcast.4), calls=%async_computation.2 | async-start | bytes 3670016 | tf_op jit(solution)/shard_map/all_to_all | solution.py:122
  103.3 25.2 %all-to-all-done.1 = bf16[32,2,16,896]{3,2,1,0:T(8,128)(2,1)S(1)} async-done(((bf16[32,2,16,896]{3,2,1,0:T(8,128)(2,1)}), bf16[32,2,16,896]{3,2,1,0:T(8,128)(2,1)S(1)}, u32[]{:S(2)}, u32[]{:S(2)}) %all-to-all-start.1) | async-done | bytes 1835040 | tf_op jit(solution)/shard_map/all_to_all | solution.py:122
  128.5 1.5 gather_fusion.1
  130.1 1.3 fusion.48
  131.4 1.3 fusion.50
  132.7 1.3 fusion.52
  134.0 1.3 fusion.54
  137.9 1.3 fusion.60
  139.1 1.3 fusion.37
  140.5 5.9 %fusion.77 = f32[577,512]{1,0:T(8,128)S(1)} fusion(bf16[577,4096]{1,0:T(8,128)(2,1)} %all-gather.4.cloned.1.call-done, bf16[4096,512]{1,0:T(8,128)(2,1)} %param.13), kind=kOutput, calls=%fused_computation.107 | convolution fusion | flops 2420113408 | bytes 10102784 | tf_op jit(solution)/shard_map/dot_general | solution.py:132
  147.7 1.7 reshape.246
  150.3 1.7 fusion.47
  152.2 53.3 %all-gather.6.cloned.1.call-done = bf16[24,128,896]{2,1,0:T(8,128)(2,1)} async-done(((bf16[24,16,896]{2,1,0:T(8,128)(2,1)}), bf16[24,128,896]{2,1,0:T(8,128)(2,1)}) %all-gather.6.cloned.1.call-update) | async-done | bytes 5505040 | tf_op jit(solution)/shard_map/all_gather | solution.py:126
  205.5 6.9 %fusion = (f32[4,3072]{1,0:T(4,128)S(1)}, f32[3072,4,128]{2,0,1:T(8,128)S(1)}) fusion(bf16[3072,896,1]{1,0,2:T(8,128)(2,1)} %bitcast.79, bf16[896,512]{1,0:T(8,128)(2,1)S(1)} %copy-done), kind=kOutput, calls=%fused_computation.6 | convolution fusion | flops 2821705728 | bytes 12763136 | tf_op jit(solution)/shard_map/ke,ehd->hkd/dot_general | solution.py:140
  212.4 3.6 %convolution_convert_fusion = bf16[3072,4,128]{2,0,1:T(8,128)(2,1)S(1)} fusion(bf16[3072,896,1]{1,0,2:T(8,128)(2,1)S(1)} %bitcast.80, bf16[896,512]{1,0:T(8,128)(2,1)S(1)} %copy-done.10), kind=kOutput, calls=%fused_computation.9 | convolution fusion | flops 2820145152 | bytes 9568256 | tf_op jit(solution)/shard_map/ke,ehd->hkd/dot_general | solution.py:147
  216.1 1.9 fusion.1
  218.0 1.3 fusion.15
  (71 shorter events, 13.0 us)
Async XLA Ops:
  6.5 199.0 %copy-start = (bf16[896,512]{1,0:T(8,128)(2,1)S(1)}, bf16[896,512]{1,0:T(8,128)(2,1)}, u32[]{:S(2)}) copy-start(bf16[896,512]{1,0:T(8,128)(2,1)} %param.14) | copy-start | bytes 2752516
  6.5 3.0 %copy-start.12 = (bf16[896,448]{0,1:T(8,128)(2,1)S(1)}, bf16[896,448]{0,1:T(8,128)(2,1)}, u32[]{:S(2)}) copy-start(bf16[896,448]{0,1:T(8,128)(2,1)} %param.11) | copy-start | bytes 2408452
  6.5 3.0 %copy-start.11 = (bf16[448,896]{1,0:T(8,128)(2,1)S(1)}, bf16[448,896]{1,0:T(8,128)(2,1)}, u32[]{:S(2)}) copy-start(bf16[448,896]{1,0:T(8,128)(2,1)} %param.12) | copy-start | bytes 2408452
  6.5 70.6 %reduce-scatter.2.cloned.1.call-start = ((), (), s32[]{:S(2)}) async-start(), calls=%async_computation.3 | async-start | bytes 4128768 | tf_op jit(solution)/shard_map/reduce_scatter | solution.py:112
  17.3 1.1 copy-start.2
  17.3 59.9 %copy-start.8 = (s32[12,2]{0,1:T(2,128)S(1)}, s32[12,2]{0,1:T(2,128)}, u32[]{:S(2)}) copy-start(s32[12,2]{0,1:T(2,128)} %param.9) | copy-start | bytes 292
  17.3 123.2 %all-gather.4.cloned.1.call-start = ((), (), s32[]{:S(2)}) async-start(), calls=%async_computation.4 | async-start | bytes 5382144 | tf_op jit(solution)/shard_map/all_gather | solution.py:128
  18.4 9.7 %collective-permute-start.3 = (bf16[128,512]{1,0:T(8,128)(2,1)S(1)}, bf16[128,512]{1,0:T(8,128)(2,1)S(1)}, u32[]{:S(2)}, u32[]{:S(2)}) collective-permute-start(bf16[128,512]{1,0:T(8,128)(2,1)S(1)} %slice.14), channel_id=1, source_target_pairs={{0,1},{1,2},{2,3},{3,4},{4,5},{5,6},{6,7},{7,0},{8,9},{9,10},{10,1... | collective-permute-start | bytes 393224 | tf_op jit(solution)/shard_map/ppermute | solution.py:58
  21.0 7.1 %collective-permute-start = (bf16[128,512]{1,0:T(8,128)(2,1)S(1)}, bf16[128,512]{1,0:T(8,128)(2,1)S(1)}, u32[]{:S(2)}, u32[]{:S(2)}) collective-permute-start(bf16[128,512]{1,0:T(8,128)(2,1)S(1)} %slice.14), channel_id=1, source_target_pairs={{0,7},{1,0},{2,1},{3,2},{4,3},{5,4},{6,5},{7,6},{8,15},{9,8},{10,9... | collective-permute-start | bytes 393224 | tf_op jit(solution)/shard_map/ppermute | solution.py:61
  28.1 5.0 %collective-permute-start.4 = (bf16[128,512]{1,0:T(8,128)(2,1)S(1)}, bf16[128,512]{1,0:T(8,128)(2,1)S(1)}, u32[]{:S(2)}, u32[]{:S(2)}) collective-permute-start(bf16[128,512]{1,0:T(8,128)(2,1)S(1)} %collective-permute-done.3), channel_id=1, source_target_pairs={{0,1},{1,2},{2,3},{3,4},{4,5},{5,6},{6,7},{7,0},{8,9},{9,10},{10,1... | collective-permute-start | bytes 393224 | tf_op jit(solution)/shard_map/ppermute | solution.py:58
  28.1 5.0 %collective-permute-start.1 = (bf16[128,512]{1,0:T(8,128)(2,1)S(1)}, bf16[128,512]{1,0:T(8,128)(2,1)S(1)}, u32[]{:S(2)}, u32[]{:S(2)}) collective-permute-start(bf16[128,512]{1,0:T(8,128)(2,1)S(1)} %collective-permute-done), channel_id=1, source_target_pairs={{0,7},{1,0},{2,1},{3,2},{4,3},{5,4},{6,5},{7,6},{8,15},{9,8},{10,9... | collective-permute-start | bytes 393224 | tf_op jit(solution)/shard_map/ppermute | solution.py:61
  33.1 8.4 %collective-permute-start.5 = (bf16[128,512]{1,0:T(8,128)(2,1)S(1)}, bf16[128,512]{1,0:T(8,128)(2,1)S(1)}, u32[]{:S(2)}, u32[]{:S(2)}) collective-permute-start(bf16[128,512]{1,0:T(8,128)(2,1)S(1)} %collective-permute-done.4), channel_id=1, source_target_pairs={{0,1},{1,2},{2,3},{3,4},{4,5},{5,6},{6,7},{7,0},{8,9},{9,10},{10,1... | collective-permute-start | bytes 393224 | tf_op jit(solution)/shard_map/ppermute | solution.py:58
  33.1 9.4 %collective-permute-start.2 = (bf16[128,512]{1,0:T(8,128)(2,1)S(1)}, bf16[128,512]{1,0:T(8,128)(2,1)S(1)}, u32[]{:S(2)}, u32[]{:S(2)}) collective-permute-start(bf16[128,512]{1,0:T(8,128)(2,1)S(1)} %collective-permute-done.1), channel_id=1, source_target_pairs={{0,7},{1,0},{2,1},{3,2},{4,3},{5,4},{6,5},{7,6},{8,15},{9,8},{10,9... | collective-permute-start | bytes 393224 | tf_op jit(solution)/shard_map/ppermute | solution.py:61
  41.5 8.5 %collective-permute-start.6 = (bf16[128,512]{1,0:T(8,128)(2,1)S(1)}, bf16[128,512]{1,0:T(8,128)(2,1)S(1)}, u32[]{:S(2)}, u32[]{:S(2)}) collective-permute-start(bf16[128,512]{1,0:T(8,128)(2,1)S(1)} %collective-permute-done.5), channel_id=1, source_target_pairs={{0,1},{1,2},{2,3},{3,4},{4,5},{5,6},{6,7},{7,0},{8,9},{9,10},{10,1... | collective-permute-start | bytes 393224 | tf_op jit(solution)/shard_map/ppermute | solution.py:58
  42.5 43.6 %copy-start.4 = (bf16[128,512]{1,0:T(8,128)(2,1)}, bf16[128,512]{1,0:T(8,128)(2,1)S(1)}, u32[]{:S(2)}) copy-start(bf16[128,512]{1,0:T(8,128)(2,1)S(1)} %collective-permute-done.2) | copy-start | bytes 393220
  50.0 41.9 %copy-start.6 = (bf16[128,512]{1,0:T(8,128)(2,1)}, bf16[128,512]{1,0:T(8,128)(2,1)S(1)}, u32[]{:S(2)}) copy-start(bf16[128,512]{1,0:T(8,128)(2,1)S(1)} %collective-permute-done.6) | copy-start | bytes 393220
  78.5 14.5 %all-to-all-start = ((s32[32,1,2]{2,1,0:T(1,128)}), s32[32,1,2]{2,1,0:T(1,128)S(1)}, u32[]{:S(2)}, u32[]{:S(2)}) async-start(s32[32,1,2]{2,1,0:T(1,128)} %bitcast.2), calls=%async_computation.1 | async-start | bytes 32768 | tf_op jit(solution)/shard_map/all_to_all | solution.py:121
  86.1 7.2 %copy-start.3 = (bf16[16,16,896]{2,1,0:T(8,128)(2,1)S(1)}, bf16[16,16,896]{2,1,0:T(8,128)(2,1)}, u32[]{:S(2)}) copy-start(bf16[16,16,896]{2,1,0:T(8,128)(2,1)} %reduce-scatter.2.cloned.1.call-done) | copy-start | bytes 1376260
  96.6 31.9 %all-to-all-start.1 = ((bf16[32,2,16,896]{3,2,1,0:T(8,128)(2,1)}), bf16[32,2,16,896]{3,2,1,0:T(8,128)(2,1)S(1)}, u32[]{:S(2)}, u32[]{:S(2)}) async-start(bf16[32,2,16,896]{3,2,1,0:T(8,128)(2,1)} %bitcast.4), calls=%async_computation.2 | async-start | bytes 3670016 | tf_op jit(solution)/shard_map/all_to_all | solution.py:122
  103.0 102.5 %all-gather.6.cloned.1.call-start = ((), (), s32[]{:S(2)}) async-start(), calls=%async_computation.5 | async-start | bytes 6193152 | tf_op jit(solution)/shard_map/all_gather | solution.py:126
  130.0 4.0 %copy-start.7 = (bf16[128,512]{1,0:T(8,128)(2,1)S(1)}, bf16[128,512]{1,0:T(8,128)(2,1)}, u32[]{:S(2)}) copy-start(bf16[128,512]{1,0:T(8,128)(2,1)} %copy-done.6) | copy-start | bytes 393220
  130.0 5.3 %copy-start.5 = (bf16[128,512]{1,0:T(8,128)(2,1)S(1)}, bf16[128,512]{1,0:T(8,128)(2,1)}, u32[]{:S(2)}) copy-start(bf16[128,512]{1,0:T(8,128)(2,1)} %copy-done.4) | copy-start | bytes 393220
  205.5 6.9 %copy-start.9 = (bf16[24,128,896]{2,1,0:T(8,128)(2,1)S(1)}, bf16[24,128,896]{2,1,0:T(8,128)(2,1)}, u32[]{:S(2)}) copy-start(bf16[24,128,896]{2,1,0:T(8,128)(2,1)} %all-gather.6.cloned.1.call-done) | copy-start | bytes 16515076
  205.5 6.9 %copy-start.10 = (bf16[896,512]{1,0:T(8,128)(2,1)S(1)}, bf16[896,512]{1,0:T(8,128)(2,1)}, u32[]{:S(2)}) copy-start(bf16[896,512]{1,0:T(8,128)(2,1)} %param.15) | copy-start | bytes 2752516
  219.3 3.0 %copy-start.1 = (bf16[896,512]{1,0:T(8,128)(2,1)S(1)}, bf16[896,512]{1,0:T(8,128)(2,1)}, u32[]{:S(2)}) copy-start(bf16[896,512]{1,0:T(8,128)(2,1)} %param.14) | copy-start | bytes 2752516
Sparse Core Ops, SparseCore 0:
  17.4 59.7 reduce-scatter.1
  79.0 59.0 all-gather.3
  139.8 65.6 all-gather.5

commit v11 on v10

--- a/solution.py
+++ b/solution.py
@@ -105,7 +105,7 @@
     partial = jnp.einsum("btf,fe->bte", active, w_down, preferred_element_type=jnp.float32)
     rows_here = block_tokens // tensor_count
     states = hidden_states[SPAN - 1 :]
-    head_rows = 2 * SPAN
+    head_rows = 3 * SPAN
     head_got = {0: states[:head_rows]}
     for step in ring_hops(states[:head_rows], tensor_count):
         head_got.update(step)

time: 230 us -> 229 us (level)
  matrix products: 37.1 us -> 33.5 us
  waiting for transfers between devices: 125 us -> 128 us
    ppermute x3, waiting for transfers between devices: 0.01 us -> 7.73 us  [ring_hops(): going_left = lax.ppermute(going_left, 'tensor', to_left)]
    dot_general x8, matrix products: 10.3 us -> 6.74 us  [ring_query(): term = jnp.dot(got[offset], rows, preferred_element_type=jnp.float32)]
    reduce_scatter x1, waiting for transfers between devices: 27.1 us -> 23.8 us  [shards(): lax.psum_scatter(partial.astype(jnp.bfloat16), 'tensor', scatter_dimensio...]
  transfers between devices with their start and end apart: 12 -> 12, of which waited for: 8 -> 10; matrix products, arithmetic and copies ran while one was open for 15% -> 13% of each run, Pallas kernels for 0% -> 0%
where the time goes in v11:
time: 229 us
  waiting for transfers between devices  128 us (56%)
  matrix products  33.5 us (15%)
  starting transfers between devices  27 us (12%)
  other arithmetic  16 us (7%)
  between operations  13.6 us (6%)
  local copies, waits for them, and re-layouts  10.6 us (5%)
    all_gather x1, waiting for transfers between devices, shards(): encoded = lax.all_gather(mine, 'tensor', axis=1, tiled=True)  52.7 us
    all_to_all x1, waiting for transfers between devices, shards(): lax.all_to_all(encoded_own[asked], 'dp', split_axis=0, concat_axis=0, til...  25.2 us
    reduce_scatter x1, waiting for transfers between devices, shards(): lax.psum_scatter(partial.astype(jnp.bfloat16), 'tensor', scatter_dimensio...  23.8 us
    ppermute x4, waiting for transfers between devices, ring_hops(): going_right = lax.ppermute(going_right, 'tensor', to_right)  17.8 us
    ppermute x3, starting transfers between devices, ring_hops(): going_left = lax.ppermute(going_left, 'tensor', to_left)  10.2 us
    ppermute x3, waiting for transfers between devices, ring_hops(): going_left = lax.ppermute(going_left, 'tensor', to_left)  7.73 us
    dot_general x1, matrix products, shards(): jnp.einsum('btf,fe->bte', active, w_down, preferred_element_type=jnp.floa...  7.69 us
    all_to_all x1, starting transfers between devices, shards(): lax.all_to_all(requests, 'dp', split_axis=0, concat_axis=0, tiled=True)  7.59 us
  transfers between devices with their start and end apart: 12, of which 10 were waited for; matrix products, arithmetic and copies ran while one was open for 13% of the time, Pallas kernels for 0%

profile of v11, /device:TPU:1, one launch (start us, length us, event | category | flops | bytes accessed | tf_op | source)
XLA Modules:
  0.0 229.0 jit_solution(14006398751083424595)
XLA Ops:
  6.5 3.0 %multiply_reduce_fusion = f32[16,128]{1,0:T(8,128)S(1)} fusion(bf16[16,128,896]{2,1,0:T(8,128)(2,1)} %param.10), kind=kLoop, calls=%fused_computation.3 | loop fusion | flops 5502976 | bytes 3678208 | tf_op jit(solution)/shard_map/reduce_sum | solution.py:101
  9.6 7.7 %convolution_convert_fusion.1 = bf16[16,128,896]{2,1,0:T(8,128)(2,1)} fusion(f32[16,128]{1,0:T(8,128)S(1)} %add_rsqrt_fusion.2, bf16[16,128,896]{2,1,0:T(8,128)(2,1)} %param.10, bf16[448,896]{1,0:T(8,128)(2,1)S(1)} %copy-done.14, bf16[896,448]{0,1:T(8,128)(2,1)S(1)} %copy-done.15), kind=kOutput, calls=%fused_computation.26 | convolution fusion | flops 3303931904 | bytes 8953856 | tf_op jit(solution)/shard_map/btf,fe->bte/dot_general | solution.py:105
  18.4 2.5 %collective-permute-start.3 = (bf16[192,512]{1,0:T(8,128)(2,1)S(1)}, bf16[192,512]{1,0:T(8,128)(2,1)S(1)}, u32[]{:S(2)}, u32[]{:S(2)}) collective-permute-start(bf16[192,512]{1,0:T(8,128)(2,1)S(1)} %slice.14), channel_id=1, source_target_pairs={{0,1},{1,2},{2,3},{3,4},{4,5},{5,6},{6,7},{7,0},{8,9},{9,10},{10,1... | collective-permute-start | bytes 589832 | tf_op jit(solution)/shard_map/ppermute | solution.py:58
  21.0 4.0 %collective-permute-start = (bf16[192,512]{1,0:T(8,128)(2,1)S(1)}, bf16[192,512]{1,0:T(8,128)(2,1)S(1)}, u32[]{:S(2)}, u32[]{:S(2)}) collective-permute-start(bf16[192,512]{1,0:T(8,128)(2,1)S(1)} %slice.14), channel_id=1, source_target_pairs={{0,7},{1,0},{2,1},{3,2},{4,3},{5,4},{6,5},{7,6},{8,15},{9,8},{10,9... | collective-permute-start | bytes 589832 | tf_op jit(solution)/shard_map/ppermute | solution.py:61
  25.0 4.5 %collective-permute-done.3 = bf16[192,512]{1,0:T(8,128)(2,1)S(1)} collective-permute-done((bf16[192,512]{1,0:T(8,128)(2,1)S(1)}, bf16[192,512]{1,0:T(8,128)(2,1)S(1)}, u32[]{:S(2)}, u32[]{:S(2)}) %collective-permute-start.3) | collective-permute-done | bytes 196640 | tf_op jit(solution)/shard_map/ppermute | solution.py:58
  29.5 2.7 %collective-permute-start.1 = (bf16[192,512]{1,0:T(8,128)(2,1)S(1)}, bf16[192,512]{1,0:T(8,128)(2,1)S(1)}, u32[]{:S(2)}, u32[]{:S(2)}) collective-permute-start(bf16[192,512]{1,0:T(8,128)(2,1)S(1)} %collective-permute-done), channel_id=1, source_target_pairs={{0,7},{1,0},{2,1},{3,2},{4,3},{5,4},{6,5},{7,6},{8,15},{9,8},{10,9... | collective-permute-start | bytes 589832 | tf_op jit(solution)/shard_map/ppermute | solution.py:61
  32.2 3.7 %collective-permute-done.4 = bf16[192,512]{1,0:T(8,128)(2,1)S(1)} collective-permute-done((bf16[192,512]{1,0:T(8,128)(2,1)S(1)}, bf16[192,512]{1,0:T(8,128)(2,1)S(1)}, u32[]{:S(2)}, u32[]{:S(2)}) %collective-permute-start.4) | collective-permute-done | bytes 196640 | tf_op jit(solution)/shard_map/ppermute | solution.py:58
  35.9 4.0 %collective-permute-done.1 = bf16[192,512]{1,0:T(8,128)(2,1)S(1)} collective-permute-done((bf16[192,512]{1,0:T(8,128)(2,1)S(1)}, bf16[192,512]{1,0:T(8,128)(2,1)S(1)}, u32[]{:S(2)}, u32[]{:S(2)}) %collective-permute-start.1) | collective-permute-done | bytes 196640 | tf_op jit(solution)/shard_map/ppermute | solution.py:61
  39.9 3.5 %collective-permute-start.2 = (bf16[192,512]{1,0:T(8,128)(2,1)S(1)}, bf16[192,512]{1,0:T(8,128)(2,1)S(1)}, u32[]{:S(2)}, u32[]{:S(2)}) collective-permute-start(bf16[192,512]{1,0:T(8,128)(2,1)S(1)} %collective-permute-done.1), channel_id=1, source_target_pairs={{0,7},{1,0},{2,1},{3,2},{4,3},{5,4},{6,5},{7,6},{8,15},{9,8},{10,9... | collective-permute-start | bytes 589832 | tf_op jit(solution)/shard_map/ppermute | solution.py:61
  43.4 3.4 %collective-permute-done.5 = bf16[192,512]{1,0:T(8,128)(2,1)S(1)} collective-permute-done((bf16[192,512]{1,0:T(8,128)(2,1)S(1)}, bf16[192,512]{1,0:T(8,128)(2,1)S(1)}, u32[]{:S(2)}, u32[]{:S(2)}) %collective-permute-start.5) | collective-permute-done | bytes 196640 | tf_op jit(solution)/shard_map/ppermute | solution.py:58
  47.7 3.8 %collective-permute-done.2 = bf16[192,512]{1,0:T(8,128)(2,1)S(1)} collective-permute-done((bf16[192,512]{1,0:T(8,128)(2,1)S(1)}, bf16[192,512]{1,0:T(8,128)(2,1)S(1)}, u32[]{:S(2)}, u32[]{:S(2)}) %collective-permute-start.2) | collective-permute-done | bytes 196640 | tf_op jit(solution)/shard_map/ppermute | solution.py:61
  51.5 6.2 %collective-permute-done.6 = bf16[192,512]{1,0:T(8,128)(2,1)S(1)} collective-permute-done((bf16[192,512]{1,0:T(8,128)(2,1)S(1)}, bf16[192,512]{1,0:T(8,128)(2,1)S(1)}, u32[]{:S(2)}, u32[]{:S(2)}) %collective-permute-start.6) | collective-permute-done | bytes 196640 | tf_op jit(solution)/shard_map/ppermute | solution.py:58
  57.7 23.8 %reduce-scatter.2.cloned.1.call-done = bf16[16,16,896]{2,1,0:T(8,128)(2,1)} async-done(((bf16[16,128,896]{2,1,0:T(8,128)(2,1)}), bf16[16,16,896]{2,1,0:T(8,128)(2,1)}) %reduce-scatter.2.cloned.1.call-update) | async-done | bytes 458768 | tf_op jit(solution)/shard_map/reduce_scatter | solution.py:112
  82.8 7.6 %all-to-all-start = ((s32[32,1,2]{2,1,0:T(1,128)}), s32[32,1,2]{2,1,0:T(1,128)S(1)}, u32[]{:S(2)}, u32[]{:S(2)}) async-start(s32[32,1,2]{2,1,0:T(1,128)} %bitcast.2), calls=%async_computation.1 | async-start | bytes 32768 | tf_op jit(solution)/shard_map/all_to_all | solution.py:121
  90.5 5.8 %convert_element_type.41 = f32[16,128,896]{2,1,0:T(8,128)} convert(bf16[16,128,896]{2,1,0:T(8,128)(2,1)} %param.10) | non-fusion elementwise | flops 1835008 | bytes 11010048 | tf_op jit(solution)/shard_map/convert_element_type | solution.py:99
  97.7 1.3 add_convert_fusion
  98.9 2.0 gather_fusion
  100.9 6.4 %all-to-all-start.1 = ((bf16[32,2,16,896]{3,2,1,0:T(8,128)(2,1)}), bf16[32,2,16,896]{3,2,1,0:T(8,128)(2,1)S(1)}, u32[]{:S(2)}, u32[]{:S(2)}) async-start(bf16[32,2,16,896]{3,2,1,0:T(8,128)(2,1)} %bitcast.4), calls=%async_computation.2 | async-start | bytes 3670016 | tf_op jit(solution)/shard_map/all_to_all | solution.py:122
  107.7 25.2 %all-to-all-done.1 = bf16[32,2,16,896]{3,2,1,0:T(8,128)(2,1)S(1)} async-done(((bf16[32,2,16,896]{3,2,1,0:T(8,128)(2,1)}), bf16[32,2,16,896]{3,2,1,0:T(8,128)(2,1)S(1)}, u32[]{:S(2)}, u32[]{:S(2)}) %all-to-all-start.1) | async-done | bytes 1835040 | tf_op jit(solution)/shard_map/all_to_all | solution.py:122
  132.8 1.5 gather_fusion.1
  134.5 1.5 fusion.48
  136.0 1.4 fusion.50
  137.4 1.4 fusion.52
  138.8 1.3 fusion.54
  141.3 5.8 %fusion.77 = f32[513,512]{1,0:T(8,128)S(1)} fusion(bf16[513,4096]{1,0:T(8,128)(2,1)} %all-gather.4.cloned.1.call-done, bf16[4096,512]{1,0:T(8,128)(2,1)} %param.13), kind=kOutput, calls=%fused_computation.107 | convolution fusion | flops 2151677952 | bytes 9447424 | tf_op jit(solution)/shard_map/dot_general | solution.py:132
  148.5 1.7 reshape.246
  151.1 1.7 fusion.47
  152.9 52.7 %all-gather.6.cloned.1.call-done = bf16[24,128,896]{2,1,0:T(8,128)(2,1)} async-done(((bf16[24,16,896]{2,1,0:T(8,128)(2,1)}), bf16[24,128,896]{2,1,0:T(8,128)(2,1)}) %all-gather.6.cloned.1.call-update) | async-done | bytes 5505040 | tf_op jit(solution)/shard_map/all_gather | solution.py:126
  205.7 6.9 %fusion = (f32[4,3072]{1,0:T(4,128)S(1)}, f32[3072,4,128]{2,0,1:T(8,128)S(1)}) fusion(bf16[3072,896,1]{1,0,2:T(8,128)(2,1)} %bitcast.79, bf16[896,512]{1,0:T(8,128)(2,1)S(1)} %copy-done), kind=kOutput, calls=%fused_computation.6 | convolution fusion | flops 2821705728 | bytes 12763136 | tf_op jit(solution)/shard_map/ke,ehd->hkd/dot_general | solution.py:140
  212.6 3.6 %convolution_convert_fusion = bf16[3072,4,128]{2,0,1:T(8,128)(2,1)S(1)} fusion(bf16[3072,896,1]{1,0,2:T(8,128)(2,1)S(1)} %bitcast.80, bf16[896,512]{1,0:T(8,128)(2,1)S(1)} %copy-done.13), kind=kOutput, calls=%fused_computation.9 | convolution fusion | flops 2820145152 | bytes 9568256 | tf_op jit(solution)/shard_map/ke,ehd->hkd/dot_general | solution.py:147
  216.2 1.9 fusion.1
  218.2 1.3 fusion.15
  (77 shorter events, 11.6 us)
Async XLA Ops:
  6.5 199.1 %copy-start = (bf16[896,512]{1,0:T(8,128)(2,1)S(1)}, bf16[896,512]{1,0:T(8,128)(2,1)}, u32[]{:S(2)}) copy-start(bf16[896,512]{1,0:T(8,128)(2,1)} %param.14) | copy-start | bytes 2752516
  6.5 3.0 %copy-start.15 = (bf16[896,448]{0,1:T(8,128)(2,1)S(1)}, bf16[896,448]{0,1:T(8,128)(2,1)}, u32[]{:S(2)}) copy-start(bf16[896,448]{0,1:T(8,128)(2,1)} %param.11) | copy-start | bytes 2408452
  6.5 3.0 %copy-start.14 = (bf16[448,896]{1,0:T(8,128)(2,1)S(1)}, bf16[448,896]{1,0:T(8,128)(2,1)}, u32[]{:S(2)}) copy-start(bf16[448,896]{1,0:T(8,128)(2,1)} %param.12) | copy-start | bytes 2408452
  6.5 74.9 %reduce-scatter.2.cloned.1.call-start = ((), (), s32[]{:S(2)}) async-start(), calls=%async_computation.3 | async-start | bytes 4128768 | tf_op jit(solution)/shard_map/reduce_scatter | solution.py:112
  17.3 1.1 copy-start.3
  17.3 64.3 %copy-start.11 = (s32[12,2]{0,1:T(2,128)S(1)}, s32[12,2]{0,1:T(2,128)}, u32[]{:S(2)}) copy-start(s32[12,2]{0,1:T(2,128)} %param.9) | copy-start | bytes 292
  17.3 124.1 %all-gather.4.cloned.1.call-start = ((), (), s32[]{:S(2)}) async-start(), calls=%async_computation.4 | async-start | bytes 4792320 | tf_op jit(solution)/shard_map/all_gather | solution.py:128
  18.4 11.1 %collective-permute-start.3 = (bf16[192,512]{1,0:T(8,128)(2,1)S(1)}, bf16[192,512]{1,0:T(8,128)(2,1)S(1)}, u32[]{:S(2)}, u32[]{:S(2)}) collective-permute-start(bf16[192,512]{1,0:T(8,128)(2,1)S(1)} %slice.14), channel_id=1, source_target_pairs={{0,1},{1,2},{2,3},{3,4},{4,5},{5,6},{6,7},{7,0},{8,9},{9,10},{10,1... | collective-permute-start | bytes 589832 | tf_op jit(solution)/shard_map/ppermute | solution.py:58
  21.0 8.6 %collective-permute-start = (bf16[192,512]{1,0:T(8,128)(2,1)S(1)}, bf16[192,512]{1,0:T(8,128)(2,1)S(1)}, u32[]{:S(2)}, u32[]{:S(2)}) collective-permute-start(bf16[192,512]{1,0:T(8,128)(2,1)S(1)} %slice.14), channel_id=1, source_target_pairs={{0,7},{1,0},{2,1},{3,2},{4,3},{5,4},{6,5},{7,6},{8,15},{9,8},{10,9... | collective-permute-start | bytes 589832 | tf_op jit(solution)/shard_map/ppermute | solution.py:61
  29.5 6.4 %collective-permute-start.4 = (bf16[192,512]{1,0:T(8,128)(2,1)S(1)}, bf16[192,512]{1,0:T(8,128)(2,1)S(1)}, u32[]{:S(2)}, u32[]{:S(2)}) collective-permute-start(bf16[192,512]{1,0:T(8,128)(2,1)S(1)} %collective-permute-done.3), channel_id=1, source_target_pairs={{0,1},{1,2},{2,3},{3,4},{4,5},{5,6},{6,7},{7,0},{8,9},{9,10},{10,1... | collective-permute-start | bytes 589832 | tf_op jit(solution)/shard_map/ppermute | solution.py:58
  29.5 10.4 %collective-permute-start.1 = (bf16[192,512]{1,0:T(8,128)(2,1)S(1)}, bf16[192,512]{1,0:T(8,128)(2,1)S(1)}, u32[]{:S(2)}, u32[]{:S(2)}) collective-permute-start(bf16[192,512]{1,0:T(8,128)(2,1)S(1)} %collective-permute-done), channel_id=1, source_target_pairs={{0,7},{1,0},{2,1},{3,2},{4,3},{5,4},{6,5},{7,6},{8,15},{9,8},{10,9... | collective-permute-start | bytes 589832 | tf_op jit(solution)/shard_map/ppermute | solution.py:61
  35.9 54.5 %copy-start.5 = (bf16[192,512]{1,0:T(8,128)(2,1)}, bf16[192,512]{1,0:T(8,128)(2,1)S(1)}, u32[]{:S(2)}) copy-start(bf16[192,512]{1,0:T(8,128)(2,1)S(1)} %collective-permute-done.4) | copy-start | bytes 589828
  35.9 10.8 %collective-permute-start.5 = (bf16[192,512]{1,0:T(8,128)(2,1)S(1)}, bf16[192,512]{1,0:T(8,128)(2,1)S(1)}, u32[]{:S(2)}, u32[]{:S(2)}) collective-permute-start(bf16[192,512]{1,0:T(8,128)(2,1)S(1)} %collective-permute-done.4), channel_id=1, source_target_pairs={{0,1},{1,2},{2,3},{3,4},{4,5},{5,6},{6,7},{7,0},{8,9},{9,10},{10,1... | collective-permute-start | bytes 589832 | tf_op jit(solution)/shard_map/ppermute | solution.py:58
  39.9 11.6 %collective-permute-start.2 = (bf16[192,512]{1,0:T(8,128)(2,1)S(1)}, bf16[192,512]{1,0:T(8,128)(2,1)S(1)}, u32[]{:S(2)}, u32[]{:S(2)}) collective-permute-start(bf16[192,512]{1,0:T(8,128)(2,1)S(1)} %collective-permute-done.1), channel_id=1, source_target_pairs={{0,7},{1,0},{2,1},{3,2},{4,3},{5,4},{6,5},{7,6},{8,15},{9,8},{10,9... | collective-permute-start | bytes 589832 | tf_op jit(solution)/shard_map/ppermute | solution.py:61
  46.8 49.5 %copy-start.6 = (bf16[192,512]{1,0:T(8,128)(2,1)}, bf16[192,512]{1,0:T(8,128)(2,1)S(1)}, u32[]{:S(2)}) copy-start(bf16[192,512]{1,0:T(8,128)(2,1)S(1)} %collective-permute-done.5) | copy-start | bytes 589828
  46.8 10.9 %collective-permute-start.6 = (bf16[192,512]{1,0:T(8,128)(2,1)S(1)}, bf16[192,512]{1,0:T(8,128)(2,1)S(1)}, u32[]{:S(2)}, u32[]{:S(2)}) collective-permute-start(bf16[192,512]{1,0:T(8,128)(2,1)S(1)} %collective-permute-done.5), channel_id=1, source_target_pairs={{0,1},{1,2},{2,3},{3,4},{4,5},{5,6},{6,7},{7,0},{8,9},{9,10},{10,1... | collective-permute-start | bytes 589832 | tf_op jit(solution)/shard_map/ppermute | solution.py:58
  51.5 44.8 %copy-start.7 = (bf16[192,512]{1,0:T(8,128)(2,1)}, bf16[192,512]{1,0:T(8,128)(2,1)S(1)}, u32[]{:S(2)}) copy-start(bf16[192,512]{1,0:T(8,128)(2,1)S(1)} %collective-permute-done.2) | copy-start | bytes 589828
  57.7 38.7 %copy-start.9 = (bf16[192,512]{1,0:T(8,128)(2,1)}, bf16[192,512]{1,0:T(8,128)(2,1)S(1)}, u32[]{:S(2)}) copy-start(bf16[192,512]{1,0:T(8,128)(2,1)S(1)} %collective-permute-done.6) | copy-start | bytes 589828
  82.8 14.5 %all-to-all-start = ((s32[32,1,2]{2,1,0:T(1,128)}), s32[32,1,2]{2,1,0:T(1,128)S(1)}, u32[]{:S(2)}, u32[]{:S(2)}) async-start(s32[32,1,2]{2,1,0:T(1,128)} %bitcast.2), calls=%async_computation.1 | async-start | bytes 32768 | tf_op jit(solution)/shard_map/all_to_all | solution.py:121
  90.5 7.2 %copy-start.4 = (bf16[16,16,896]{2,1,0:T(8,128)(2,1)S(1)}, bf16[16,16,896]{2,1,0:T(8,128)(2,1)}, u32[]{:S(2)}) copy-start(bf16[16,16,896]{2,1,0:T(8,128)(2,1)} %reduce-scatter.2.cloned.1.call-done) | copy-start | bytes 1376260
  100.9 31.9 %all-to-all-start.1 = ((bf16[32,2,16,896]{3,2,1,0:T(8,128)(2,1)}), bf16[32,2,16,896]{3,2,1,0:T(8,128)(2,1)S(1)}, u32[]{:S(2)}, u32[]{:S(2)}) async-start(bf16[32,2,16,896]{3,2,1,0:T(8,128)(2,1)} %bitcast.4), calls=%async_computation.2 | async-start | bytes 3670016 | tf_op jit(solution)/shard_map/all_to_all | solution.py:122
  107.3 98.3 %all-gather.6.cloned.1.call-start = ((), (), s32[]{:S(2)}) async-start(), calls=%async_computation.5 | async-start | bytes 6193152 | tf_op jit(solution)/shard_map/all_gather | solution.py:126
  134.3 4.5 %copy-start.10 = (bf16[192,512]{1,0:T(8,128)(2,1)S(1)}, bf16[192,512]{1,0:T(8,128)(2,1)}, u32[]{:S(2)}) copy-start(bf16[192,512]{1,0:T(8,128)(2,1)} %copy-done.9) | copy-start | bytes 589828
  134.3 5.8 %copy-start.8 = (bf16[192,512]{1,0:T(8,128)(2,1)S(1)}, bf16[192,512]{1,0:T(8,128)(2,1)}, u32[]{:S(2)}) copy-start(bf16[192,512]{1,0:T(8,128)(2,1)} %copy-done.7) | copy-start | bytes 589828
  134.5 5.7 %copy-start.2 = (bf16[4096,512]{1,0:T(8,128)(2,1)S(1)}, bf16[4096,512]{1,0:T(8,128)(2,1)}, u32[]{:S(2)}) copy-start(bf16[4096,512]{1,0:T(8,128)(2,1)} %param.13) | copy-start | bytes 12582916
  205.7 6.9 %copy-start.12 = (bf16[24,128,896]{2,1,0:T(8,128)(2,1)S(1)}, bf16[24,128,896]{2,1,0:T(8,128)(2,1)}, u32[]{:S(2)}) copy-start(bf16[24,128,896]{2,1,0:T(8,128)(2,1)} %all-gather.6.cloned.1.call-done) | copy-start | bytes 16515076
  205.7 6.9 %copy-start.13 = (bf16[896,512]{1,0:T(8,128)(2,1)S(1)}, bf16[896,512]{1,0:T(8,128)(2,1)}, u32[]{:S(2)}) copy-start(bf16[896,512]{1,0:T(8,128)(2,1)} %param.15) | copy-start | bytes 2752516
  219.5 3.0 %copy-start.1 = (bf16[896,512]{1,0:T(8,128)(2,1)S(1)}, bf16[896,512]{1,0:T(8,128)(2,1)}, u32[]{:S(2)}) copy-start(bf16[896,512]{1,0:T(8,128)(2,1)} %param.14) | copy-start | bytes 2752516
Sparse Core Ops, SparseCore 0:
  17.4 64.0 reduce-scatter.1
  83.3 54.8 all-gather.3
  139.9 65.6 all-gather.5

commit v12 on v11

--- a/solution.py
+++ b/solution.py
@@ -105,7 +105,7 @@
     partial = jnp.einsum("btf,fe->bte", active, w_down, preferred_element_type=jnp.float32)
     rows_here = block_tokens // tensor_count
     states = hidden_states[SPAN - 1 :]
-    head_rows = 3 * SPAN
+    head_rows = 4 * SPAN
     head_got = {0: states[:head_rows]}
     for step in ring_hops(states[:head_rows], tensor_count):
         head_got.update(step)

time: 229 us -> 230 us (level)
    ppermute x4, waiting for transfers between devices: 17.8 us -> 33 us  [ring_hops(): going_right = lax.ppermute(going_right, 'tensor', to_right)]
    reduce_scatter x1, waiting for transfers between devices: 23.8 us -> 18.2 us  [shards(): lax.psum_scatter(partial.astype(jnp.bfloat16), 'tensor', scatter_dimensio...]
    all_gather x1, waiting for transfers between devices: 52.7 us -> 48 us  [shards(): encoded = lax.all_gather(mine, 'tensor', axis=1, tiled=True)]
    ppermute x3, waiting for transfers between devices: 7.73 us -> 3.84 us  [ring_hops(): going_left = lax.ppermute(going_left, 'tensor', to_left)]
where the time goes in v12:
time: 230 us
  waiting for transfers between devices  129 us (56%)
  matrix products  33.3 us (14%)
  starting transfers between devices  27 us (12%)
  other arithmetic  16 us (7%)
  between operations  13.6 us (6%)
  local copies, waits for them, and re-layouts  10.6 us (5%)
    all_gather x1, waiting for transfers between devices, shards(): encoded = lax.all_gather(mine, 'tensor', axis=1, tiled=True)  48 us
    ppermute x4, waiting for transfers between devices, ring_hops(): going_right = lax.ppermute(going_right, 'tensor', to_right)  33 us
    all_to_all x1, waiting for transfers between devices, shards(): lax.all_to_all(encoded_own[asked], 'dp', split_axis=0, concat_axis=0, til...  25.2 us
    reduce_scatter x1, waiting for transfers between devices, shards(): lax.psum_scatter(partial.astype(jnp.bfloat16), 'tensor', scatter_dimensio...  18.2 us
    ppermute x3, starting transfers between devices, ring_hops(): going_left = lax.ppermute(going_left, 'tensor', to_left)  10.2 us
    dot_general x1, matrix products, shards(): jnp.einsum('btf,fe->bte', active, w_down, preferred_element_type=jnp.floa...  7.69 us
    all_to_all x1, starting transfers between devices, shards(): lax.all_to_all(requests, 'dp', split_axis=0, concat_axis=0, tiled=True)  7.53 us
    dot_general x8, matrix products, ring_query(): term = jnp.dot(got[offset], rows, preferred_element_type=jnp.float32)  6.98 us
  transfers between devices with their start and end apart: 12, of which 10 were waited for; matrix products, arithmetic and copies ran while one was open for 13% of the time, Pallas kernels for 0%

profile of v12, /device:TPU:1, one launch (start us, length us, event | category | flops | bytes accessed | tf_op | source)
XLA Modules:
  0.0 229.7 jit_solution(17215782379591059361)
XLA Ops:
  6.5 3.0 %multiply_reduce_fusion = f32[16,128]{1,0:T(8,128)S(1)} fusion(bf16[16,128,896]{2,1,0:T(8,128)(2,1)} %param.10), kind=kLoop, calls=%fused_computation.3 | loop fusion | flops 5502976 | bytes 3678208 | tf_op jit(solution)/shard_map/reduce_sum | solution.py:101
  9.6 7.7 %convolution_convert_fusion.1 = bf16[16,128,896]{2,1,0:T(8,128)(2,1)} fusion(f32[16,128]{1,0:T(8,128)S(1)} %add_rsqrt_fusion.2, bf16[16,128,896]{2,1,0:T(8,128)(2,1)} %param.10, bf16[448,896]{1,0:T(8,128)(2,1)S(1)} %copy-done.15, bf16[896,448]{0,1:T(8,128)(2,1)S(1)} %copy-done.16), kind=kOutput, calls=%fused_computation.26 | convolution fusion | flops 3303931904 | bytes 8953856 | tf_op jit(solution)/shard_map/btf,fe->bte/dot_general | solution.py:105
  18.4 2.5 %collective-permute-start.3 = (bf16[256,512]{1,0:T(8,128)(2,1)S(1)}, bf16[256,512]{1,0:T(8,128)(2,1)S(1)}, u32[]{:S(2)}, u32[]{:S(2)}) collective-permute-start(bf16[256,512]{1,0:T(8,128)(2,1)S(1)} %slice.14), channel_id=1, source_target_pairs={{0,1},{1,2},{2,3},{3,4},{4,5},{5,6},{6,7},{7,0},{8,9},{9,10},{10,1... | collective-permute-start | bytes 786440 | tf_op jit(solution)/shard_map/ppermute | solution.py:58
  21.0 4.0 %collective-permute-start = (bf16[256,512]{1,0:T(8,128)(2,1)S(1)}, bf16[256,512]{1,0:T(8,128)(2,1)S(1)}, u32[]{:S(2)}, u32[]{:S(2)}) collective-permute-start(bf16[256,512]{1,0:T(8,128)(2,1)S(1)} %slice.14), channel_id=1, source_target_pairs={{0,7},{1,0},{2,1},{3,2},{4,3},{5,4},{6,5},{7,6},{8,15},{9,8},{10,9... | collective-permute-start | bytes 786440 | tf_op jit(solution)/shard_map/ppermute | solution.py:61
  25.0 5.9 %collective-permute-done.3 = bf16[256,512]{1,0:T(8,128)(2,1)S(1)} collective-permute-done((bf16[256,512]{1,0:T(8,128)(2,1)S(1)}, bf16[256,512]{1,0:T(8,128)(2,1)S(1)}, u32[]{:S(2)}, u32[]{:S(2)}) %collective-permute-start.3) | collective-permute-done | bytes 262176 | tf_op jit(solution)/shard_map/ppermute | solution.py:58
  30.9 2.7 %collective-permute-start.1 = (bf16[256,512]{1,0:T(8,128)(2,1)S(1)}, bf16[256,512]{1,0:T(8,128)(2,1)S(1)}, u32[]{:S(2)}, u32[]{:S(2)}) collective-permute-start(bf16[256,512]{1,0:T(8,128)(2,1)S(1)} %collective-permute-done), channel_id=1, source_target_pairs={{0,7},{1,0},{2,1},{3,2},{4,3},{5,4},{6,5},{7,6},{8,15},{9,8},{10,9... | collective-permute-start | bytes 786440 | tf_op jit(solution)/shard_map/ppermute | solution.py:61
  33.6 8.0 %collective-permute-done.4 = bf16[256,512]{1,0:T(8,128)(2,1)S(1)} collective-permute-done((bf16[256,512]{1,0:T(8,128)(2,1)S(1)}, bf16[256,512]{1,0:T(8,128)(2,1)S(1)}, u32[]{:S(2)}, u32[]{:S(2)}) %collective-permute-start.4) | collective-permute-done | bytes 262176 | tf_op jit(solution)/shard_map/ppermute | solution.py:58
  41.7 2.5 %collective-permute-done.1 = bf16[256,512]{1,0:T(8,128)(2,1)S(1)} collective-permute-done((bf16[256,512]{1,0:T(8,128)(2,1)S(1)}, bf16[256,512]{1,0:T(8,128)(2,1)S(1)}, u32[]{:S(2)}, u32[]{:S(2)}) %collective-permute-start.1) | collective-permute-done | bytes 262176 | tf_op jit(solution)/shard_map/ppermute | solution.py:61
  44.1 3.5 %collective-permute-start.2 = (bf16[256,512]{1,0:T(8,128)(2,1)S(1)}, bf16[256,512]{1,0:T(8,128)(2,1)S(1)}, u32[]{:S(2)}, u32[]{:S(2)}) collective-permute-start(bf16[256,512]{1,0:T(8,128)(2,1)S(1)} %collective-permute-done.1), channel_id=1, source_target_pairs={{0,7},{1,0},{2,1},{3,2},{4,3},{5,4},{6,5},{7,6},{8,15},{9,8},{10,9... | collective-permute-start | bytes 786440 | tf_op jit(solution)/shard_map/ppermute | solution.py:61
  47.6 7.6 %collective-permute-done.5 = bf16[256,512]{1,0:T(8,128)(2,1)S(1)} collective-permute-done((bf16[256,512]{1,0:T(8,128)(2,1)S(1)}, bf16[256,512]{1,0:T(8,128)(2,1)S(1)}, u32[]{:S(2)}, u32[]{:S(2)}) %collective-permute-start.5) | collective-permute-done | bytes 262176 | tf_op jit(solution)/shard_map/ppermute | solution.py:58
  56.2 1.4 collective-permute-done.2
  57.6 11.4 %collective-permute-done.6 = bf16[256,512]{1,0:T(8,128)(2,1)} collective-permute-done((bf16[256,512]{1,0:T(8,128)(2,1)S(1)}, bf16[256,512]{1,0:T(8,128)(2,1)}, u32[]{:S(2)}, u32[]{:S(2)}) %collective-permute-start.6) | collective-permute-done | bytes 262176 | tf_op jit(solution)/shard_map/ppermute | solution.py:58
  69.0 18.2 %reduce-scatter.2.cloned.1.call-done = bf16[16,16,896]{2,1,0:T(8,128)(2,1)} async-done(((bf16[16,128,896]{2,1,0:T(8,128)(2,1)}), bf16[16,16,896]{2,1,0:T(8,128)(2,1)}) %reduce-scatter.2.cloned.1.call-update) | async-done | bytes 458768 | tf_op jit(solution)/shard_map/reduce_scatter | solution.py:112
  88.5 7.5 %all-to-all-start = ((s32[32,1,2]{2,1,0:T(1,128)}), s32[32,1,2]{2,1,0:T(1,128)S(1)}, u32[]{:S(2)}, u32[]{:S(2)}) async-start(s32[32,1,2]{2,1,0:T(1,128)} %bitcast.2), calls=%async_computation.1 | async-start | bytes 32768 | tf_op jit(solution)/shard_map/all_to_all | solution.py:121
  96.1 5.8 %convert_element_type.41 = f32[16,128,896]{2,1,0:T(8,128)} convert(bf16[16,128,896]{2,1,0:T(8,128)(2,1)} %param.10) | non-fusion elementwise | flops 1835008 | bytes 11010048 | tf_op jit(solution)/shard_map/convert_element_type | solution.py:99
  103.3 1.3 add_convert_fusion
  104.6 2.0 gather_fusion
  106.6 6.4 %all-to-all-start.1 = ((bf16[32,2,16,896]{3,2,1,0:T(8,128)(2,1)}), bf16[32,2,16,896]{3,2,1,0:T(8,128)(2,1)S(1)}, u32[]{:S(2)}, u32[]{:S(2)}) async-start(bf16[32,2,16,896]{3,2,1,0:T(8,128)(2,1)} %bitcast.4), calls=%async_computation.2 | async-start | bytes 3670016 | tf_op jit(solution)/shard_map/all_to_all | solution.py:122
  113.3 25.2 %all-to-all-done.1 = bf16[32,2,16,896]{3,2,1,0:T(8,128)(2,1)S(1)} async-done(((bf16[32,2,16,896]{3,2,1,0:T(8,128)(2,1)}), bf16[32,2,16,896]{3,2,1,0:T(8,128)(2,1)S(1)}, u32[]{:S(2)}, u32[]{:S(2)}) %all-to-all-start.1) | async-done | bytes 1835040 | tf_op jit(solution)/shard_map/all_to_all | solution.py:122
  138.5 1.5 gather_fusion.1
  140.1 1.5 fusion.48
  141.6 1.4 fusion.50
  143.0 1.3 fusion.52
  144.4 1.4 fusion.54
  147.2 5.4 %fusion.77 = f32[449,512]{1,0:T(8,128)S(1)} fusion(bf16[449,4096]{1,0:T(8,128)(2,1)} %all-gather.4.cloned.1.call-done, bf16[4096,512]{1,0:T(8,128)(2,1)} %param.13), kind=kOutput, calls=%fused_computation.107 | convolution fusion | flops 1883242496 | bytes 8792064 | tf_op jit(solution)/shard_map/dot_general | solution.py:132
  153.9 1.7 reshape.246
  156.5 1.7 fusion.47
  158.4 48.0 %all-gather.6.cloned.1.call-done = bf16[24,128,896]{2,1,0:T(8,128)(2,1)} async-done(((bf16[24,16,896]{2,1,0:T(8,128)(2,1)}), bf16[24,128,896]{2,1,0:T(8,128)(2,1)}) %all-gather.6.cloned.1.call-update) | async-done | bytes 5505040 | tf_op jit(solution)/shard_map/all_gather | solution.py:126
  206.4 6.9 %fusion = (f32[4,3072]{1,0:T(4,128)S(1)}, f32[3072,4,128]{2,0,1:T(8,128)S(1)}) fusion(bf16[3072,896,1]{1,0,2:T(8,128)(2,1)} %bitcast.79, bf16[896,512]{1,0:T(8,128)(2,1)S(1)} %copy-done), kind=kOutput, calls=%fused_computation.6 | convolution fusion | flops 2821705728 | bytes 12763136 | tf_op jit(solution)/shard_map/ke,ehd->hkd/dot_general | solution.py:140
  213.3 3.6 %convolution_convert_fusion = bf16[3072,4,128]{2,0,1:T(8,128)(2,1)S(1)} fusion(bf16[3072,896,1]{1,0,2:T(8,128)(2,1)S(1)} %bitcast.80, bf16[896,512]{1,0:T(8,128)(2,1)S(1)} %copy-done.14), kind=kOutput, calls=%fused_computation.9 | convolution fusion | flops 2820145152 | bytes 9568256 | tf_op jit(solution)/shard_map/ke,ehd->hkd/dot_general | solution.py:147
  216.9 1.9 fusion.1
  218.9 1.3 fusion.15
  (79 shorter events, 11.8 us)
Async XLA Ops:
  6.5 199.8 %copy-start = (bf16[896,512]{1,0:T(8,128)(2,1)S(1)}, bf16[896,512]{1,0:T(8,128)(2,1)}, u32[]{:S(2)}) copy-start(bf16[896,512]{1,0:T(8,128)(2,1)} %param.14) | copy-start | bytes 2752516
  6.5 3.0 %copy-start.16 = (bf16[896,448]{0,1:T(8,128)(2,1)S(1)}, bf16[896,448]{0,1:T(8,128)(2,1)}, u32[]{:S(2)}) copy-start(bf16[896,448]{0,1:T(8,128)(2,1)} %param.11) | copy-start | bytes 2408452
  6.5 3.0 %copy-start.15 = (bf16[448,896]{1,0:T(8,128)(2,1)S(1)}, bf16[448,896]{1,0:T(8,128)(2,1)}, u32[]{:S(2)}) copy-start(bf16[448,896]{1,0:T(8,128)(2,1)} %param.12) | copy-start | bytes 2408452
  6.5 80.6 %reduce-scatter.2.cloned.1.call-start = ((), (), s32[]{:S(2)}) async-start(), calls=%async_computation.3 | async-start | bytes 4128768 | tf_op jit(solution)/shard_map/reduce_scatter | solution.py:112
  17.2 1.1 copy-start.3
  17.2 69.9 %copy-start.12 = (s32[12,2]{0,1:T(2,128)S(1)}, s32[12,2]{0,1:T(2,128)}, u32[]{:S(2)}) copy-start(s32[12,2]{0,1:T(2,128)} %param.9) | copy-start | bytes 292
  17.3 129.9 %all-gather.4.cloned.1.call-start = ((), (), s32[]{:S(2)}) async-start(), calls=%async_computation.4 | async-start | bytes 4202496 | tf_op jit(solution)/shard_map/all_gather | solution.py:128
  18.4 12.5 %collective-permute-start.3 = (bf16[256,512]{1,0:T(8,128)(2,1)S(1)}, bf16[256,512]{1,0:T(8,128)(2,1)S(1)}, u32[]{:S(2)}, u32[]{:S(2)}) collective-permute-start(bf16[256,512]{1,0:T(8,128)(2,1)S(1)} %slice.14), channel_id=1, source_target_pairs={{0,1},{1,2},{2,3},{3,4},{4,5},{5,6},{6,7},{7,0},{8,9},{9,10},{10,1... | collective-permute-start | bytes 786440 | tf_op jit(solution)/shard_map/ppermute | solution.py:58
  21.0 10.0 %collective-permute-start = (bf16[256,512]{1,0:T(8,128)(2,1)S(1)}, bf16[256,512]{1,0:T(8,128)(2,1)S(1)}, u32[]{:S(2)}, u32[]{:S(2)}) collective-permute-start(bf16[256,512]{1,0:T(8,128)(2,1)S(1)} %slice.14), channel_id=1, source_target_pairs={{0,7},{1,0},{2,1},{3,2},{4,3},{5,4},{6,5},{7,6},{8,15},{9,8},{10,9... | collective-permute-start | bytes 786440 | tf_op jit(solution)/shard_map/ppermute | solution.py:61
  30.9 10.7 %collective-permute-start.4 = (bf16[256,512]{1,0:T(8,128)(2,1)S(1)}, bf16[256,512]{1,0:T(8,128)(2,1)S(1)}, u32[]{:S(2)}, u32[]{:S(2)}) collective-permute-start(bf16[256,512]{1,0:T(8,128)(2,1)S(1)} %collective-permute-done.3), channel_id=1, source_target_pairs={{0,1},{1,2},{2,3},{3,4},{4,5},{5,6},{6,7},{7,0},{8,9},{9,10},{10,1... | collective-permute-start | bytes 786440 | tf_op jit(solution)/shard_map/ppermute | solution.py:58
  30.9 13.2 %collective-permute-start.1 = (bf16[256,512]{1,0:T(8,128)(2,1)S(1)}, bf16[256,512]{1,0:T(8,128)(2,1)S(1)}, u32[]{:S(2)}, u32[]{:S(2)}) collective-permute-start(bf16[256,512]{1,0:T(8,128)(2,1)S(1)} %collective-permute-done), channel_id=1, source_target_pairs={{0,7},{1,0},{2,1},{3,2},{4,3},{5,4},{6,5},{7,6},{8,15},{9,8},{10,9... | collective-permute-start | bytes 786440 | tf_op jit(solution)/shard_map/ppermute | solution.py:61
  41.6 60.3 %copy-start.7 = (bf16[256,512]{1,0:T(8,128)(2,1)}, bf16[256,512]{1,0:T(8,128)(2,1)S(1)}, u32[]{:S(2)}) copy-start(bf16[256,512]{1,0:T(8,128)(2,1)S(1)} %collective-permute-done.4) | copy-start | bytes 786436
  41.6 13.7 %collective-permute-start.5 = (bf16[256,512]{1,0:T(8,128)(2,1)S(1)}, bf16[256,512]{1,0:T(8,128)(2,1)S(1)}, u32[]{:S(2)}, u32[]{:S(2)}) collective-permute-start(bf16[256,512]{1,0:T(8,128)(2,1)S(1)} %collective-permute-done.4), channel_id=1, source_target_pairs={{0,1},{1,2},{2,3},{3,4},{4,5},{5,6},{6,7},{7,0},{8,9},{9,10},{10,1... | collective-permute-start | bytes 786440 | tf_op jit(solution)/shard_map/ppermute | solution.py:58
  44.1 52.0 %copy-start.5 = (bf16[256,512]{1,0:T(8,128)(2,1)}, bf16[256,512]{1,0:T(8,128)(2,1)S(1)}, u32[]{:S(2)}) copy-start(bf16[256,512]{1,0:T(8,128)(2,1)S(1)} %collective-permute-done.1) | copy-start | bytes 786436
  44.1 13.4 %collective-permute-start.2 = (bf16[256,512]{1,0:T(8,128)(2,1)S(1)}, bf16[256,512]{1,0:T(8,128)(2,1)S(1)}, u32[]{:S(2)}, u32[]{:S(2)}) collective-permute-start(bf16[256,512]{1,0:T(8,128)(2,1)S(1)} %collective-permute-done.1), channel_id=1, source_target_pairs={{0,7},{1,0},{2,1},{3,2},{4,3},{5,4},{6,5},{7,6},{8,15},{9,8},{10,9... | collective-permute-start | bytes 786440 | tf_op jit(solution)/shard_map/ppermute | solution.py:61
  55.3 46.7 %copy-start.8 = (bf16[256,512]{1,0:T(8,128)(2,1)}, bf16[256,512]{1,0:T(8,128)(2,1)S(1)}, u32[]{:S(2)}) copy-start(bf16[256,512]{1,0:T(8,128)(2,1)S(1)} %collective-permute-done.5) | copy-start | bytes 786436
  55.3 13.7 %collective-permute-start.6 = (bf16[256,512]{1,0:T(8,128)(2,1)S(1)}, bf16[256,512]{1,0:T(8,128)(2,1)}, u32[]{:S(2)}, u32[]{:S(2)}) collective-permute-start(bf16[256,512]{1,0:T(8,128)(2,1)S(1)} %collective-permute-done.5), channel_id=1, source_target_pairs={{0,1},{1,2},{2,3},{3,4},{4,5},{5,6},{6,7},{7,0},{8,9},{9,10},{10,1... | collective-permute-start | bytes 786440 | tf_op jit(solution)/shard_map/ppermute | solution.py:58
  57.6 44.4 %copy-start.10 = (bf16[256,512]{1,0:T(8,128)(2,1)}, bf16[256,512]{1,0:T(8,128)(2,1)S(1)}, u32[]{:S(2)}) copy-start(bf16[256,512]{1,0:T(8,128)(2,1)S(1)} %collective-permute-done.2) | copy-start | bytes 786436
  88.5 14.4 %all-to-all-start = ((s32[32,1,2]{2,1,0:T(1,128)}), s32[32,1,2]{2,1,0:T(1,128)S(1)}, u32[]{:S(2)}, u32[]{:S(2)}) async-start(s32[32,1,2]{2,1,0:T(1,128)} %bitcast.2), calls=%async_computation.1 | async-start | bytes 32768 | tf_op jit(solution)/shard_map/all_to_all | solution.py:121
  96.1 7.2 %copy-start.4 = (bf16[16,16,896]{2,1,0:T(8,128)(2,1)S(1)}, bf16[16,16,896]{2,1,0:T(8,128)(2,1)}, u32[]{:S(2)}) copy-start(bf16[16,16,896]{2,1,0:T(8,128)(2,1)} %reduce-scatter.2.cloned.1.call-done) | copy-start | bytes 1376260
  106.6 31.9 %all-to-all-start.1 = ((bf16[32,2,16,896]{3,2,1,0:T(8,128)(2,1)}), bf16[32,2,16,896]{3,2,1,0:T(8,128)(2,1)S(1)}, u32[]{:S(2)}, u32[]{:S(2)}) async-start(bf16[32,2,16,896]{3,2,1,0:T(8,128)(2,1)} %bitcast.4), calls=%async_computation.2 | async-start | bytes 3670016 | tf_op jit(solution)/shard_map/all_to_all | solution.py:122
  112.9 93.4 %all-gather.6.cloned.1.call-start = ((), (), s32[]{:S(2)}) async-start(), calls=%async_computation.5 | async-start | bytes 6193152 | tf_op jit(solution)/shard_map/all_gather | solution.py:126
  140.0 3.1 %copy-start.9 = (bf16[256,512]{1,0:T(8,128)(2,1)S(1)}, bf16[256,512]{1,0:T(8,128)(2,1)}, u32[]{:S(2)}) copy-start(bf16[256,512]{1,0:T(8,128)(2,1)} %copy-done.8) | copy-start | bytes 786436
  140.0 5.9 %copy-start.11 = (bf16[256,512]{1,0:T(8,128)(2,1)S(1)}, bf16[256,512]{1,0:T(8,128)(2,1)}, u32[]{:S(2)}) copy-start(bf16[256,512]{1,0:T(8,128)(2,1)} %copy-done.10) | copy-start | bytes 786436
  140.0 6.2 %copy-start.6 = (bf16[256,512]{1,0:T(8,128)(2,1)S(1)}, bf16[256,512]{1,0:T(8,128)(2,1)}, u32[]{:S(2)}) copy-start(bf16[256,512]{1,0:T(8,128)(2,1)} %copy-done.5) | copy-start | bytes 786436
  140.1 5.7 %copy-start.2 = (bf16[4096,512]{1,0:T(8,128)(2,1)S(1)}, bf16[4096,512]{1,0:T(8,128)(2,1)}, u32[]{:S(2)}) copy-start(bf16[4096,512]{1,0:T(8,128)(2,1)} %param.13) | copy-start | bytes 12582916
  206.4 6.9 %copy-start.13 = (bf16[24,128,896]{2,1,0:T(8,128)(2,1)S(1)}, bf16[24,128,896]{2,1,0:T(8,128)(2,1)}, u32[]{:S(2)}) copy-start(bf16[24,128,896]{2,1,0:T(8,128)(2,1)} %all-gather.6.cloned.1.call-done) | copy-start | bytes 16515076
  206.4 6.9 %copy-start.14 = (bf16[896,512]{1,0:T(8,128)(2,1)S(1)}, bf16[896,512]{1,0:T(8,128)(2,1)}, u32[]{:S(2)}) copy-start(bf16[896,512]{1,0:T(8,128)(2,1)} %param.15) | copy-start | bytes 2752516
  220.2 3.0 %copy-start.1 = (bf16[896,512]{1,0:T(8,128)(2,1)S(1)}, bf16[896,512]{1,0:T(8,128)(2,1)}, u32[]{:S(2)}) copy-start(bf16[896,512]{1,0:T(8,128)(2,1)} %param.14) | copy-start | bytes 2752516
Sparse Core Ops, SparseCore 0:
  17.4 69.7 reduce-scatter.1
  89.0 49.8 all-gather.3
  140.6 65.6 all-gather.5
